TPU v7x, 256 devices: a whole 4x4x8 slice. The times are simulated.
256 devices in a mesh: gx: 32 (over z, y), gy: 8 (over x, core).
Axes of the slice: x: 4, y: 4, z: 8, core: 2. Of those that a mesh axis runs over, the one named last changes fastest.
Arguments:
- fields: float32 [4, 8, 4096, 1024], P(None, None, 'gx', 'gy'), may hold values from -6 to 6
- shift_x: float32 [8, 4096, 1024], P(None, 'gx', 'gy'), may hold values from -0.5 to 0.5
- shift_y: float32 [8, 4096, 1024], P(None, 'gx', 'gy'), may hold values from -0.5 to 0.5
- block_offset: int32 [256, 8], P(None, 'gy'), may hold values from -23 to 23, as said below
- group_inverse: float32 [8, 4096, 128], P(None, 'gx'), as said below
- lower_coupling: float32 [8, 32], P(None, 'gx'), as said below
- upper_coupling: float32 [8, 32], P(None, 'gx'), as said below
Outputs:
- wind_fields: float32 [2, 8, 4096, 1024], P(None, None, 'gx', 'gy')
- tracers: float32 [2, 8, 4096, 1024], P(None, None, 'gx', 'gy')
Inputs may be any that keep to these rules, and one draw needn't show every extreme that they name: `block_offset`: within each aligned run of 8 x-blocks (the blocks of 128 consecutive columns at one y-block), every block departs from a block in the same run or in one of the two runs before or after it, and that run lies inside the grid; at most 4 blocks of a run depart from any one run, and exactly 4 depart from a run two runs away. `group_inverse`: entries are positive. `lower_coupling`: Negative. `upper_coupling`: Negative.
All inputs are finite; a program needn't handle non-finite values.
Results may differ from a plain program's by a relative error of at most 0.0003.
Values sent between devices are 32-bit elements; how exact they have to be, the bound alone decides.
No kernel may reach another device: no remote copies, remote signals or barrier semaphores. Data moves between devices by JAX's collectives and lax.ppermute only.
A program may use at most 128 MiB of HBM per device.

v0:
```python
import jax
import jax.numpy as jnp
from jax import lax
from jax.sharding import PartitionSpec as P
from jax.experimental import pallas as pl
from jax.experimental.pallas import tpu as pltpu

BX = 16


PRECISE = lax.Precision.HIGHEST


def padded_2(block, sides, width):
    for axis, dim in sides:
        count = lax.axis_size(axis)
        forward = [(i, i + 1) for i in range(count - 1)]
        backward = [(target, source) for source, target in forward]
        low = lax.ppermute(
            lax.slice_in_dim(block, block.shape[dim] - width, None, axis=dim), axis, forward
        )
        high = lax.ppermute(lax.slice_in_dim(block, 0, width, axis=dim), axis, backward)
        block = jnp.concatenate([low, block, high], axis=dim)
    return block


def shifted_2(value, axis, steps):
    count = lax.axis_size(axis)
    leading, last = (max(0, -steps), min(count, count - steps))
    return lax.ppermute(value, axis, [(source, source + steps) for source in range(leading, last)])


def lagrange(displace):
    position = -displace
    weights = []
    for target in range(-2, 3):
        factor = jnp.ones_like(position)
        for anchor in range(-2, 3):
            if anchor != target:
                factor = factor * ((position - anchor) / (target - anchor))
        weights.append(factor)
    return weights


def interpolate(window, across, along, span_x, span_y):
    weights_x = lagrange(across)
    weights_y = lagrange(along)
    running_total = None
    for column_tap in range(5):
        partial_sum = weights_y[0] * window[..., column_tap : column_tap + span_x, 0:span_y]
        for row_tap in range(1, 5):
            partial_sum = (
                partial_sum
                + weights_y[row_tap]
                * window[..., column_tap : column_tap + span_x, row_tap : row_tap + span_y]
            )
        tap_term = weights_x[column_tap] * partial_sum
        running_total = tap_term if running_total is None else running_total + tap_term
    return running_total


def _solve_body(pos_ref, packed_ref, left_ref, right_ref, alpha_s, beta_s, p_s, q_s, f_s):
    count = packed_ref.shape[0]
    width = left_ref.shape[0]
    levels, lanes = left_ref.shape[1], left_ref.shape[2]
    p = jnp.zeros((width, levels, lanes), jnp.float32)
    q = jnp.zeros((levels, lanes), jnp.float32)
    for j in range(count):
        first = packed_ref[j, 0:width]
        last = packed_ref[j, width : 2 * width]
        coef = packed_ref[j, 2 * width]
        lead_left = jnp.broadcast_to(coef[:, 0:1], (levels, lanes))
        tail_left = jnp.broadcast_to(coef[:, 1:2], (levels, lanes))
        lead_right = jnp.broadcast_to(coef[:, 2:3], (levels, lanes))
        tail_right = jnp.broadcast_to(coef[:, 3:4], (levels, lanes))
        pivot = 1.0 + lead_left * q
        alpha = (first - lead_left * p) / pivot
        beta = -lead_right / pivot
        p_s[j] = p
        q_s[j] = q
        alpha_s[j] = alpha
        beta_s[j] = beta
        p = last - tail_left * p - tail_left * q * alpha
        q = -(tail_left * q * beta) - tail_right
    ahead = jnp.zeros((width, levels, lanes), jnp.float32)
    f_s[count] = ahead
    for j in range(count - 1, -1, -1):
        ahead = alpha_s[j] + beta_s[j] * ahead
        f_s[j] = ahead
    pos = pos_ref[0]
    left_ref[...] = p_s[pos] + q_s[pos] * f_s[pos]
    right_ref[...] = f_s[pos + 1]

def interface_solve(packed_all, position, width):
    count, _, levels, lanes = packed_all.shape
    out = jax.ShapeDtypeStruct((width, levels, lanes), jnp.float32)
    vmem = pltpu.VMEM
    return pl.pallas_call(
        _solve_body,
        out_shape=(out, out),
        in_specs=[pl.BlockSpec(memory_space=pltpu.SMEM), pl.BlockSpec(memory_space=vmem)],
        out_specs=(pl.BlockSpec(memory_space=vmem), pl.BlockSpec(memory_space=vmem)),
        scratch_shapes=[
            pltpu.VMEM((count, width, levels, lanes), jnp.float32),
            pltpu.VMEM((count, levels, lanes), jnp.float32),
            pltpu.VMEM((count, width, levels, lanes), jnp.float32),
            pltpu.VMEM((count, levels, lanes), jnp.float32),
            pltpu.VMEM((count + 1, width, levels, lanes), jnp.float32),
        ],
    )(jnp.reshape(position, (1,)).astype(jnp.int32), packed_all)


def halo_x(block, axis, width):
    count = lax.axis_size(axis)
    forward = [(i, i + 1) for i in range(count - 1)]
    backward = [(target, source) for source, target in forward]
    low = lax.ppermute(block[:, block.shape[1] - width :], axis, forward)
    high = lax.ppermute(block[:, 0:width], axis, backward)
    return jnp.concatenate([low, block, high], axis=1)


def halo_y(block, axis, width):
    count = lax.axis_size(axis)
    forward = [(i, i + 1) for i in range(count - 1)]
    backward = [(target, source) for source, target in forward]
    low = lax.ppermute(block[:, :, block.shape[2] - width :], axis, forward)
    high = lax.ppermute(block[:, :, 0:width], axis, backward)
    return jnp.concatenate([low, high], axis=2)


def source_of(offsets, run, block_count):
    blocks = run * block_count + jnp.arange(block_count, dtype=jnp.int32)
    return blocks - lax.dynamic_slice_in_dim(offsets, run * block_count, block_count)


def slot_rank(mask):
    return jnp.cumsum(mask.astype(jnp.int32)) - 1


def send_windows(main, halo, offsets, position, count, block_count):
    window = BX + 4
    cap = 4
    channels, _, rows_here = main.shape
    deltas = (-2, -1, 1, 2)
    received_main = {}
    received_halo = {}
    for delta in deltas:
        target = jnp.clip(position - delta, 0, count - 1)
        source = source_of(offsets, target, block_count)
        local_start = (source - position * block_count) * BX
        mask = (source >= position * block_count) & (source < (position + 1) * block_count)
        rank = slot_rank(mask)
        starts = [
            jnp.sum(jnp.where(mask & (rank == slot), local_start, 0)) for slot in range(cap)
        ]
        send_main = jnp.concatenate(
            [lax.dynamic_slice_in_dim(main, start, window, 1) for start in starts], axis=1
        )
        send_halo = jnp.concatenate(
            [lax.dynamic_slice_in_dim(halo, start, window, 2) for start in starts], axis=2
        )
        span = cap * window
        send_halo = jnp.pad(send_halo, ((0, 0), (0, 0), (0, rows_here - span)))
        sent = shifted_2(jnp.concatenate([send_main, send_halo], axis=1), "gx", -delta)
        received_main[delta] = sent[:, 0:span]
        received_halo[delta] = sent[:, span:, 0:span]
    return received_main, received_halo


def assemble_windows(main, halo, received_main, received_halo, offsets, position, block_count):
    window = BX + 4
    order = (-2, -1, 0, 1, 2)
    pieces_main = [main if delta == 0 else received_main[delta] for delta in order]
    pieces_halo = [halo if delta == 0 else received_halo[delta] for delta in order]
    bases = {}
    base = 0
    for delta, piece in zip(order, pieces_main):
        bases[delta] = base
        base += piece.shape[1]
    all_main = jnp.concatenate(pieces_main, axis=1)
    all_halo = jnp.concatenate(pieces_halo, axis=2)
    own_source = source_of(offsets, position, block_count)
    own_delta = own_source // block_count - position
    start_here = jnp.zeros((block_count,), jnp.int32)
    for delta in order:
        if delta == 0:
            candidate = bases[0] + (own_source - position * block_count) * BX
        else:
            rank = slot_rank(own_delta == delta)
            candidate = bases[delta] + rank * window
        start_here = jnp.where(own_delta == delta, candidate, start_here)
    window_main = jnp.stack(
        [lax.dynamic_slice_in_dim(all_main, start_here[b], window, 1) for b in range(block_count)]
    )
    window_halo = jnp.stack(
        [lax.dynamic_slice_in_dim(all_halo, start_here[b], window, 2) for b in range(block_count)]
    ).transpose(0, 1, 3, 2)
    return jnp.concatenate(
        [window_halo[..., 0:2], window_main, window_halo[..., 2:4]], axis=3
    )


def advect_group(windows, shift_x, shift_y, field_count):
    block_count = windows.shape[0]
    level_count, columns, rows_here = shift_x.shape
    windows = windows.reshape(block_count, field_count, level_count, BX + 4, rows_here + 4)
    across = shift_x.reshape(level_count, block_count, BX, rows_here).transpose(1, 0, 2, 3)[:, None]
    along = shift_y.reshape(level_count, block_count, BX, rows_here).transpose(1, 0, 2, 3)[:, None]
    interpolated = interpolate(windows, across, along, BX, rows_here)
    return interpolated.transpose(1, 2, 0, 3, 4).reshape(
        field_count, level_count, columns, rows_here
    )


def local(fields, shift_x, shift_y, block_offset, group_inverse, lower_coupling, upper_coupling):
    field_count, level_count, columns, rows_here = fields.shape
    block_count = columns // BX
    channels = field_count * level_count
    wind_channels = 2 * level_count
    count = lax.axis_size("gx")
    position = lax.axis_index("gx")
    flat = fields.reshape(channels, columns, rows_here)
    main = halo_x(flat, "gx", 2)
    halo = halo_y(main, "gy", 2).transpose(0, 2, 1)
    offsets = block_offset[:, 0]
    wind_main, wind_halo = main[:wind_channels], halo[:wind_channels]
    tracer_main, tracer_halo = main[wind_channels:], halo[wind_channels:]
    wind_received = send_windows(wind_main, wind_halo, offsets, position, count, block_count)
    tracer_received = send_windows(tracer_main, tracer_halo, offsets, position, count, block_count)
    wind_windows = assemble_windows(
        wind_main, wind_halo, *wind_received, offsets, position, block_count
    )
    winds = advect_group(wind_windows, shift_x, shift_y, 2)
    local_solve = jnp.einsum("lij,wljy->wliy", group_inverse, winds, precision=PRECISE)
    lower_here = lower_coupling[:, 0]
    upper_here = upper_coupling[:, 0]
    left_spike = group_inverse[:, :, 0] * lower_here[:, None]
    right_spike = group_inverse[:, :, columns - 1] * upper_here[:, None]
    coef = jnp.stack(
        [left_spike[:, 0], left_spike[:, columns - 1], right_spike[:, 0], right_spike[:, columns - 1]],
        axis=-1,
    )
    coef_rows = jnp.pad(coef, ((0, 0), (0, rows_here - 4)))
    first_row = local_solve[:, :, 0, :]
    last_row = local_solve[:, :, columns - 1, :]
    packed = jnp.concatenate([first_row, last_row, coef_rows[None]], axis=0)
    held = packed[None]
    step = 1
    while step < count:
        ring = [(i, (i + step) % count) for i in range(count)]
        held = jnp.concatenate([held, lax.ppermute(held, "gx", ring)], axis=0)
        if step == 1:
            held, tracer_received = lax.optimization_barrier((held, tracer_received))
        step *= 2
    reverse = held[::-1]
    doubled = jnp.concatenate([reverse, reverse], axis=0)
    packed_all = lax.dynamic_slice_in_dim(doubled, count - 1 - position, count, 0)
    left_value, right_value = interface_solve(packed_all, position, first_row.shape[0])
    wind_fields = (
        local_solve
        - left_spike[None, :, :, None] * left_value[:, :, None, :]
        - right_spike[None, :, :, None] * right_value[:, :, None, :]
    )
    tracer_windows = assemble_windows(
        tracer_main, tracer_halo, *tracer_received, offsets, position, block_count
    )
    tracers = advect_group(tracer_windows, shift_x, shift_y, field_count - 2)
    return (wind_fields, tracers)


def solution(mesh):
    return jax.shard_map(
        local,
        mesh=mesh,
        in_specs=(
            P(None, None, "gx", "gy"),
            P(None, "gx", "gy"),
            P(None, "gx", "gy"),
            P(None, "gy"),
            P(None, "gx", None),
            P(None, "gx"),
            P(None, "gx"),
        ),
        out_specs=(P(None, None, "gx", "gy"), P(None, None, "gx", "gy")),
        check_vma=False,
    )
```

profile of v0, /device:TPU:34, one launch (start us, length us, event | category | flops | bytes accessed | tf_op | source)
XLA Modules:
  0.0 254.0 jit_solution(5556086871291543050)
XLA Ops:
  0.7 2.9 %copy.83 = f32[4,8,128,128]{3,1,0,2:T(8,128)S(1)} copy(f32[4,8,128,128]{3,2,1,0:T(8,128)} %param.7) | data formatting | bytes 4194304 | tf_op args[0]
  3.6 1.3 copy-done.4
  4.9 3.5 %collective-permute-start = (f32[32,2,128]{2,0,1:T(8,128)S(1)}, f32[32,2,128]{2,0,1:T(8,128)S(1)}, u32[]{:S(2)}, u32[]{:S(2)}) collective-permute-start(f32[32,2,128]{2,0,1:T(8,128)S(1)} %get-tuple-element.54), channel_id=1, source_target_pairs={{0,8},{8,16},{16,24},{24,32},{32,40},{40,48},{48,56},{56,64},{64,7... | collective-permute-start | bytes 98312 | tf_op jit(solution)/shard_map/ppermute | solution.py:117
  8.4 4.5 %collective-permute-start.1 = (f32[32,2,128]{2,0,1:T(8,128)S(1)}, f32[32,2,128]{2,0,1:T(8,128)S(1)}, u32[]{:S(2)}, u32[]{:S(2)}) collective-permute-start(f32[32,2,128]{2,0,1:T(8,128)S(1)} %get-tuple-element.55), channel_id=1, source_target_pairs={{8,0},{16,8},{24,16},{32,24},{40,32},{48,40},{56,48},{64,56},{72,6... | collective-permute-start | bytes 98312 | tf_op jit(solution)/shard_map/ppermute | solution.py:118
  15.3 3.9 %fusion.64 = (f32[8,8,16,128]{3,1,2,0:T(8,128)}, f32[8,8,16,128]{3,1,2,0:T(8,128)}, f32[8,8,16,128]{3,1,2,0:T(8,128)}, f32[8,8,16,128]{3,1,2,0:T(8,128)}, f32[8,...) fusion(f32[8,8,16,128]{3,2,1,0:T(8,128)S(1)} %bitcast.371, ...), kind=kLoop, calls=%fused_computation.134 | loop fusion | flops 9175040 | bytes 6291456 | tf_op jit(solution)/shard_map/mul | solution.py:40
  19.5 0.8 fusion.101
  20.3 0.8 fusion.109
  51.4 1.8 pad_maximum_fusion
  53.2 2.9 %fusion.116 = (f32[32,132,2]{2,0,1:T(8,128)}, f32[32,132,2]{2,0,1:T(8,128)}) fusion(f32[32,132,128]{2,0,1:T(8,128)S(1)} %pad_maximum_fusion), kind=kLoop, calls=%fused_computation.408 | loop fusion | bytes 135168 | tf_op jit(solution)/shard_map/slice | solution.py:126
  56.1 3.2 %copy.50 = f32[32,132,2]{1,0,2:T(8,128)S(1)} copy(f32[32,132,2]{2,0,1:T(8,128)} %get-tuple-element.52) | data formatting | bytes 67584 | tf_op jit(solution)/shard_map/slice | solution.py:126
  59.3 1.9 collective-permute-start.2
  61.3 3.2 %copy.51 = f32[32,132,2]{1,0,2:T(8,128)S(1)} copy(f32[32,132,2]{2,0,1:T(8,128)} %get-tuple-element.53) | data formatting | bytes 67584 | tf_op jit(solution)/shard_map/slice | solution.py:127
  64.5 3.6 %collective-permute-start.3 = (f32[32,132,2]{1,0,2:T(8,128)S(1)}, f32[32,132,2]{1,0,2:T(8,128)S(1)}, u32[]{:S(2)}, u32[]{:S(2)}) collective-permute-start(f32[32,132,2]{1,0,2:T(8,128)S(1)} %copy.51), channel_id=1, source_target_pairs={{1,0},{2,1},{3,2},{4,3},{5,4},{6,5},{7,6},{9,8},{10,9},{11,10},{12... | collective-permute-start | bytes 101384 | tf_op jit(solution)/shard_map/ppermute | solution.py:127
  71.4 0.9 constant_dynamic-update-slice_fusion
  72.3 3.0 %collective-permute-start.4 = (f32[16,84,128]{2,0,1:T(8,128)}, f32[16,84,128]{2,0,1:T(8,128)S(1)}, u32[]{:S(2)}, u32[]{:S(2)}) collective-permute-start(f32[16,84,128]{2,0,1:T(8,128)} %constant_dynamic-update-slice_fusion), channel_id=1, source_target_pairs={{0,16},{8,24},{16,32},{24,40},{32,48},{40,56},{48,64},{56,72},{64,... | collective-permute-start | bytes 2064392 | tf_op jit(solution)/shard_map/ppermute | solution.py:30
  91.7 2.6 %collective-permute-start.5 = (f32[16,84,128]{2,0,1:T(8,128)}, f32[16,84,128]{2,0,1:T(8,128)S(1)}, u32[]{:S(2)}, u32[]{:S(2)}) collective-permute-start(f32[16,84,128]{2,0,1:T(8,128)} %constant_dynamic-update-slice_fusion.5), channel_id=1, source_target_pairs={{0,8},{8,16},{16,24},{24,32},{32,40},{40,48},{48,56},{56,64},{64,7... | collective-permute-start | bytes 2064392 | tf_op jit(solution)/shard_map/ppermute | solution.py:30
  95.1 5.4 %collective-permute-start.6 = (f32[16,84,128]{2,0,1:T(8,128)}, f32[16,84,128]{2,0,1:T(8,128)S(1)}, u32[]{:S(2)}, u32[]{:S(2)}) collective-permute-start(f32[16,84,128]{2,0,1:T(8,128)} %constant_dynamic-update-slice_fusion.10), channel_id=1, source_target_pairs={{8,0},{16,8},{24,16},{32,24},{40,32},{48,40},{56,48},{64,56},{72,6... | collective-permute-start | bytes 2064392 | tf_op jit(solution)/shard_map/ppermute | solution.py:30
  101.2 3.3 %collective-permute-start.7 = (f32[16,84,128]{2,0,1:T(8,128)}, f32[16,84,128]{2,0,1:T(8,128)S(1)}, u32[]{:S(2)}, u32[]{:S(2)}) collective-permute-start(f32[16,84,128]{2,0,1:T(8,128)} %constant_dynamic-update-slice_fusion.15), channel_id=1, source_target_pairs={{16,0},{24,8},{32,16},{40,24},{48,32},{56,40},{64,48},{72,56},{80,... | collective-permute-start | bytes 2064392 | tf_op jit(solution)/shard_map/ppermute | solution.py:30
  104.9 8.9 %collective-permute-done.5 = f32[16,84,128]{2,0,1:T(8,128)S(1)} collective-permute-done((f32[16,84,128]{2,0,1:T(8,128)}, f32[16,84,128]{2,0,1:T(8,128)S(1)}, u32[]{:S(2)}, u32[]{:S(2)}) %collective-permute-start.5) | collective-permute-done | bytes 688160 | tf_op jit(solution)/shard_map/ppermute | solution.py:30
  114.0 0.9 constant_dynamic-update-slice_fusion.56
  114.8 0.9 constant_dynamic-update-slice_fusion.55
  115.7 0.9 constant_dynamic-update-slice_fusion.54
  116.6 0.9 constant_dynamic-update-slice_fusion.53
  118.2 2.8 %collective-permute-start.12 = (f32[16,84,128]{2,0,1:T(8,128)}, f32[16,84,128]{2,0,1:T(8,128)}, u32[]{:S(2)}, u32[]{:S(2)}) collective-permute-start(f32[16,84,128]{2,0,1:T(8,128)} %constant_dynamic-update-slice_fusion.52), channel_id=1, source_target_pairs={{16,0},{24,8},{32,16},{40,24},{48,32},{56,40},{64,48},{72,56},{80,... | collective-permute-start | bytes 2064392 | tf_op jit(solution)/shard_map/ppermute | solution.py:30
  121.7 2.2 collective-permute-start.11
  124.6 3.7 %collective-permute-start.10 = (f32[16,84,128]{2,0,1:T(8,128)}, f32[16,84,128]{2,0,1:T(8,128)}, u32[]{:S(2)}, u32[]{:S(2)}) collective-permute-start(f32[16,84,128]{2,0,1:T(8,128)} %constant_dynamic-update-slice_fusion.42), channel_id=1, source_target_pairs={{0,8},{8,16},{16,24},{24,32},{32,40},{40,48},{48,56},{56,64},{64,7... | collective-permute-start | bytes 2064392 | tf_op jit(solution)/shard_map/ppermute | solution.py:30
  129.0 1.5 collective-permute-done.6
  130.5 3.0 %collective-permute-start.9 = (f32[16,84,128]{2,0,1:T(8,128)}, f32[16,84,128]{2,0,1:T(8,128)}, u32[]{:S(2)}, u32[]{:S(2)}) collective-permute-start(f32[16,84,128]{2,0,1:T(8,128)} %constant_dynamic-update-slice_fusion.37), channel_id=1, source_target_pairs={{0,16},{8,24},{16,32},{24,40},{32,48},{40,56},{48,64},{56,72},{64,... | collective-permute-start | bytes 2064392 | tf_op jit(solution)/shard_map/ppermute | solution.py:30
  133.5 9.9 %collective-permute-done.7 = f32[16,84,128]{2,0,1:T(8,128)S(1)} collective-permute-done((f32[16,84,128]{2,0,1:T(8,128)}, f32[16,84,128]{2,0,1:T(8,128)S(1)}, u32[]{:S(2)}, u32[]{:S(2)}) %collective-permute-start.7) | collective-permute-done | bytes 688160 | tf_op jit(solution)/shard_map/ppermute | solution.py:30
  143.6 1.7 copy-done.9
  145.5 0.9 constant_dynamic-update-slice_fusion.35
  146.5 0.9 constant_dynamic-update-slice_fusion.34
  147.5 0.9 constant_dynamic-update-slice_fusion.33
  148.6 0.9 constant_dynamic-update-slice_fusion.32
  149.6 0.9 constant_dynamic-update-slice_fusion.31
  150.6 0.9 constant_dynamic-update-slice_fusion.30
  151.6 0.9 constant_dynamic-update-slice_fusion.29
  152.7 2.0 copy.52
  154.7 2.0 copy.53
  156.7 3.2 %maximum_bitcast_fusion = f32[8,2,8,20,132]{4,2,1,3,0:T(8,128)S(1)} fusion(f32[8,16,20,2]{3,1,2,0:T(8,128)} %copy.53, f32[8,16,20,128]{3,1,2,0:T(8,128)} %copy-done.7, f32[8,16,20,2]{3,1,2,0:T(8,128)} %copy.52), kind=kLoop, calls=%fused_computation | loop fusion | flops 675840 | bytes 2703360 | tf_op jit(solution)/shard_map/reshape | solution.py:206
  159.9 8.0 %fusion.31 = f32[8,2,8,16,128]{4,2,1,3,0:T(8,128)} fusion(f32[8,2,8,20,132]{4,2,1,3,0:T(8,128)S(1)} %maximum_bitcast_fusion, f32[8,8,16,128]{3,1,2,0:T(8,128)} %get-tuple-element.181, f32[8,8,16,128]{3,1,2,0:T(8,128)} %get-tuple-element.180, f32[8,8,16,128]{3,1,2,0:T(8,128)} %get-tuple-element.178, f32[8,8,16,128]{3,1,2,0:T(8,128)} %get-tuple-element.179, ...), kind=kLoop, calls=%fused_computation.63 | loop fusion | flops 14155776 | bytes 32505856 | tf_op jit(solution)/shard_map/add | solution.py:58
  167.9 2.7 %fusion.58 = f32[8,2,128,128]{2,3,1,0:T(8,128)S(1)} fusion(f32[2,8,128,128]{3,1,0,2:T(8,128)} %bitcast.369, f32[8,128,128]{2,1,0:T(8,128)} %param.11), kind=kOutput, calls=%fused_computation.115 | convolution fusion | flops 402653184 | bytes 2621440 | tf_op jit(solution)/shard_map/lij,wljy->wliy/dot_general | solution.py:234
  170.6 1.0 copy-done.2
  173.8 13.0 %collective-permute-done.8 = f32[1,5,8,128]{3,2,1,0:T(8,128)S(1)} collective-permute-done((f32[1,5,8,128]{3,2,1,0:T(8,128)S(1)}, f32[1,5,8,128]{3,2,1,0:T(8,128)S(1)}, u32[]{:S(2)}, u32[]{:S(2)}) %collective-permute-start.8) | collective-permute-done | bytes 20512 | tf_op jit(solution)/shard_map/ppermute | solution.py:251
  186.8 1.1 slice.448
  188.7 1.1 slice.447
  190.6 1.1 slice.446
  191.7 0.9 slice.450
  192.6 1.1 slice.445
  195.0 1.6 copy-done.10
  197.5 4.2 %collective-permute-start.13 = (f32[2,5,8,128]{3,2,1,0:T(8,128)S(1)}, f32[2,5,8,128]{3,2,1,0:T(8,128)S(1)}, u32[]{:S(2)}, u32[]{:S(2)}) collective-permute-start(f32[2,5,8,128]{3,2,1,0:T(8,128)S(1)} %pad_maximum_fusion.4), channel_id=1, source_target_pairs={{0,16},{8,24},{16,32},{24,40},{32,48},{40,56},{48,64},{56,72},{64,... | collective-permute-start | bytes 122888 | tf_op jit(solution)/shard_map/ppermute | solution.py:251
  201.7 0.9 constant_dynamic-update-slice_fusion.75
  202.7 2.1 copy.60
  204.8 2.0 copy.61
  206.8 1.3 collective-permute-start.14
  208.1 3.2 %maximum_bitcast_fusion.1 = f32[8,2,8,20,132]{4,2,1,3,0:T(8,128)S(1)} fusion(f32[8,16,20,2]{3,1,2,0:T(8,128)} %copy.61, f32[8,16,20,128]{3,1,2,0:T(8,128)} %copy-done.8, f32[8,16,20,2]{3,1,2,0:T(8,128)} %copy.60), kind=kLoop, calls=%fused_computation.1 | loop fusion | flops 675840 | bytes 2703360 | tf_op jit(solution)/shard_map/reshape | solution.py:206
  212.0 5.8 %collective-permute-start.15 = (f32[8,5,8,128]{3,2,1,0:T(8,128)}, f32[8,5,8,128]{3,2,1,0:T(8,128)S(1)}, u32[]{:S(2)}, u32[]{:S(2)}) collective-permute-start(f32[8,5,8,128]{3,2,1,0:T(8,128)} %pad_maximum_fusion.2), channel_id=1, source_target_pairs={{0,64},{8,72},{16,80},{24,88},{32,96},{40,104},{48,112},{56,120},{... | collective-permute-start | bytes 491528 | tf_op jit(solution)/shard_map/ppermute | solution.py:251
  217.8 8.0 %fusion.2 = f32[8,2,8,16,128]{4,2,1,3,0:T(8,128)} fusion(f32[8,2,8,20,132]{4,2,1,3,0:T(8,128)S(1)} %maximum_bitcast_fusion.1, f32[8,8,16,128]{3,1,2,0:T(8,128)} %get-tuple-element.181, f32[8,8,16,128]{3,1,2,0:T(8,128)} %get-tuple-element.180, f32[8,8,16,128]{3,1,2,0:T(8,128)} %get-tuple-element.178, f32[8,8,16,128]{3,1,2,0:T(8,128)} %get-tuple-element.179, ...), kind=kLoop, calls=%fused_computation.9 | loop fusion | flops 14155776 | bytes 32505856 | tf_op jit(solution)/shard_map/add | solution.py:58
  225.8 2.5 copy.63
  229.2 18.9 %collective-permute-done.16 = f32[16,5,8,128]{3,2,1,0:T(8,128)S(1)} collective-permute-done((f32[16,5,8,128]{3,2,1,0:T(8,128)S(1)}, f32[16,5,8,128]{3,2,1,0:T(8,128)S(1)}, u32[]{:S(2)}, u32[]{:S(2)}) %collective-permute-start.16) | collective-permute-done | bytes 327712 | tf_op jit(solution)/shard_map/ppermute | solution.py:251
  248.1 1.0 fusion.60.packed_ref
  249.1 2.2 shard_map.86
  251.3 1.4 multiply_subtract_fusion
  252.7 1.3 copy.62
  (151 shorter events, 20.5 us)
Async XLA Ops:
  0.6 12.3 %copy-start.15 = (s32[256,1]{0,1:T(1,128)S(1)}, s32[256,1]{0,1:T(1,128)}, u32[]{:S(2)}) copy-start(s32[256,1]{0,1:T(1,128)} %param.10) | copy-start | bytes 3076
  0.6 13.9 %copy-start.11 = (f32[8,128,128]{2,1,0:T(8,128)S(1)}, f32[8,128,128]{2,1,0:T(8,128)}, u32[]{:S(2)}) copy-start(f32[8,128,128]{2,1,0:T(8,128)} %param.8) | copy-start | bytes 1572868
  0.7 14.0 %copy-start.12 = (f32[8,128,128]{2,1,0:T(8,128)S(1)}, f32[8,128,128]{2,1,0:T(8,128)}, u32[]{:S(2)}) copy-start(f32[8,128,128]{2,1,0:T(8,128)} %param.9) | copy-start | bytes 1572868
  3.6 1.4 copy-start.4
  3.6 11.1 %copy-start.6 = (f32[8,128,128]{2,1,0:T(8,128)S(1)}, f32[8,128,128]{2,1,0:T(8,128)}, u32[]{:S(2)}) copy-start(f32[8,128,128]{2,1,0:T(8,128)} %param.11) | copy-start | bytes 1572868
  4.9 46.4 %collective-permute-start = (f32[32,2,128]{2,0,1:T(8,128)S(1)}, f32[32,2,128]{2,0,1:T(8,128)S(1)}, u32[]{:S(2)}, u32[]{:S(2)}) collective-permute-start(f32[32,2,128]{2,0,1:T(8,128)S(1)} %get-tuple-element.54), channel_id=1, source_target_pairs={{0,8},{8,16},{16,24},{24,32},{32,40},{40,48},{48,56},{56,64},{64,7... | collective-permute-start | bytes 98312 | tf_op jit(solution)/shard_map/ppermute | solution.py:117
  8.4 43.0 %collective-permute-start.1 = (f32[32,2,128]{2,0,1:T(8,128)S(1)}, f32[32,2,128]{2,0,1:T(8,128)S(1)}, u32[]{:S(2)}, u32[]{:S(2)}) collective-permute-start(f32[32,2,128]{2,0,1:T(8,128)S(1)} %get-tuple-element.55), channel_id=1, source_target_pairs={{8,0},{16,8},{24,16},{32,24},{40,32},{48,40},{56,48},{64,56},{72,6... | collective-permute-start | bytes 98312 | tf_op jit(solution)/shard_map/ppermute | solution.py:118
  15.3 3.9 %copy-start.19 = (f32[8,1]{0,1:T(1,128)S(1)}, f32[8,1]{0,1:T(1,128)}, u32[]{:S(2)}) copy-start(f32[8,1]{0,1:T(1,128)} %param.13) | copy-start | bytes 100
  15.3 4.0 %copy-start.20 = (f32[8,1]{0,1:T(1,128)S(1)}, f32[8,1]{0,1:T(1,128)}, u32[]{:S(2)}) copy-start(f32[8,1]{0,1:T(1,128)} %param.12) | copy-start | bytes 100
  53.1 60.7 %copy-start = (f32[32,132,128]{2,0,1:T(8,128)}, f32[32,132,128]{2,0,1:T(8,128)S(1)}, u32[]{:S(2)}) copy-start(f32[32,132,128]{2,0,1:T(8,128)S(1)} %pad_maximum_fusion) | copy-start | bytes 6488068
  59.3 11.7 %collective-permute-start.2 = (f32[32,132,2]{1,0,2:T(8,128)S(1)}, f32[32,132,2]{1,0,2:T(8,128)S(1)}, u32[]{:S(2)}, u32[]{:S(2)}) collective-permute-start(f32[32,132,2]{1,0,2:T(8,128)S(1)} %copy.50), channel_id=1, source_target_pairs={{0,1},{1,2},{2,3},{3,4},{4,5},{5,6},{6,7},{8,9},{9,10},{10,11},{11... | collective-permute-start | bytes 101384 | tf_op jit(solution)/shard_map/ppermute | solution.py:126
  64.5 6.5 %collective-permute-start.3 = (f32[32,132,2]{1,0,2:T(8,128)S(1)}, f32[32,132,2]{1,0,2:T(8,128)S(1)}, u32[]{:S(2)}, u32[]{:S(2)}) collective-permute-start(f32[32,132,2]{1,0,2:T(8,128)S(1)} %copy.51), channel_id=1, source_target_pairs={{1,0},{2,1},{3,2},{4,3},{5,4},{6,5},{7,6},{9,8},{10,9},{11,10},{12... | collective-permute-start | bytes 101384 | tf_op jit(solution)/shard_map/ppermute | solution.py:127
  71.0 5.0 %copy-start.16 = (f32[16,84,128]{2,0,1:T(8,128)}, f32[16,84,128]{2,0,1:T(8,128)S(1)}, u32[]{:S(2)}) copy-start(f32[16,84,128]{2,0,1:T(8,128)S(1)} %get-tuple-element.72) | copy-start | bytes 2064388
  71.0 5.0 %copy-start.17 = (f32[16,84,128]{2,0,1:T(8,128)}, f32[16,84,128]{2,0,1:T(8,128)S(1)}, u32[]{:S(2)}) copy-start(f32[16,84,128]{2,0,1:T(8,128)S(1)} %get-tuple-element.73) | copy-start | bytes 2064388
  71.0 5.0 %copy-start.18 = (f32[16,84,128]{2,0,1:T(8,128)}, f32[16,84,128]{2,0,1:T(8,128)S(1)}, u32[]{:S(2)}) copy-start(f32[16,84,128]{2,0,1:T(8,128)S(1)} %get-tuple-element.74) | copy-start | bytes 2064388
  72.3 32.5 %collective-permute-start.4 = (f32[16,84,128]{2,0,1:T(8,128)}, f32[16,84,128]{2,0,1:T(8,128)S(1)}, u32[]{:S(2)}, u32[]{:S(2)}) collective-permute-start(f32[16,84,128]{2,0,1:T(8,128)} %constant_dynamic-update-slice_fusion), channel_id=1, source_target_pairs={{0,16},{8,24},{16,32},{24,40},{32,48},{40,56},{48,64},{56,72},{64,... | collective-permute-start | bytes 2064392 | tf_op jit(solution)/shard_map/ppermute | solution.py:30
  91.7 22.0 %collective-permute-start.5 = (f32[16,84,128]{2,0,1:T(8,128)}, f32[16,84,128]{2,0,1:T(8,128)S(1)}, u32[]{:S(2)}, u32[]{:S(2)}) collective-permute-start(f32[16,84,128]{2,0,1:T(8,128)} %constant_dynamic-update-slice_fusion.5), channel_id=1, source_target_pairs={{0,8},{8,16},{16,24},{24,32},{32,40},{40,48},{48,56},{56,64},{64,7... | collective-permute-start | bytes 2064392 | tf_op jit(solution)/shard_map/ppermute | solution.py:30
  95.1 35.4 %collective-permute-start.6 = (f32[16,84,128]{2,0,1:T(8,128)}, f32[16,84,128]{2,0,1:T(8,128)S(1)}, u32[]{:S(2)}, u32[]{:S(2)}) collective-permute-start(f32[16,84,128]{2,0,1:T(8,128)} %constant_dynamic-update-slice_fusion.10), channel_id=1, source_target_pairs={{8,0},{16,8},{24,16},{32,24},{40,32},{48,40},{56,48},{64,56},{72,6... | collective-permute-start | bytes 2064392 | tf_op jit(solution)/shard_map/ppermute | solution.py:30
  101.2 42.3 %collective-permute-start.7 = (f32[16,84,128]{2,0,1:T(8,128)}, f32[16,84,128]{2,0,1:T(8,128)S(1)}, u32[]{:S(2)}, u32[]{:S(2)}) collective-permute-start(f32[16,84,128]{2,0,1:T(8,128)} %constant_dynamic-update-slice_fusion.15), channel_id=1, source_target_pairs={{16,0},{24,8},{32,16},{40,24},{48,32},{56,40},{64,48},{72,56},{80,... | collective-permute-start | bytes 2064392 | tf_op jit(solution)/shard_map/ppermute | solution.py:30
  118.2 68.6 %collective-permute-start.12 = (f32[16,84,128]{2,0,1:T(8,128)}, f32[16,84,128]{2,0,1:T(8,128)}, u32[]{:S(2)}, u32[]{:S(2)}) collective-permute-start(f32[16,84,128]{2,0,1:T(8,128)} %constant_dynamic-update-slice_fusion.52), channel_id=1, source_target_pairs={{16,0},{24,8},{32,16},{40,24},{48,32},{56,40},{64,48},{72,56},{80,... | collective-permute-start | bytes 2064392 | tf_op jit(solution)/shard_map/ppermute | solution.py:30
  121.7 67.0 %collective-permute-start.11 = (f32[16,84,128]{2,0,1:T(8,128)}, f32[16,84,128]{2,0,1:T(8,128)}, u32[]{:S(2)}, u32[]{:S(2)}) collective-permute-start(f32[16,84,128]{2,0,1:T(8,128)} %constant_dynamic-update-slice_fusion.47), channel_id=1, source_target_pairs={{8,0},{16,8},{24,16},{32,24},{40,32},{48,40},{56,48},{64,56},{72,6... | collective-permute-start | bytes 2064392 | tf_op jit(solution)/shard_map/ppermute | solution.py:30
  124.6 66.0 %collective-permute-start.10 = (f32[16,84,128]{2,0,1:T(8,128)}, f32[16,84,128]{2,0,1:T(8,128)}, u32[]{:S(2)}, u32[]{:S(2)}) collective-permute-start(f32[16,84,128]{2,0,1:T(8,128)} %constant_dynamic-update-slice_fusion.42), channel_id=1, source_target_pairs={{0,8},{8,16},{16,24},{24,32},{32,40},{40,48},{48,56},{56,64},{64,7... | collective-permute-start | bytes 2064392 | tf_op jit(solution)/shard_map/ppermute | solution.py:30
  130.5 62.1 %collective-permute-start.9 = (f32[16,84,128]{2,0,1:T(8,128)}, f32[16,84,128]{2,0,1:T(8,128)}, u32[]{:S(2)}, u32[]{:S(2)}) collective-permute-start(f32[16,84,128]{2,0,1:T(8,128)} %constant_dynamic-update-slice_fusion.37), channel_id=1, source_target_pairs={{0,16},{8,24},{16,32},{24,40},{32,48},{40,56},{48,64},{56,72},{64,... | collective-permute-start | bytes 2064392 | tf_op jit(solution)/shard_map/ppermute | solution.py:30
  143.5 1.8 copy-start.9
  152.5 2.1 copy-start.7
  156.7 3.2 %copy-start.5 = (f32[8,8,16,128]{3,1,2,0:T(8,128)S(1)}, f32[8,8,16,128]{3,1,2,0:T(8,128)}, u32[]{:S(2)}) copy-start(f32[8,8,16,128]{3,1,2,0:T(8,128)} %get-tuple-element.95) | copy-start | bytes 1572868
  170.6 1.0 copy-start.2
  172.2 14.6 %collective-permute-start.8 = (f32[1,5,8,128]{3,2,1,0:T(8,128)S(1)}, f32[1,5,8,128]{3,2,1,0:T(8,128)S(1)}, u32[]{:S(2)}, u32[]{:S(2)}) collective-permute-start(f32[1,5,8,128]{3,2,1,0:T(8,128)S(1)} %maximum_bitcast_fusion.3), channel_id=1, source_target_pairs={{0,8},{8,16},{16,24},{24,32},{32,40},{40,48},{48,56},{56,64},{64,7... | collective-permute-start | bytes 61448 | tf_op jit(solution)/shard_map/ppermute | solution.py:251
  191.7 2.9 %copy-start.1 = (f32[32,132,128]{2,0,1:T(8,128)S(1)}, f32[32,132,128]{2,0,1:T(8,128)}, u32[]{:S(2)}) copy-start(f32[32,132,128]{2,0,1:T(8,128)} %copy-done) | copy-start | bytes 6488068
  194.9 1.8 copy-start.10
  197.5 9.3 %collective-permute-start.13 = (f32[2,5,8,128]{3,2,1,0:T(8,128)S(1)}, f32[2,5,8,128]{3,2,1,0:T(8,128)S(1)}, u32[]{:S(2)}, u32[]{:S(2)}) collective-permute-start(f32[2,5,8,128]{3,2,1,0:T(8,128)S(1)} %pad_maximum_fusion.4), channel_id=1, source_target_pairs={{0,16},{8,24},{16,32},{24,40},{32,48},{40,56},{48,64},{56,72},{64,... | collective-permute-start | bytes 122888 | tf_op jit(solution)/shard_map/ppermute | solution.py:251
  202.7 4.1 %copy-start.8 = (f32[8,16,20,128]{3,1,2,0:T(8,128)}, f32[8,16,20,128]{3,1,2,0:T(8,128)S(1)}, u32[]{:S(2)}) copy-start(f32[8,16,20,128]{3,1,2,0:T(8,128)S(1)} %constant_dynamic-update-slice_fusion.75) | copy-start | bytes 3932164
  206.8 4.5 %collective-permute-start.14 = (f32[4,5,8,128]{3,2,1,0:T(8,128)S(1)}, f32[4,5,8,128]{3,2,1,0:T(8,128)S(1)}, u32[]{:S(2)}, u32[]{:S(2)}) collective-permute-start(f32[4,5,8,128]{3,2,1,0:T(8,128)S(1)} %pad_maximum_fusion.3), channel_id=1, source_target_pairs={{0,32},{8,40},{16,48},{24,56},{32,64},{40,72},{48,80},{56,88},{64,... | collective-permute-start | bytes 245768 | tf_op jit(solution)/shard_map/ppermute | solution.py:251
  212.0 16.3 %collective-permute-start.15 = (f32[8,5,8,128]{3,2,1,0:T(8,128)}, f32[8,5,8,128]{3,2,1,0:T(8,128)S(1)}, u32[]{:S(2)}, u32[]{:S(2)}) collective-permute-start(f32[8,5,8,128]{3,2,1,0:T(8,128)} %pad_maximum_fusion.2), channel_id=1, source_target_pairs={{0,64},{8,72},{16,80},{24,88},{32,96},{40,104},{48,112},{56,120},{... | collective-permute-start | bytes 491528 | tf_op jit(solution)/shard_map/ppermute | solution.py:251
  228.4 19.7 %collective-permute-start.16 = (f32[16,5,8,128]{3,2,1,0:T(8,128)S(1)}, f32[16,5,8,128]{3,2,1,0:T(8,128)S(1)}, u32[]{:S(2)}, u32[]{:S(2)}) collective-permute-start(f32[16,5,8,128]{3,2,1,0:T(8,128)S(1)} %pad_maximum_fusion.1), channel_id=1, source_target_pairs={{0,128},{8,136},{16,144},{24,152},{32,160},{40,168},{48,176},{56,1... | collective-permute-start | bytes 983048 | tf_op jit(solution)/shard_map/ppermute | solution.py:251
  229.1 22.2 %copy-start.3 = (f32[8,2,128,128]{2,3,1,0:T(8,128)S(1)}, f32[8,2,128,128]{2,3,1,0:T(8,128)}, u32[]{:S(2)}) copy-start(f32[8,2,128,128]{2,3,1,0:T(8,128)} %copy-done.2) | copy-start | bytes 3145732
  229.1 22.2 %copy-start.13 = (f32[8,128]{0,1:T(8,128)S(1)}, f32[8,128]{0,1:T(8,128)}, u32[]{:S(2)}) copy-start(f32[8,128]{0,1:T(8,128)} %copy.57) | copy-start | bytes 12292
  229.1 22.2 %copy-start.14 = (f32[8,128]{0,1:T(8,128)S(1)}, f32[8,128]{0,1:T(8,128)}, u32[]{:S(2)}) copy-start(f32[8,128]{0,1:T(8,128)} %copy.59) | copy-start | bytes 12292
where the time goes:
time: 257 us; the launch traced here: 254 us
  local copies, waits for them, and re-layouts  58 us (23%)
  waiting for transfers between devices  52.3 us (20%)
  starting transfers between devices  51.4 us (20%)
  between operations  46.7 us (18%)
  other arithmetic  40.7 us (16%)
  matrix products  2.72 us (1%)
    ppermute x5, waiting for transfers between devices, local(): held = jnp.concatenate([held, lax.ppermute(held, 'gx', ring)], axis=0)  31.9 us
    unnamed x94, local copies, waits for them, and re-layouts  26.5 us
    ppermute x8, starting transfers between devices, shifted_2(): lax.ppermute(value, axis, [(source, source + steps) for source in range(l...  25.8 us
    ppermute x8, waiting for transfers between devices, shifted_2(): lax.ppermute(value, axis, [(source, source + steps) for source in range(l...  20.3 us
    add x2, other arithmetic, interpolate(): running_total + tap_term  16 us
    ppermute x5, starting transfers between devices, local(): held = jnp.concatenate([held, lax.ppermute(held, 'gx', ring)], axis=0)  12.1 us
    reshape x2, other arithmetic, advect_group(): windows.reshape(block_count, field_count, level_count, BX + 4, rows_here...  6.42 us
    slice x2, local copies, waits for them, and re-layouts, halo_y(): low = lax.ppermute(block[:, :, block.shape[2] - width:], axis, forward)  6.07 us
  transfers between devices with their start and end apart: 17, of which 6 were waited for; matrix products, arithmetic and copies ran while one was open for 30% of the time, Pallas kernels for 0%

commit v1 on v0

--- a/solution.py
+++ b/solution.py
@@ -247,11 +247,15 @@
     held = packed[None]
     step = 1
     while step < count:
-        ring = [(i, (i + step) % count) for i in range(count)]
-        held = jnp.concatenate([held, lax.ppermute(held, "gx", ring)], axis=0)
+        parts = [held]
+        for multiple in range(1, 4):
+            if step * multiple < count:
+                ring = [(i, (i + step * multiple) % count) for i in range(count)]
+                parts.append(lax.ppermute(held, "gx", ring))
+        held = jnp.concatenate(parts, axis=0)
         if step == 1:
             held, tracer_received = lax.optimization_barrier((held, tracer_received))
-        step *= 2
+        step *= 4
     reverse = held[::-1]
     doubled = jnp.concatenate([reverse, reverse], axis=0)
     packed_all = lax.dynamic_slice_in_dim(doubled, count - 1 - position, count, 0)

time: 257 us -> 266 us (1.035)
  waiting for transfers between devices: 52.3 us -> 60.7 us
  local copies, waits for them, and re-layouts: 58 us -> 61.6 us
    ppermute x5 -> x7, waiting for transfers between devices: 31.9 us -> 40.4 us  [local(): parts.append(lax.ppermute(held, 'gx', ring))]
    unnamed x94 -> x90, local copies, waits for them, and re-layouts: 26.5 us -> 30.4 us
    ppermute x5 -> x7, starting transfers between devices: 12.1 us -> 9.87 us  [local(): parts.append(lax.ppermute(held, 'gx', ring))]
  transfers between devices with their start and end apart: 17 -> 19, of which waited for: 6 -> 7; matrix products, arithmetic and copies ran while one was open for 30% -> 31% of each run, Pallas kernels for 0% -> 0%
where the time goes in v1:
time: 266 us; the launch traced here: 264 us
  local copies, waits for them, and re-layouts  61.6 us (23%)
  waiting for transfers between devices  60.7 us (23%)
  starting transfers between devices  49.2 us (18%)
  between operations  46.6 us (18%)
  other arithmetic  40.9 us (15%)
  matrix products  2.72 us (1%)
    ppermute x7, waiting for transfers between devices, local(): parts.append(lax.ppermute(held, 'gx', ring))  40.4 us
    unnamed x90, local copies, waits for them, and re-layouts  30.4 us
    ppermute x8, starting transfers between devices, shifted_2(): lax.ppermute(value, axis, [(source, source + steps) for source in range(l...  25.8 us
    ppermute x8, waiting for transfers between devices, shifted_2(): lax.ppermute(value, axis, [(source, source + steps) for source in range(l...  20.3 us
    add x2, other arithmetic, interpolate(): running_total + tap_term  16 us
    ppermute x7, starting transfers between devices, local(): parts.append(lax.ppermute(held, 'gx', ring))  9.87 us
    reshape x2, other arithmetic, advect_group(): windows.reshape(block_count, field_count, level_count, BX + 4, rows_here...  6.42 us
    slice x2, local copies, waits for them, and re-layouts, halo_y(): low = lax.ppermute(block[:, :, block.shape[2] - width:], axis, forward)  6.07 us
  transfers between devices with their start and end apart: 19, of which 7 were waited for; matrix products, arithmetic and copies ran while one was open for 31% of the time, Pallas kernels for 0%

profile of v1, /device:TPU:34, one launch (start us, length us, event | category | flops | bytes accessed | tf_op | source)
XLA Modules:
  0.0 264.1 jit_solution(9529028267310817999)
XLA Ops:
  0.7 2.9 %copy.83 = f32[4,8,128,128]{3,1,0,2:T(8,128)S(1)} copy(f32[4,8,128,128]{3,2,1,0:T(8,128)} %param.7) | data formatting | bytes 4194304 | tf_op args[0]
  3.6 1.3 copy-done.4
  4.9 3.5 %collective-permute-start = (f32[32,2,128]{2,0,1:T(8,128)S(1)}, f32[32,2,128]{2,0,1:T(8,128)S(1)}, u32[]{:S(2)}, u32[]{:S(2)}) collective-permute-start(f32[32,2,128]{2,0,1:T(8,128)S(1)} %get-tuple-element.54), channel_id=1, source_target_pairs={{0,8},{8,16},{16,24},{24,32},{32,40},{40,48},{48,56},{56,64},{64,7... | collective-permute-start | bytes 98312 | tf_op jit(solution)/shard_map/ppermute | solution.py:117
  8.4 4.5 %collective-permute-start.1 = (f32[32,2,128]{2,0,1:T(8,128)S(1)}, f32[32,2,128]{2,0,1:T(8,128)S(1)}, u32[]{:S(2)}, u32[]{:S(2)}) collective-permute-start(f32[32,2,128]{2,0,1:T(8,128)S(1)} %get-tuple-element.55), channel_id=1, source_target_pairs={{8,0},{16,8},{24,16},{32,24},{40,32},{48,40},{56,48},{64,56},{72,6... | collective-permute-start | bytes 98312 | tf_op jit(solution)/shard_map/ppermute | solution.py:118
  15.3 3.9 %fusion.64 = (f32[8,8,16,128]{3,1,2,0:T(8,128)}, f32[8,8,16,128]{3,1,2,0:T(8,128)}, f32[8,8,16,128]{3,1,2,0:T(8,128)}, f32[8,8,16,128]{3,1,2,0:T(8,128)}, f32[8,...) fusion(f32[8,8,16,128]{3,2,1,0:T(8,128)S(1)} %bitcast.371, ...), kind=kLoop, calls=%fused_computation.134 | loop fusion | flops 9175040 | bytes 6291456 | tf_op jit(solution)/shard_map/mul | solution.py:40
  51.4 1.8 pad_maximum_fusion
  53.2 2.9 %fusion.116 = (f32[32,132,2]{2,0,1:T(8,128)}, f32[32,132,2]{2,0,1:T(8,128)}) fusion(f32[32,132,128]{2,0,1:T(8,128)S(1)} %pad_maximum_fusion), kind=kLoop, calls=%fused_computation.406 | loop fusion | bytes 135168 | tf_op jit(solution)/shard_map/slice | solution.py:126
  56.1 3.2 %copy.50 = f32[32,132,2]{1,0,2:T(8,128)S(1)} copy(f32[32,132,2]{2,0,1:T(8,128)} %get-tuple-element.52) | data formatting | bytes 67584 | tf_op jit(solution)/shard_map/slice | solution.py:126
  59.3 1.9 collective-permute-start.2
  61.3 3.2 %copy.51 = f32[32,132,2]{1,0,2:T(8,128)S(1)} copy(f32[32,132,2]{2,0,1:T(8,128)} %get-tuple-element.53) | data formatting | bytes 67584 | tf_op jit(solution)/shard_map/slice | solution.py:127
  64.5 3.6 %collective-permute-start.3 = (f32[32,132,2]{1,0,2:T(8,128)S(1)}, f32[32,132,2]{1,0,2:T(8,128)S(1)}, u32[]{:S(2)}, u32[]{:S(2)}) collective-permute-start(f32[32,132,2]{1,0,2:T(8,128)S(1)} %copy.51), channel_id=1, source_target_pairs={{1,0},{2,1},{3,2},{4,3},{5,4},{6,5},{7,6},{9,8},{10,9},{11,10},{12... | collective-permute-start | bytes 101384 | tf_op jit(solution)/shard_map/ppermute | solution.py:127
  71.4 0.9 constant_dynamic-update-slice_fusion
  72.3 3.0 %collective-permute-start.4 = (f32[16,84,128]{2,0,1:T(8,128)}, f32[16,84,128]{2,0,1:T(8,128)S(1)}, u32[]{:S(2)}, u32[]{:S(2)}) collective-permute-start(f32[16,84,128]{2,0,1:T(8,128)} %constant_dynamic-update-slice_fusion), channel_id=1, source_target_pairs={{0,16},{8,24},{16,32},{24,40},{32,48},{40,56},{48,64},{56,72},{64,... | collective-permute-start | bytes 2064392 | tf_op jit(solution)/shard_map/ppermute | solution.py:30
  91.7 2.6 collective-permute-start.5
  95.1 5.4 %collective-permute-start.6 = (f32[16,84,128]{2,0,1:T(8,128)}, f32[16,84,128]{2,0,1:T(8,128)S(1)}, u32[]{:S(2)}, u32[]{:S(2)}) collective-permute-start(f32[16,84,128]{2,0,1:T(8,128)} %constant_dynamic-update-slice_fusion.10), channel_id=1, source_target_pairs={{8,0},{16,8},{24,16},{32,24},{40,32},{48,40},{56,48},{64,56},{72,6... | collective-permute-start | bytes 2064392 | tf_op jit(solution)/shard_map/ppermute | solution.py:30
  101.2 3.3 %collective-permute-start.7 = (f32[16,84,128]{2,0,1:T(8,128)}, f32[16,84,128]{2,0,1:T(8,128)S(1)}, u32[]{:S(2)}, u32[]{:S(2)}) collective-permute-start(f32[16,84,128]{2,0,1:T(8,128)} %constant_dynamic-update-slice_fusion.15), channel_id=1, source_target_pairs={{16,0},{24,8},{32,16},{40,24},{48,32},{56,40},{64,48},{72,56},{80,... | collective-permute-start | bytes 2064392 | tf_op jit(solution)/shard_map/ppermute | solution.py:30
  104.9 8.9 %collective-permute-done.5 = f32[16,84,128]{2,0,1:T(8,128)S(1)} collective-permute-done((f32[16,84,128]{2,0,1:T(8,128)}, f32[16,84,128]{2,0,1:T(8,128)S(1)}, u32[]{:S(2)}, u32[]{:S(2)}) %collective-permute-start.5) | collective-permute-done | bytes 688160 | tf_op jit(solution)/shard_map/ppermute | solution.py:30
  114.0 0.9 constant_dynamic-update-slice_fusion.56
  114.8 0.9 constant_dynamic-update-slice_fusion.55
  115.7 0.9 constant_dynamic-update-slice_fusion.54
  116.6 0.9 constant_dynamic-update-slice_fusion.53
  118.2 2.8 %collective-permute-start.14 = (f32[16,84,128]{2,0,1:T(8,128)}, f32[16,84,128]{2,0,1:T(8,128)}, u32[]{:S(2)}, u32[]{:S(2)}) collective-permute-start(f32[16,84,128]{2,0,1:T(8,128)} %constant_dynamic-update-slice_fusion.52), channel_id=1, source_target_pairs={{16,0},{24,8},{32,16},{40,24},{48,32},{56,40},{64,48},{72,56},{80,... | collective-permute-start | bytes 2064392 | tf_op jit(solution)/shard_map/ppermute | solution.py:30
  121.7 2.2 collective-permute-start.13
  124.6 3.7 %collective-permute-start.12 = (f32[16,84,128]{2,0,1:T(8,128)}, f32[16,84,128]{2,0,1:T(8,128)}, u32[]{:S(2)}, u32[]{:S(2)}) collective-permute-start(f32[16,84,128]{2,0,1:T(8,128)} %constant_dynamic-update-slice_fusion.42), channel_id=1, source_target_pairs={{0,8},{8,16},{16,24},{24,32},{32,40},{40,48},{48,56},{56,64},{64,7... | collective-permute-start | bytes 2064392 | tf_op jit(solution)/shard_map/ppermute | solution.py:30
  129.0 1.5 collective-permute-done.6
  130.5 3.0 %collective-permute-start.11 = (f32[16,84,128]{2,0,1:T(8,128)}, f32[16,84,128]{2,0,1:T(8,128)}, u32[]{:S(2)}, u32[]{:S(2)}) collective-permute-start(f32[16,84,128]{2,0,1:T(8,128)} %constant_dynamic-update-slice_fusion.37), channel_id=1, source_target_pairs={{0,16},{8,24},{16,32},{24,40},{32,48},{40,56},{48,64},{56,72},{64,... | collective-permute-start | bytes 2064392 | tf_op jit(solution)/shard_map/ppermute | solution.py:30
  133.5 9.9 %collective-permute-done.7 = f32[16,84,128]{2,0,1:T(8,128)S(1)} collective-permute-done((f32[16,84,128]{2,0,1:T(8,128)}, f32[16,84,128]{2,0,1:T(8,128)S(1)}, u32[]{:S(2)}, u32[]{:S(2)}) %collective-permute-start.7) | collective-permute-done | bytes 688160 | tf_op jit(solution)/shard_map/ppermute | solution.py:30
  143.6 1.7 copy-done.8
  145.5 0.9 constant_dynamic-update-slice_fusion.35
  146.5 0.9 constant_dynamic-update-slice_fusion.34
  147.5 0.9 constant_dynamic-update-slice_fusion.33
  148.6 0.9 constant_dynamic-update-slice_fusion.32
  149.6 0.9 constant_dynamic-update-slice_fusion.31
  150.6 0.9 constant_dynamic-update-slice_fusion.30
  151.6 0.9 constant_dynamic-update-slice_fusion.29
  152.7 2.0 copy.52
  154.7 2.0 copy.53
  156.7 3.2 %maximum_bitcast_fusion = f32[8,2,8,20,132]{4,2,1,3,0:T(8,128)S(1)} fusion(f32[8,16,20,2]{3,1,2,0:T(8,128)} %copy.53, f32[8,16,20,128]{3,1,2,0:T(8,128)} %copy-done.7, f32[8,16,20,2]{3,1,2,0:T(8,128)} %copy.52), kind=kLoop, calls=%fused_computation | loop fusion | flops 675840 | bytes 2703360 | tf_op jit(solution)/shard_map/reshape | solution.py:206
  159.9 8.0 %fusion.31 = f32[8,2,8,16,128]{4,2,1,3,0:T(8,128)} fusion(f32[8,2,8,20,132]{4,2,1,3,0:T(8,128)S(1)} %maximum_bitcast_fusion, f32[8,8,16,128]{3,1,2,0:T(8,128)} %get-tuple-element.181, f32[8,8,16,128]{3,1,2,0:T(8,128)} %get-tuple-element.180, f32[8,8,16,128]{3,1,2,0:T(8,128)} %get-tuple-element.178, f32[8,8,16,128]{3,1,2,0:T(8,128)} %get-tuple-element.179, ...), kind=kLoop, calls=%fused_computation.63 | loop fusion | flops 14155776 | bytes 32505856 | tf_op jit(solution)/shard_map/add | solution.py:58
  167.9 2.7 %fusion.58 = f32[8,2,128,128]{2,3,1,0:T(8,128)S(1)} fusion(f32[2,8,128,128]{3,1,0,2:T(8,128)} %bitcast.369, f32[8,128,128]{2,1,0:T(8,128)} %param.11), kind=kOutput, calls=%fused_computation.115 | convolution fusion | flops 402653184 | bytes 2621440 | tf_op jit(solution)/shard_map/lij,wljy->wliy/dot_general | solution.py:234
  170.6 1.0 copy-done.2
  172.3 15.4 %collective-permute-done.10 = f32[1,5,8,128]{3,2,1,0:T(8,128)S(1)} collective-permute-done((f32[1,5,8,128]{3,2,1,0:T(8,128)S(1)}, f32[1,5,8,128]{3,2,1,0:T(8,128)S(1)}, u32[]{:S(2)}, u32[]{:S(2)}) %collective-permute-start.10) | collective-permute-done | bytes 20512 | tf_op jit(solution)/shard_map/ppermute | solution.py:254
  187.7 5.9 %collective-permute-done.8 = f32[1,5,8,128]{3,2,1,0:T(8,128)S(1)} collective-permute-done((f32[1,5,8,128]{3,2,1,0:T(8,128)S(1)}, f32[1,5,8,128]{3,2,1,0:T(8,128)S(1)}, u32[]{:S(2)}, u32[]{:S(2)}) %collective-permute-start.8) | collective-permute-done | bytes 20512 | tf_op jit(solution)/shard_map/ppermute | solution.py:254
  195.8 4.0 %collective-permute-done.9 = f32[1,5,8,128]{3,2,1,0:T(8,128)S(1)} collective-permute-done((f32[1,5,8,128]{3,2,1,0:T(8,128)S(1)}, f32[1,5,8,128]{3,2,1,0:T(8,128)S(1)}, u32[]{:S(2)}, u32[]{:S(2)}) %collective-permute-start.9) | collective-permute-done | bytes 20512 | tf_op jit(solution)/shard_map/ppermute | solution.py:254
  199.8 1.1 slice.448
  201.7 1.1 slice.447
  203.6 1.1 slice.446
  204.7 0.9 slice.450
  205.6 1.1 slice.445
  207.5 1.0 collective-permute-start.15
  208.5 6.9 %collective-permute-start.16 = (f32[4,5,8,128]{3,2,1,0:T(8,128)S(1)}, f32[4,5,8,128]{3,2,1,0:T(8,128)S(1)}, u32[]{:S(2)}, u32[]{:S(2)}) collective-permute-start(f32[4,5,8,128]{3,2,1,0:T(8,128)S(1)} %pad_maximum_fusion.2), channel_id=1, source_target_pairs={{0,64},{8,72},{16,80},{24,88},{32,96},{40,104},{48,112},{56,120},{... | collective-permute-start | bytes 245768 | tf_op jit(solution)/shard_map/ppermute | solution.py:254
  222.0 2.1 copy.60
  224.1 2.0 copy.61
  226.1 3.2 %maximum_bitcast_fusion.1 = f32[8,2,8,20,132]{4,2,1,3,0:T(8,128)S(1)} fusion(f32[8,16,20,2]{3,1,2,0:T(8,128)} %copy.61, f32[8,16,20,128]{3,1,2,0:T(8,128)} %constant_dynamic-update-slice_fusion.75, f32[8,16,20,2]{3,1,2,0:T(8,128)} %copy.60), kind=kLoop, calls=%fused_computation.1 | loop fusion | flops 675840 | bytes 2703360 | tf_op jit(solution)/shard_map/reshape | solution.py:206
  229.3 8.0 %fusion.2 = f32[8,2,8,16,128]{4,2,1,3,0:T(8,128)} fusion(f32[8,2,8,20,132]{4,2,1,3,0:T(8,128)S(1)} %maximum_bitcast_fusion.1, f32[8,8,16,128]{3,1,2,0:T(8,128)} %get-tuple-element.181, f32[8,8,16,128]{3,1,2,0:T(8,128)} %get-tuple-element.180, f32[8,8,16,128]{3,1,2,0:T(8,128)} %get-tuple-element.178, f32[8,8,16,128]{3,1,2,0:T(8,128)} %get-tuple-element.179, ...), kind=kLoop, calls=%fused_computation.9 | loop fusion | flops 14155776 | bytes 32505856 | tf_op jit(solution)/shard_map/add | solution.py:58
  237.3 2.5 copy.63
  239.9 0.9 pad_maximum_fusion.1
  240.8 1.2 collective-permute-start.18
  242.0 1.0 constant_dynamic-update-slice_fusion.58
  243.0 15.1 %collective-permute-done.18 = f32[16,5,8,128]{3,2,1,0:T(8,128)S(1)} collective-permute-done((f32[16,5,8,128]{3,2,1,0:T(8,128)S(1)}, f32[16,5,8,128]{3,2,1,0:T(8,128)S(1)}, u32[]{:S(2)}, u32[]{:S(2)}) %collective-permute-start.18) | collective-permute-done | bytes 327712 | tf_op jit(solution)/shard_map/ppermute | solution.py:254
  258.2 1.0 fusion.60.packed_ref
  259.1 2.2 shard_map.86
  261.4 1.4 multiply_subtract_fusion
  262.8 1.3 copy.62
  (149 shorter events, 26.6 us)
Async XLA Ops:
  0.6 12.3 %copy-start.13 = (s32[256,1]{0,1:T(1,128)S(1)}, s32[256,1]{0,1:T(1,128)}, u32[]{:S(2)}) copy-start(s32[256,1]{0,1:T(1,128)} %param.10) | copy-start | bytes 3076
  0.6 13.9 %copy-start.9 = (f32[8,128,128]{2,1,0:T(8,128)S(1)}, f32[8,128,128]{2,1,0:T(8,128)}, u32[]{:S(2)}) copy-start(f32[8,128,128]{2,1,0:T(8,128)} %param.8) | copy-start | bytes 1572868
  0.7 14.0 %copy-start.10 = (f32[8,128,128]{2,1,0:T(8,128)S(1)}, f32[8,128,128]{2,1,0:T(8,128)}, u32[]{:S(2)}) copy-start(f32[8,128,128]{2,1,0:T(8,128)} %param.9) | copy-start | bytes 1572868
  3.6 1.4 copy-start.4
  3.6 11.1 %copy-start.6 = (f32[8,128,128]{2,1,0:T(8,128)S(1)}, f32[8,128,128]{2,1,0:T(8,128)}, u32[]{:S(2)}) copy-start(f32[8,128,128]{2,1,0:T(8,128)} %param.11) | copy-start | bytes 1572868
  4.9 46.4 %collective-permute-start = (f32[32,2,128]{2,0,1:T(8,128)S(1)}, f32[32,2,128]{2,0,1:T(8,128)S(1)}, u32[]{:S(2)}, u32[]{:S(2)}) collective-permute-start(f32[32,2,128]{2,0,1:T(8,128)S(1)} %get-tuple-element.54), channel_id=1, source_target_pairs={{0,8},{8,16},{16,24},{24,32},{32,40},{40,48},{48,56},{56,64},{64,7... | collective-permute-start | bytes 98312 | tf_op jit(solution)/shard_map/ppermute | solution.py:117
  8.4 43.0 %collective-permute-start.1 = (f32[32,2,128]{2,0,1:T(8,128)S(1)}, f32[32,2,128]{2,0,1:T(8,128)S(1)}, u32[]{:S(2)}, u32[]{:S(2)}) collective-permute-start(f32[32,2,128]{2,0,1:T(8,128)S(1)} %get-tuple-element.55), channel_id=1, source_target_pairs={{8,0},{16,8},{24,16},{32,24},{40,32},{48,40},{56,48},{64,56},{72,6... | collective-permute-start | bytes 98312 | tf_op jit(solution)/shard_map/ppermute | solution.py:118
  15.3 3.9 %copy-start.17 = (f32[8,1]{0,1:T(1,128)S(1)}, f32[8,1]{0,1:T(1,128)}, u32[]{:S(2)}) copy-start(f32[8,1]{0,1:T(1,128)} %param.13) | copy-start | bytes 100
  15.3 4.0 %copy-start.18 = (f32[8,1]{0,1:T(1,128)S(1)}, f32[8,1]{0,1:T(1,128)}, u32[]{:S(2)}) copy-start(f32[8,1]{0,1:T(1,128)} %param.12) | copy-start | bytes 100
  53.1 60.7 %copy-start = (f32[32,132,128]{2,0,1:T(8,128)}, f32[32,132,128]{2,0,1:T(8,128)S(1)}, u32[]{:S(2)}) copy-start(f32[32,132,128]{2,0,1:T(8,128)S(1)} %pad_maximum_fusion) | copy-start | bytes 6488068
  59.3 11.7 %collective-permute-start.2 = (f32[32,132,2]{1,0,2:T(8,128)S(1)}, f32[32,132,2]{1,0,2:T(8,128)S(1)}, u32[]{:S(2)}, u32[]{:S(2)}) collective-permute-start(f32[32,132,2]{1,0,2:T(8,128)S(1)} %copy.50), channel_id=1, source_target_pairs={{0,1},{1,2},{2,3},{3,4},{4,5},{5,6},{6,7},{8,9},{9,10},{10,11},{11... | collective-permute-start | bytes 101384 | tf_op jit(solution)/shard_map/ppermute | solution.py:126
  64.5 6.5 %collective-permute-start.3 = (f32[32,132,2]{1,0,2:T(8,128)S(1)}, f32[32,132,2]{1,0,2:T(8,128)S(1)}, u32[]{:S(2)}, u32[]{:S(2)}) collective-permute-start(f32[32,132,2]{1,0,2:T(8,128)S(1)} %copy.51), channel_id=1, source_target_pairs={{1,0},{2,1},{3,2},{4,3},{5,4},{6,5},{7,6},{9,8},{10,9},{11,10},{12... | collective-permute-start | bytes 101384 | tf_op jit(solution)/shard_map/ppermute | solution.py:127
  71.0 5.0 %copy-start.14 = (f32[16,84,128]{2,0,1:T(8,128)}, f32[16,84,128]{2,0,1:T(8,128)S(1)}, u32[]{:S(2)}) copy-start(f32[16,84,128]{2,0,1:T(8,128)S(1)} %get-tuple-element.72) | copy-start | bytes 2064388
  71.0 5.0 %copy-start.15 = (f32[16,84,128]{2,0,1:T(8,128)}, f32[16,84,128]{2,0,1:T(8,128)S(1)}, u32[]{:S(2)}) copy-start(f32[16,84,128]{2,0,1:T(8,128)S(1)} %get-tuple-element.73) | copy-start | bytes 2064388
  71.0 5.0 %copy-start.16 = (f32[16,84,128]{2,0,1:T(8,128)}, f32[16,84,128]{2,0,1:T(8,128)S(1)}, u32[]{:S(2)}) copy-start(f32[16,84,128]{2,0,1:T(8,128)S(1)} %get-tuple-element.74) | copy-start | bytes 2064388
  72.3 32.5 %collective-permute-start.4 = (f32[16,84,128]{2,0,1:T(8,128)}, f32[16,84,128]{2,0,1:T(8,128)S(1)}, u32[]{:S(2)}, u32[]{:S(2)}) collective-permute-start(f32[16,84,128]{2,0,1:T(8,128)} %constant_dynamic-update-slice_fusion), channel_id=1, source_target_pairs={{0,16},{8,24},{16,32},{24,40},{32,48},{40,56},{48,64},{56,72},{64,... | collective-permute-start | bytes 2064392 | tf_op jit(solution)/shard_map/ppermute | solution.py:30
  91.7 22.0 %collective-permute-start.5 = (f32[16,84,128]{2,0,1:T(8,128)}, f32[16,84,128]{2,0,1:T(8,128)S(1)}, u32[]{:S(2)}, u32[]{:S(2)}) collective-permute-start(f32[16,84,128]{2,0,1:T(8,128)} %constant_dynamic-update-slice_fusion.5), channel_id=1, source_target_pairs={{0,8},{8,16},{16,24},{24,32},{32,40},{40,48},{48,56},{56,64},{64,7... | collective-permute-start | bytes 2064392 | tf_op jit(solution)/shard_map/ppermute | solution.py:30
  95.1 35.4 %collective-permute-start.6 = (f32[16,84,128]{2,0,1:T(8,128)}, f32[16,84,128]{2,0,1:T(8,128)S(1)}, u32[]{:S(2)}, u32[]{:S(2)}) collective-permute-start(f32[16,84,128]{2,0,1:T(8,128)} %constant_dynamic-update-slice_fusion.10), channel_id=1, source_target_pairs={{8,0},{16,8},{24,16},{32,24},{40,32},{48,40},{56,48},{64,56},{72,6... | collective-permute-start | bytes 2064392 | tf_op jit(solution)/shard_map/ppermute | solution.py:30
  101.2 42.3 %collective-permute-start.7 = (f32[16,84,128]{2,0,1:T(8,128)}, f32[16,84,128]{2,0,1:T(8,128)S(1)}, u32[]{:S(2)}, u32[]{:S(2)}) collective-permute-start(f32[16,84,128]{2,0,1:T(8,128)} %constant_dynamic-update-slice_fusion.15), channel_id=1, source_target_pairs={{16,0},{24,8},{32,16},{40,24},{48,32},{56,40},{64,48},{72,56},{80,... | collective-permute-start | bytes 2064392 | tf_op jit(solution)/shard_map/ppermute | solution.py:30
  118.2 81.6 %collective-permute-start.14 = (f32[16,84,128]{2,0,1:T(8,128)}, f32[16,84,128]{2,0,1:T(8,128)}, u32[]{:S(2)}, u32[]{:S(2)}) collective-permute-start(f32[16,84,128]{2,0,1:T(8,128)} %constant_dynamic-update-slice_fusion.52), channel_id=1, source_target_pairs={{16,0},{24,8},{32,16},{40,24},{48,32},{56,40},{64,48},{72,56},{80,... | collective-permute-start | bytes 2064392 | tf_op jit(solution)/shard_map/ppermute | solution.py:30
  121.7 80.0 %collective-permute-start.13 = (f32[16,84,128]{2,0,1:T(8,128)}, f32[16,84,128]{2,0,1:T(8,128)}, u32[]{:S(2)}, u32[]{:S(2)}) collective-permute-start(f32[16,84,128]{2,0,1:T(8,128)} %constant_dynamic-update-slice_fusion.47), channel_id=1, source_target_pairs={{8,0},{16,8},{24,16},{32,24},{40,32},{48,40},{56,48},{64,56},{72,6... | collective-permute-start | bytes 2064392 | tf_op jit(solution)/shard_map/ppermute | solution.py:30
  124.6 79.0 %collective-permute-start.12 = (f32[16,84,128]{2,0,1:T(8,128)}, f32[16,84,128]{2,0,1:T(8,128)}, u32[]{:S(2)}, u32[]{:S(2)}) collective-permute-start(f32[16,84,128]{2,0,1:T(8,128)} %constant_dynamic-update-slice_fusion.42), channel_id=1, source_target_pairs={{0,8},{8,16},{16,24},{24,32},{32,40},{40,48},{48,56},{56,64},{64,7... | collective-permute-start | bytes 2064392 | tf_op jit(solution)/shard_map/ppermute | solution.py:30
  130.5 75.1 %collective-permute-start.11 = (f32[16,84,128]{2,0,1:T(8,128)}, f32[16,84,128]{2,0,1:T(8,128)}, u32[]{:S(2)}, u32[]{:S(2)}) collective-permute-start(f32[16,84,128]{2,0,1:T(8,128)} %constant_dynamic-update-slice_fusion.37), channel_id=1, source_target_pairs={{0,16},{8,24},{16,32},{24,40},{32,48},{40,56},{48,64},{56,72},{64,... | collective-permute-start | bytes 2064392 | tf_op jit(solution)/shard_map/ppermute | solution.py:30
  143.5 1.8 copy-start.8
  152.5 2.1 copy-start.7
  156.7 3.2 %copy-start.5 = (f32[8,8,16,128]{3,1,2,0:T(8,128)S(1)}, f32[8,8,16,128]{3,1,2,0:T(8,128)}, u32[]{:S(2)}) copy-start(f32[8,8,16,128]{3,1,2,0:T(8,128)} %get-tuple-element.95) | copy-start | bytes 1572868
  170.6 1.0 copy-start.2
  172.2 15.5 %collective-permute-start.10 = (f32[1,5,8,128]{3,2,1,0:T(8,128)S(1)}, f32[1,5,8,128]{3,2,1,0:T(8,128)S(1)}, u32[]{:S(2)}, u32[]{:S(2)}) collective-permute-start(f32[1,5,8,128]{3,2,1,0:T(8,128)S(1)} %maximum_bitcast_fusion.3), channel_id=1, source_target_pairs={{0,24},{8,32},{16,40},{24,48},{32,56},{40,64},{48,72},{56,80},{64,... | collective-permute-start | bytes 61448 | tf_op jit(solution)/shard_map/ppermute | solution.py:254
  187.7 5.9 %collective-permute-start.8 = (f32[1,5,8,128]{3,2,1,0:T(8,128)S(1)}, f32[1,5,8,128]{3,2,1,0:T(8,128)S(1)}, u32[]{:S(2)}, u32[]{:S(2)}) collective-permute-start(f32[1,5,8,128]{3,2,1,0:T(8,128)S(1)} %maximum_bitcast_fusion.3), channel_id=1, source_target_pairs={{0,8},{8,16},{16,24},{24,32},{32,40},{40,48},{48,56},{56,64},{64,7... | collective-permute-start | bytes 61448 | tf_op jit(solution)/shard_map/ppermute | solution.py:254
  193.6 6.2 %collective-permute-start.9 = (f32[1,5,8,128]{3,2,1,0:T(8,128)S(1)}, f32[1,5,8,128]{3,2,1,0:T(8,128)S(1)}, u32[]{:S(2)}, u32[]{:S(2)}) collective-permute-start(f32[1,5,8,128]{3,2,1,0:T(8,128)S(1)} %maximum_bitcast_fusion.3), channel_id=1, source_target_pairs={{0,16},{8,24},{16,32},{24,40},{32,48},{40,56},{48,64},{56,72},{64,... | collective-permute-start | bytes 61448 | tf_op jit(solution)/shard_map/ppermute | solution.py:254
  204.7 10.8 %copy-start.1 = (f32[32,132,128]{2,0,1:T(8,128)S(1)}, f32[32,132,128]{2,0,1:T(8,128)}, u32[]{:S(2)}) copy-start(f32[32,132,128]{2,0,1:T(8,128)} %copy-done) | copy-start | bytes 6488068
  207.5 32.3 %collective-permute-start.15 = (f32[4,5,8,128]{3,2,1,0:T(8,128)S(1)}, f32[4,5,8,128]{3,2,1,0:T(8,128)S(1)}, u32[]{:S(2)}, u32[]{:S(2)}) collective-permute-start(f32[4,5,8,128]{3,2,1,0:T(8,128)S(1)} %pad_maximum_fusion.2), channel_id=1, source_target_pairs={{0,32},{8,40},{16,48},{24,56},{32,64},{40,72},{48,80},{56,88},{64,... | collective-permute-start | bytes 245768 | tf_op jit(solution)/shard_map/ppermute | solution.py:254
  208.5 31.3 %collective-permute-start.16 = (f32[4,5,8,128]{3,2,1,0:T(8,128)S(1)}, f32[4,5,8,128]{3,2,1,0:T(8,128)S(1)}, u32[]{:S(2)}, u32[]{:S(2)}) collective-permute-start(f32[4,5,8,128]{3,2,1,0:T(8,128)S(1)} %pad_maximum_fusion.2), channel_id=1, source_target_pairs={{0,64},{8,72},{16,80},{24,88},{32,96},{40,104},{48,112},{56,120},{... | collective-permute-start | bytes 245768 | tf_op jit(solution)/shard_map/ppermute | solution.py:254
  215.4 24.4 %collective-permute-start.17 = (f32[4,5,8,128]{3,2,1,0:T(8,128)S(1)}, f32[4,5,8,128]{3,2,1,0:T(8,128)}, u32[]{:S(2)}, u32[]{:S(2)}) collective-permute-start(f32[4,5,8,128]{3,2,1,0:T(8,128)S(1)} %pad_maximum_fusion.2), channel_id=1, source_target_pairs={{0,96},{8,104},{16,112},{24,120},{32,128},{40,136},{48,144},{56,15... | collective-permute-start | bytes 245768 | tf_op jit(solution)/shard_map/ppermute | solution.py:254
  240.8 17.3 %collective-permute-start.18 = (f32[16,5,8,128]{3,2,1,0:T(8,128)S(1)}, f32[16,5,8,128]{3,2,1,0:T(8,128)S(1)}, u32[]{:S(2)}, u32[]{:S(2)}) collective-permute-start(f32[16,5,8,128]{3,2,1,0:T(8,128)S(1)} %pad_maximum_fusion.1), channel_id=1, source_target_pairs={{0,128},{8,136},{16,144},{24,152},{32,160},{40,168},{48,176},{56,1... | collective-permute-start | bytes 983048 | tf_op jit(solution)/shard_map/ppermute | solution.py:254
  242.0 19.4 %copy-start.3 = (f32[8,2,128,128]{2,3,1,0:T(8,128)S(1)}, f32[8,2,128,128]{2,3,1,0:T(8,128)}, u32[]{:S(2)}) copy-start(f32[8,2,128,128]{2,3,1,0:T(8,128)} %copy-done.2) | copy-start | bytes 3145732
  242.0 19.4 %copy-start.11 = (f32[8,128]{0,1:T(8,128)S(1)}, f32[8,128]{0,1:T(8,128)}, u32[]{:S(2)}) copy-start(f32[8,128]{0,1:T(8,128)} %copy.57) | copy-start | bytes 12292
  242.0 19.4 %copy-start.12 = (f32[8,128]{0,1:T(8,128)S(1)}, f32[8,128]{0,1:T(8,128)}, u32[]{:S(2)}) copy-start(f32[8,128]{0,1:T(8,128)} %copy.59) | copy-start | bytes 12292

commit v2 on v0

--- a/solution.py
+++ b/solution.py
@@ -219,9 +219,13 @@
     wind_channels = 2 * level_count
     count = lax.axis_size("gx")
     position = lax.axis_index("gx")
-    flat = fields.reshape(channels, columns, rows_here)
-    main = halo_x(flat, "gx", 2)
-    halo = halo_y(main, "gy", 2).transpose(0, 2, 1)
+    padded = padded_2(fields, (("gx", 2), ("gy", 3)), 2).reshape(
+        channels, columns + 4, rows_here + 4
+    )
+    main = padded[:, :, 2 : rows_here + 2]
+    halo = jnp.concatenate(
+        [padded[:, :, 0:2], padded[:, :, rows_here + 2 :]], axis=2
+    ).transpose(0, 2, 1)
     offsets = block_offset[:, 0]
     wind_main, wind_halo = main[:wind_channels], halo[:wind_channels]
     tracer_main, tracer_halo = main[wind_channels:], halo[wind_channels:]

time: 257 us -> 275 us (1.070)
  local copies, waits for them, and re-layouts: 58 us -> 73.1 us
  other arithmetic: 40.7 us -> 47.2 us
  waiting for transfers between devices: 52.3 us -> 49.2 us
    concatenate x0 -> x1, local copies, waits for them, and re-layouts: none -> 6.1 us  [padded_2(): block = jnp.concatenate([low, block, high], axis=dim)]
    ppermute x0 -> x2, local copies, waits for them, and re-layouts: none -> 3.96 us  [the longest x1 2.01 us: padded_2(): lax.ppermute(lax.slice_in_dim(block, 0, width, axis=dim), axis, backward)]
    ppermute x8, waiting for transfers between devices: 20.3 us -> 16.5 us  [shifted_2(): lax.ppermute(value, axis, [(source, source + steps) for source in range(l...]
    concatenate x1, other arithmetic: 1.77 us -> 5.03 us  [padded_2(): block = jnp.concatenate([low, block, high], axis=dim)]
    slice x2, local copies, waits for them, and re-layouts: 0.15 us -> 2.92 us  [local(): tracer_main, tracer_halo = (main[wind_channels:], halo[wind_channels:])]
    unnamed x94 -> x82, local copies, waits for them, and re-layouts: 26.5 us -> 26.1 us
  transfers between devices with their start and end apart: 17 -> 17, of which waited for: 6 -> 5; matrix products, arithmetic and copies ran while one was open for 30% -> 29% of each run, Pallas kernels for 0% -> 0%
where the time goes in v2:
time: 275 us; the launch traced here: 272 us
  local copies, waits for them, and re-layouts  73.1 us (27%)
  starting transfers between devices  52.1 us (19%)
  waiting for transfers between devices  49.2 us (18%)
  other arithmetic  47.2 us (17%)
  between operations  46 us (17%)
    ppermute x5, waiting for transfers between devices, local(): held = jnp.concatenate([held, lax.ppermute(held, 'gx', ring)], axis=0)  32.7 us
    ppermute x8, starting transfers between devices, shifted_2(): lax.ppermute(value, axis, [(source, source + steps) for source in range(l...  27.4 us
    unnamed x82, local copies, waits for them, and re-layouts  26.1 us
    ppermute x8, waiting for transfers between devices, shifted_2(): lax.ppermute(value, axis, [(source, source + steps) for source in range(l...  16.5 us
    add x2, other arithmetic, interpolate(): running_total + tap_term  16 us
    ppermute x5, starting transfers between devices, local(): held = jnp.concatenate([held, lax.ppermute(held, 'gx', ring)], axis=0)  10.9 us
    ppermute x2, starting transfers between devices, padded_2(): lax.ppermute(lax.slice_in_dim(block, 0, width, axis=dim), axis, backward)  8.29 us
    slice x2, local copies, waits for them, and re-layouts, local(): padded[:, :, 0:2]  7.58 us
  transfers between devices with their start and end apart: 17, of which 5 were waited for; matrix products, arithmetic and copies ran while one was open for 29% of the time, Pallas kernels for 0%

profile of v2, /device:TPU:34, one launch (start us, length us, event | category | flops | bytes accessed | tf_op | source)
XLA Modules:
  0.0 272.4 jit_solution(13744024970931316274)
XLA Ops:
  0.6 1.1 fusion.117
  1.7 3.5 %collective-permute-start = (f32[4,8,2,128]{3,1,2,0:T(8,128)S(1)}, f32[4,8,2,128]{3,1,2,0:T(8,128)S(1)}, u32[]{:S(2)}, u32[]{:S(2)}) collective-permute-start(f32[4,8,2,128]{3,1,2,0:T(8,128)S(1)} %copy.90), channel_id=1, source_target_pairs={{0,8},{8,16},{16,24},{24,32},{32,40},{40,48},{48,56},{56,64},{64,7... | collective-permute-start | bytes 98312 | tf_op jit(solution)/shard_map/ppermute | solution.py:19
  5.2 4.5 %collective-permute-start.1 = (f32[4,8,2,128]{3,1,2,0:T(8,128)S(1)}, f32[4,8,2,128]{3,1,2,0:T(8,128)S(1)}, u32[]{:S(2)}, u32[]{:S(2)}) collective-permute-start(f32[4,8,2,128]{3,1,2,0:T(8,128)S(1)} %copy.91), channel_id=1, source_target_pairs={{8,0},{16,8},{24,16},{32,24},{40,32},{48,40},{56,48},{64,56},{72,6... | collective-permute-start | bytes 98312 | tf_op jit(solution)/shard_map/ppermute | solution.py:22
  12.6 1.1 neg.22
  13.7 1.1 neg.25
  15.4 3.9 %fusion.64 = (f32[8,8,16,128]{3,1,2,0:T(8,128)}, f32[8,8,16,128]{3,1,2,0:T(8,128)}, f32[8,8,16,128]{3,1,2,0:T(8,128)}, f32[8,8,16,128]{3,1,2,0:T(8,128)}, f32[8,...) fusion(f32[8,8,16,128]{3,2,1,0:T(8,128)S(1)} %bitcast.371, ...), kind=kLoop, calls=%fused_computation.133 | loop fusion | flops 9175040 | bytes 6291456 | tf_op jit(solution)/shard_map/mul | solution.py:40
  20.4 2.0 copy.72
  22.8 2.0 copy.71
  24.7 2.0 copy.73
  27.7 1.9 collective-permute-start.2
  29.6 3.8 %collective-permute-start.3 = (f32[4,8,132,2]{2,1,3,0:T(8,128)S(1)}, f32[4,8,132,2]{2,1,3,0:T(8,128)S(1)}, u32[]{:S(2)}, u32[]{:S(2)}) collective-permute-start(f32[4,8,132,2]{2,1,3,0:T(8,128)S(1)} %get-tuple-element.53), channel_id=1, source_target_pairs={{1,0},{2,1},{3,2},{4,3},{5,4},{6,5},{7,6},{9,8},{10,9},{11,10},{12... | collective-permute-start | bytes 101384 | tf_op jit(solution)/shard_map/ppermute | solution.py:22
  64.1 5.0 %pad_maximum_fusion = f32[4,8,132,132]{2,1,3,0:T(8,128)} fusion(f32[4,8,132,2]{2,1,3,0:T(8,128)S(1)} %collective-permute-done.3, f32[4,8,2,128]{2,1,3,0:T(8,128)} %copy.73, f32[4,8,128,128]{2,1,3,0:T(8,128)S(1)} %copy.72, f32[4,8,2,128]{2,1,3,0:T(8,128)} %copy.71, f32[4,8,132,2]{2,1,3,0:T(8,128)S(1)} %collective-permute-done.2), kind=kLoop, calls=%fused_computation | loop fusion | flops 2230272 | bytes 4460544 | tf_op jit(solution)/shard_map/concatenate | solution.py:23
  69.2 6.1 %copy.74 = f32[4,8,132,132]{3,1,0,2:T(8,128)} copy(f32[4,8,132,132]{2,1,3,0:T(8,128)} %pad_maximum_fusion) | data formatting | bytes 4460544 | tf_op jit(solution)/shard_map/concatenate | solution.py:23
  75.3 4.4 %fusion.116 = (f32[32,132,2]{2,0,1:T(8,128)}, f32[32,132,2]{2,0,1:T(8,128)S(1)}) fusion(f32[32,132,132]{2,0,1:T(8,128)} %bitcast.364), kind=kLoop, calls=%fused_computation.410 | loop fusion | bytes 135168 | tf_op jit(solution)/shard_map/slice | solution.py:227
  79.6 2.0 slice.411
  81.6 3.2 %copy.75 = f32[32,132,2]{1,0,2:T(8,128)S(1)} copy(f32[32,132,2]{2,0,1:T(8,128)} %get-tuple-element.56) | data formatting | bytes 67584 | tf_op jit(solution)/shard_map/slice | solution.py:227
  84.8 1.7 copy.76
  90.6 3.0 %collective-permute-start.4 = (f32[16,84,128]{2,0,1:T(8,128)}, f32[16,84,128]{2,0,1:T(8,128)S(1)}, u32[]{:S(2)}, u32[]{:S(2)}) collective-permute-start(f32[16,84,128]{2,0,1:T(8,128)} %constant_dynamic-update-slice_fusion), channel_id=1, source_target_pairs={{0,16},{8,24},{16,32},{24,40},{32,48},{40,56},{48,64},{56,72},{64,... | collective-permute-start | bytes 2064392 | tf_op jit(solution)/shard_map/ppermute | solution.py:30
  109.8 2.6 collective-permute-start.5
  112.6 5.4 %collective-permute-start.6 = (f32[16,84,128]{2,0,1:T(8,128)S(1)}, f32[16,84,128]{2,0,1:T(8,128)S(1)}, u32[]{:S(2)}, u32[]{:S(2)}) collective-permute-start(f32[16,84,128]{2,0,1:T(8,128)S(1)} %constant_dynamic-update-slice_fusion.10), channel_id=1, source_target_pairs={{8,0},{16,8},{24,16},{32,24},{40,32},{48,40},{56,48},{64,56},{72,6... | collective-permute-start | bytes 2064392 | tf_op jit(solution)/shard_map/ppermute | solution.py:30
  118.1 3.1 %collective-permute-start.7 = (f32[16,84,128]{2,0,1:T(8,128)S(1)}, f32[16,84,128]{2,0,1:T(8,128)S(1)}, u32[]{:S(2)}, u32[]{:S(2)}) collective-permute-start(f32[16,84,128]{2,0,1:T(8,128)S(1)} %constant_dynamic-update-slice_fusion.15), channel_id=1, source_target_pairs={{16,0},{24,8},{32,16},{40,24},{48,32},{56,40},{64,48},{72,56},{80,... | collective-permute-start | bytes 2064392 | tf_op jit(solution)/shard_map/ppermute | solution.py:30
  121.6 10.0 %collective-permute-done.5 = f32[16,84,128]{2,0,1:T(8,128)S(1)} collective-permute-done((f32[16,84,128]{2,0,1:T(8,128)}, f32[16,84,128]{2,0,1:T(8,128)S(1)}, u32[]{:S(2)}, u32[]{:S(2)}) %collective-permute-start.5) | collective-permute-done | bytes 688160 | tf_op jit(solution)/shard_map/ppermute | solution.py:30
  131.6 2.9 %fusion.115 = (f32[16,132,128]{2,0,1:T(8,128)S(1)}, f32[16,452,128]{2,0,1:T(8,128)S(1)}) fusion(f32[32,132,132]{2,0,1:T(8,128)} %bitcast.366, f32[16,452,128]{2,0,1:T(8,128)S(1)} %slice_dynamic-update-slice_fusion.2), kind=kLoop, calls=%fused_computation.409 | loop fusion | bytes 4325376 | tf_op jit(solution)/shard_map/slice | solution.py:231
  138.7 2.5 collective-permute-start.12
  141.9 2.2 collective-permute-start.11
  144.8 3.7 %collective-permute-start.10 = (f32[16,84,128]{2,0,1:T(8,128)}, f32[16,84,128]{2,0,1:T(8,128)}, u32[]{:S(2)}, u32[]{:S(2)}) collective-permute-start(f32[16,84,128]{2,0,1:T(8,128)} %constant_dynamic-update-slice_fusion.42), channel_id=1, source_target_pairs={{0,8},{8,16},{16,24},{24,32},{32,40},{40,48},{48,56},{56,64},{64,7... | collective-permute-start | bytes 2064392 | tf_op jit(solution)/shard_map/ppermute | solution.py:30
  149.2 5.0 %collective-permute-start.9 = (f32[16,84,128]{2,0,1:T(8,128)}, f32[16,84,128]{2,0,1:T(8,128)}, u32[]{:S(2)}, u32[]{:S(2)}) collective-permute-start(f32[16,84,128]{2,0,1:T(8,128)} %constant_dynamic-update-slice_fusion.37), channel_id=1, source_target_pairs={{0,16},{8,24},{16,32},{24,40},{32,48},{40,56},{48,64},{56,72},{64,... | collective-permute-start | bytes 2064392 | tf_op jit(solution)/shard_map/ppermute | solution.py:30
  154.3 6.5 %collective-permute-done.7 = f32[16,84,128]{2,0,1:T(8,128)S(1)} collective-permute-done((f32[16,84,128]{2,0,1:T(8,128)S(1)}, f32[16,84,128]{2,0,1:T(8,128)S(1)}, u32[]{:S(2)}, u32[]{:S(2)}) %collective-permute-start.7) | collective-permute-done | bytes 688160 | tf_op jit(solution)/shard_map/ppermute | solution.py:30
  160.9 1.7 copy-done.6
  162.9 0.9 constant_dynamic-update-slice_fusion.35
  163.9 0.9 constant_dynamic-update-slice_fusion.34
  164.9 0.9 constant_dynamic-update-slice_fusion.33
  165.9 0.9 constant_dynamic-update-slice_fusion.32
  166.9 0.9 constant_dynamic-update-slice_fusion.31
  167.9 0.9 constant_dynamic-update-slice_fusion.30
  169.0 0.9 constant_dynamic-update-slice_fusion.29
  170.0 2.0 copy.77
  172.0 2.0 copy.78
  174.0 3.2 %maximum_bitcast_fusion = f32[8,2,8,20,132]{4,2,1,3,0:T(8,128)S(1)} fusion(f32[8,16,20,2]{3,1,2,0:T(8,128)} %copy.78, f32[8,16,20,128]{3,1,2,0:T(8,128)} %copy-done.4, f32[8,16,20,2]{3,1,2,0:T(8,128)} %copy.77), kind=kLoop, calls=%fused_computation.1 | loop fusion | flops 675840 | bytes 2703360 | tf_op jit(solution)/shard_map/reshape | solution.py:206
  177.3 8.0 %fusion.31 = f32[8,2,8,16,128]{4,2,1,3,0:T(8,128)} fusion(f32[8,2,8,20,132]{4,2,1,3,0:T(8,128)S(1)} %maximum_bitcast_fusion, f32[8,8,16,128]{3,1,2,0:T(8,128)} %get-tuple-element.185, f32[8,8,16,128]{3,1,2,0:T(8,128)} %get-tuple-element.184, f32[8,8,16,128]{3,1,2,0:T(8,128)} %get-tuple-element.182, f32[8,8,16,128]{3,1,2,0:T(8,128)} %get-tuple-element.183, ...), kind=kLoop, calls=%fused_computation.62 | loop fusion | flops 14155776 | bytes 32505856 | tf_op jit(solution)/shard_map/add | solution.py:58
  185.2 2.7 fusion.58
  188.0 1.0 copy-done
  191.1 13.8 %collective-permute-done.8 = f32[1,5,8,128]{3,2,1,0:T(8,128)S(1)} collective-permute-done((f32[1,5,8,128]{3,2,1,0:T(8,128)S(1)}, f32[1,5,8,128]{3,2,1,0:T(8,128)S(1)}, u32[]{:S(2)}, u32[]{:S(2)}) %collective-permute-start.8) | collective-permute-done | bytes 20512 | tf_op jit(solution)/shard_map/ppermute | solution.py:255
  204.9 1.1 slice.457
  206.8 1.1 slice.456
  208.7 1.1 slice.455
  210.6 1.1 slice.454
  212.6 2.0 constant_dynamic-update-slice_fusion.72
  214.9 1.6 copy-done.7
  217.3 4.0 %collective-permute-start.13 = (f32[2,5,8,128]{3,2,1,0:T(8,128)S(1)}, f32[2,5,8,128]{3,2,1,0:T(8,128)S(1)}, u32[]{:S(2)}, u32[]{:S(2)}) collective-permute-start(f32[2,5,8,128]{3,2,1,0:T(8,128)S(1)} %pad_maximum_fusion.7), channel_id=1, source_target_pairs={{0,16},{8,24},{16,32},{24,40},{32,48},{40,56},{48,64},{56,72},{64,... | collective-permute-start | bytes 122888 | tf_op jit(solution)/shard_map/ppermute | solution.py:255
  221.3 0.9 constant_dynamic-update-slice_fusion.75
  222.3 2.0 copy.85
  224.3 2.0 copy.86
  227.0 3.2 %maximum_bitcast_fusion.1 = f32[8,2,8,20,132]{4,2,1,3,0:T(8,128)S(1)} fusion(f32[8,16,20,2]{3,1,2,0:T(8,128)} %copy.86, f32[8,16,20,128]{3,1,2,0:T(8,128)} %copy-done.5, f32[8,16,20,2]{3,1,2,0:T(8,128)} %copy.85), kind=kLoop, calls=%fused_computation.2 | loop fusion | flops 675840 | bytes 2703360 | tf_op jit(solution)/shard_map/reshape | solution.py:206
  230.2 0.9 collective-permute-done.14
  231.8 4.5 %collective-permute-start.15 = (f32[8,5,8,128]{3,2,1,0:T(8,128)}, f32[8,5,8,128]{3,2,1,0:T(8,128)S(1)}, u32[]{:S(2)}, u32[]{:S(2)}) collective-permute-start(f32[8,5,8,128]{3,2,1,0:T(8,128)} %pad_maximum_fusion.2), channel_id=1, source_target_pairs={{0,64},{8,72},{16,80},{24,88},{32,96},{40,104},{48,112},{56,120},{... | collective-permute-start | bytes 491528 | tf_op jit(solution)/shard_map/ppermute | solution.py:255
  236.3 8.0 %fusion.2 = f32[8,2,8,16,128]{4,2,1,3,0:T(8,128)} fusion(f32[8,2,8,20,132]{4,2,1,3,0:T(8,128)S(1)} %maximum_bitcast_fusion.1, f32[8,8,16,128]{3,1,2,0:T(8,128)} %get-tuple-element.185, f32[8,8,16,128]{3,1,2,0:T(8,128)} %get-tuple-element.184, f32[8,8,16,128]{3,1,2,0:T(8,128)} %get-tuple-element.182, f32[8,8,16,128]{3,1,2,0:T(8,128)} %get-tuple-element.183, ...), kind=kLoop, calls=%fused_computation.8 | loop fusion | flops 14155776 | bytes 32505856 | tf_op jit(solution)/shard_map/add | solution.py:58
  244.3 2.5 copy.88
  246.8 1.7 collective-permute-start.16
  248.6 17.9 %collective-permute-done.16 = f32[16,5,8,128]{3,2,1,0:T(8,128)S(1)} collective-permute-done((f32[16,5,8,128]{3,2,1,0:T(8,128)S(1)}, f32[16,5,8,128]{3,2,1,0:T(8,128)S(1)}, u32[]{:S(2)}, u32[]{:S(2)}) %collective-permute-start.16) | collective-permute-done | bytes 327712 | tf_op jit(solution)/shard_map/ppermute | solution.py:255
  266.6 1.0 fusion.60.packed_ref
  267.5 2.2 shard_map.86
  269.8 1.4 multiply_subtract_fusion
  271.2 1.3 copy.87
  (143 shorter events, 27.8 us)
Async XLA Ops:
  0.6 14.2 %copy-start.3 = (f32[8,128,128]{2,1,0:T(8,128)S(1)}, f32[8,128,128]{2,1,0:T(8,128)}, u32[]{:S(2)}) copy-start(f32[8,128,128]{2,1,0:T(8,128)} %param.11) | copy-start | bytes 1572868
  1.7 21.1 %collective-permute-start = (f32[4,8,2,128]{3,1,2,0:T(8,128)S(1)}, f32[4,8,2,128]{3,1,2,0:T(8,128)S(1)}, u32[]{:S(2)}, u32[]{:S(2)}) collective-permute-start(f32[4,8,2,128]{3,1,2,0:T(8,128)S(1)} %copy.90), channel_id=1, source_target_pairs={{0,8},{8,16},{16,24},{24,32},{32,40},{40,48},{48,56},{56,64},{64,7... | collective-permute-start | bytes 98312 | tf_op jit(solution)/shard_map/ppermute | solution.py:19
  5.2 19.5 %collective-permute-start.1 = (f32[4,8,2,128]{3,1,2,0:T(8,128)S(1)}, f32[4,8,2,128]{3,1,2,0:T(8,128)S(1)}, u32[]{:S(2)}, u32[]{:S(2)}) collective-permute-start(f32[4,8,2,128]{3,1,2,0:T(8,128)S(1)} %copy.91), channel_id=1, source_target_pairs={{8,0},{16,8},{24,16},{32,24},{40,32},{48,40},{56,48},{64,56},{72,6... | collective-permute-start | bytes 98312 | tf_op jit(solution)/shard_map/ppermute | solution.py:22
  15.4 3.9 %copy-start.12 = (f32[8,1]{0,1:T(1,128)S(1)}, f32[8,1]{0,1:T(1,128)}, u32[]{:S(2)}) copy-start(f32[8,1]{0,1:T(1,128)} %param.13) | copy-start | bytes 100
  15.4 3.9 %copy-start.13 = (f32[8,1]{0,1:T(1,128)S(1)}, f32[8,1]{0,1:T(1,128)}, u32[]{:S(2)}) copy-start(f32[8,1]{0,1:T(1,128)} %param.12) | copy-start | bytes 100
  15.4 4.1 %copy-start.10 = (s32[256,1]{0,1:T(1,128)S(1)}, s32[256,1]{0,1:T(1,128)}, u32[]{:S(2)}) copy-start(s32[256,1]{0,1:T(1,128)} %param.10) | copy-start | bytes 3076
  27.7 36.5 %collective-permute-start.2 = (f32[4,8,132,2]{2,1,3,0:T(8,128)S(1)}, f32[4,8,132,2]{2,1,3,0:T(8,128)S(1)}, u32[]{:S(2)}, u32[]{:S(2)}) collective-permute-start(f32[4,8,132,2]{2,1,3,0:T(8,128)S(1)} %get-tuple-element.52), channel_id=1, source_target_pairs={{0,1},{1,2},{2,3},{3,4},{4,5},{5,6},{6,7},{8,9},{9,10},{10,11},{11... | collective-permute-start | bytes 101384 | tf_op jit(solution)/shard_map/ppermute | solution.py:19
  29.6 34.5 %collective-permute-start.3 = (f32[4,8,132,2]{2,1,3,0:T(8,128)S(1)}, f32[4,8,132,2]{2,1,3,0:T(8,128)S(1)}, u32[]{:S(2)}, u32[]{:S(2)}) collective-permute-start(f32[4,8,132,2]{2,1,3,0:T(8,128)S(1)} %get-tuple-element.53), channel_id=1, source_target_pairs={{1,0},{2,1},{3,2},{4,3},{5,4},{6,5},{7,6},{9,8},{10,9},{11,10},{12... | collective-permute-start | bytes 101384 | tf_op jit(solution)/shard_map/ppermute | solution.py:22
  89.7 4.5 %copy-start.11 = (f32[16,84,128]{2,0,1:T(8,128)}, f32[16,84,128]{2,0,1:T(8,128)S(1)}, u32[]{:S(2)}) copy-start(f32[16,84,128]{2,0,1:T(8,128)S(1)} %get-tuple-element.78) | copy-start | bytes 2064388
  90.6 30.9 %collective-permute-start.4 = (f32[16,84,128]{2,0,1:T(8,128)}, f32[16,84,128]{2,0,1:T(8,128)S(1)}, u32[]{:S(2)}, u32[]{:S(2)}) collective-permute-start(f32[16,84,128]{2,0,1:T(8,128)} %constant_dynamic-update-slice_fusion), channel_id=1, source_target_pairs={{0,16},{8,24},{16,32},{24,40},{32,48},{40,56},{48,64},{56,72},{64,... | collective-permute-start | bytes 2064392 | tf_op jit(solution)/shard_map/ppermute | solution.py:30
  109.8 21.8 %collective-permute-start.5 = (f32[16,84,128]{2,0,1:T(8,128)}, f32[16,84,128]{2,0,1:T(8,128)S(1)}, u32[]{:S(2)}, u32[]{:S(2)}) collective-permute-start(f32[16,84,128]{2,0,1:T(8,128)} %constant_dynamic-update-slice_fusion.5), channel_id=1, source_target_pairs={{0,8},{8,16},{16,24},{24,32},{32,40},{40,48},{48,56},{56,64},{64,7... | collective-permute-start | bytes 2064392 | tf_op jit(solution)/shard_map/ppermute | solution.py:30
  112.6 36.6 %collective-permute-start.6 = (f32[16,84,128]{2,0,1:T(8,128)S(1)}, f32[16,84,128]{2,0,1:T(8,128)S(1)}, u32[]{:S(2)}, u32[]{:S(2)}) collective-permute-start(f32[16,84,128]{2,0,1:T(8,128)S(1)} %constant_dynamic-update-slice_fusion.10), channel_id=1, source_target_pairs={{8,0},{16,8},{24,16},{32,24},{40,32},{48,40},{56,48},{64,56},{72,6... | collective-permute-start | bytes 2064392 | tf_op jit(solution)/shard_map/ppermute | solution.py:30
  118.1 42.7 %collective-permute-start.7 = (f32[16,84,128]{2,0,1:T(8,128)S(1)}, f32[16,84,128]{2,0,1:T(8,128)S(1)}, u32[]{:S(2)}, u32[]{:S(2)}) collective-permute-start(f32[16,84,128]{2,0,1:T(8,128)S(1)} %constant_dynamic-update-slice_fusion.15), channel_id=1, source_target_pairs={{16,0},{24,8},{32,16},{40,24},{48,32},{56,40},{64,48},{72,56},{80,... | collective-permute-start | bytes 2064392 | tf_op jit(solution)/shard_map/ppermute | solution.py:30
  138.7 66.2 %collective-permute-start.12 = (f32[16,84,128]{2,0,1:T(8,128)}, f32[16,84,128]{2,0,1:T(8,128)}, u32[]{:S(2)}, u32[]{:S(2)}) collective-permute-start(f32[16,84,128]{2,0,1:T(8,128)} %constant_dynamic-update-slice_fusion.52), channel_id=1, source_target_pairs={{16,0},{24,8},{32,16},{40,24},{48,32},{56,40},{64,48},{72,56},{80,... | collective-permute-start | bytes 2064392 | tf_op jit(solution)/shard_map/ppermute | solution.py:30
  141.9 64.9 %collective-permute-start.11 = (f32[16,84,128]{2,0,1:T(8,128)}, f32[16,84,128]{2,0,1:T(8,128)}, u32[]{:S(2)}, u32[]{:S(2)}) collective-permute-start(f32[16,84,128]{2,0,1:T(8,128)} %constant_dynamic-update-slice_fusion.47), channel_id=1, source_target_pairs={{8,0},{16,8},{24,16},{32,24},{40,32},{48,40},{56,48},{64,56},{72,6... | collective-permute-start | bytes 2064392 | tf_op jit(solution)/shard_map/ppermute | solution.py:30
  144.8 63.9 %collective-permute-start.10 = (f32[16,84,128]{2,0,1:T(8,128)}, f32[16,84,128]{2,0,1:T(8,128)}, u32[]{:S(2)}, u32[]{:S(2)}) collective-permute-start(f32[16,84,128]{2,0,1:T(8,128)} %constant_dynamic-update-slice_fusion.42), channel_id=1, source_target_pairs={{0,8},{8,16},{16,24},{24,32},{32,40},{40,48},{48,56},{56,64},{64,7... | collective-permute-start | bytes 2064392 | tf_op jit(solution)/shard_map/ppermute | solution.py:30
  149.2 61.5 %collective-permute-start.9 = (f32[16,84,128]{2,0,1:T(8,128)}, f32[16,84,128]{2,0,1:T(8,128)}, u32[]{:S(2)}, u32[]{:S(2)}) collective-permute-start(f32[16,84,128]{2,0,1:T(8,128)} %constant_dynamic-update-slice_fusion.37), channel_id=1, source_target_pairs={{0,16},{8,24},{16,32},{24,40},{32,48},{40,56},{48,64},{56,72},{64,... | collective-permute-start | bytes 2064392 | tf_op jit(solution)/shard_map/ppermute | solution.py:30
  160.8 1.8 copy-start.6
  169.9 2.1 copy-start.4
  174.0 3.2 %copy-start.2 = (f32[8,8,16,128]{3,1,2,0:T(8,128)S(1)}, f32[8,8,16,128]{3,1,2,0:T(8,128)}, u32[]{:S(2)}) copy-start(f32[8,8,16,128]{3,1,2,0:T(8,128)} %get-tuple-element.99) | copy-start | bytes 1572868
  188.0 1.0 copy-start
  189.6 15.4 %collective-permute-start.8 = (f32[1,5,8,128]{3,2,1,0:T(8,128)S(1)}, f32[1,5,8,128]{3,2,1,0:T(8,128)S(1)}, u32[]{:S(2)}, u32[]{:S(2)}) collective-permute-start(f32[1,5,8,128]{3,2,1,0:T(8,128)S(1)} %maximum_bitcast_fusion.3), channel_id=1, source_target_pairs={{0,8},{8,16},{16,24},{24,32},{32,40},{40,48},{48,56},{56,64},{64,7... | collective-permute-start | bytes 61448 | tf_op jit(solution)/shard_map/ppermute | solution.py:255
  214.7 1.8 copy-start.7
  217.3 9.0 %collective-permute-start.13 = (f32[2,5,8,128]{3,2,1,0:T(8,128)S(1)}, f32[2,5,8,128]{3,2,1,0:T(8,128)S(1)}, u32[]{:S(2)}, u32[]{:S(2)}) collective-permute-start(f32[2,5,8,128]{3,2,1,0:T(8,128)S(1)} %pad_maximum_fusion.7), channel_id=1, source_target_pairs={{0,16},{8,24},{16,32},{24,40},{32,48},{40,56},{48,64},{56,72},{64,... | collective-permute-start | bytes 122888 | tf_op jit(solution)/shard_map/ppermute | solution.py:255
  222.3 4.1 %copy-start.5 = (f32[8,16,20,128]{3,1,2,0:T(8,128)}, f32[8,16,20,128]{3,1,2,0:T(8,128)S(1)}, u32[]{:S(2)}) copy-start(f32[8,16,20,128]{3,1,2,0:T(8,128)S(1)} %constant_dynamic-update-slice_fusion.75) | copy-start | bytes 3932164
  226.3 4.8 %collective-permute-start.14 = (f32[4,5,8,128]{3,2,1,0:T(8,128)S(1)}, f32[4,5,8,128]{3,2,1,0:T(8,128)S(1)}, u32[]{:S(2)}, u32[]{:S(2)}) collective-permute-start(f32[4,5,8,128]{3,2,1,0:T(8,128)S(1)} %pad_maximum_fusion.3), channel_id=1, source_target_pairs={{0,32},{8,40},{16,48},{24,56},{32,64},{40,72},{48,80},{56,88},{64,... | collective-permute-start | bytes 245768 | tf_op jit(solution)/shard_map/ppermute | solution.py:255
  231.8 15.0 %collective-permute-start.15 = (f32[8,5,8,128]{3,2,1,0:T(8,128)}, f32[8,5,8,128]{3,2,1,0:T(8,128)S(1)}, u32[]{:S(2)}, u32[]{:S(2)}) collective-permute-start(f32[8,5,8,128]{3,2,1,0:T(8,128)} %pad_maximum_fusion.2), channel_id=1, source_target_pairs={{0,64},{8,72},{16,80},{24,88},{32,96},{40,104},{48,112},{56,120},{... | collective-permute-start | bytes 491528 | tf_op jit(solution)/shard_map/ppermute | solution.py:255
  246.8 19.7 %collective-permute-start.16 = (f32[16,5,8,128]{3,2,1,0:T(8,128)S(1)}, f32[16,5,8,128]{3,2,1,0:T(8,128)S(1)}, u32[]{:S(2)}, u32[]{:S(2)}) collective-permute-start(f32[16,5,8,128]{3,2,1,0:T(8,128)S(1)} %pad_maximum_fusion.1), channel_id=1, source_target_pairs={{0,128},{8,136},{16,144},{24,152},{32,160},{40,168},{48,176},{56,1... | collective-permute-start | bytes 983048 | tf_op jit(solution)/shard_map/ppermute | solution.py:255
  248.5 21.2 %copy-start.1 = (f32[8,2,128,128]{2,3,1,0:T(8,128)S(1)}, f32[8,2,128,128]{2,3,1,0:T(8,128)}, u32[]{:S(2)}) copy-start(f32[8,2,128,128]{2,3,1,0:T(8,128)} %copy-done) | copy-start | bytes 3145732
  248.5 21.2 %copy-start.8 = (f32[8,128]{0,1:T(8,128)S(1)}, f32[8,128]{0,1:T(8,128)}, u32[]{:S(2)}) copy-start(f32[8,128]{0,1:T(8,128)} %copy.82) | copy-start | bytes 12292
  248.5 21.2 %copy-start.9 = (f32[8,128]{0,1:T(8,128)S(1)}, f32[8,128]{0,1:T(8,128)}, u32[]{:S(2)}) copy-start(f32[8,128]{0,1:T(8,128)} %copy.84) | copy-start | bytes 12292

commit v3 on v0

--- a/solution.py
+++ b/solution.py
@@ -110,6 +110,37 @@
     )(jnp.reshape(position, (1,)).astype(jnp.int32), packed_all)
 
 
+def halos_at_once(block, width):
+    count_x = lax.axis_size("gx")
+    count_y = lax.axis_size("gy")
+    columns, rows = block.shape[1], block.shape[2]
+
+    def moved(piece, step_x, step_y):
+        pairs = []
+        for sx in range(count_x):
+            for sy in range(count_y):
+                tx, ty = sx + step_x, sy + step_y
+                if 0 <= tx < count_x and 0 <= ty < count_y:
+                    pairs.append((sx * count_y + sy, tx * count_y + ty))
+        return lax.ppermute(piece, ("gx", "gy"), pairs)
+
+    low_x = block[:, columns - width :]
+    high_x = block[:, 0:width]
+    left = moved(low_x, 1, 0)
+    right = moved(high_x, -1, 0)
+    below = moved(block[:, :, rows - width :], 0, 1)
+    above = moved(block[:, :, 0:width], 0, -1)
+    corner_ll = moved(low_x[:, :, rows - width :], 1, 1)
+    corner_lh = moved(low_x[:, :, 0:width], 1, -1)
+    corner_hl = moved(high_x[:, :, rows - width :], -1, 1)
+    corner_hh = moved(high_x[:, :, 0:width], -1, -1)
+    main = jnp.concatenate([left, block, right], axis=1)
+    low_rows = jnp.concatenate([corner_ll, below, corner_hl], axis=1)
+    high_rows = jnp.concatenate([corner_lh, above, corner_hh], axis=1)
+    halo = jnp.concatenate([low_rows, high_rows], axis=2).transpose(0, 2, 1)
+    return main, halo
+
+
 def halo_x(block, axis, width):
     count = lax.axis_size(axis)
     forward = [(i, i + 1) for i in range(count - 1)]
@@ -220,8 +251,7 @@
     count = lax.axis_size("gx")
     position = lax.axis_index("gx")
     flat = fields.reshape(channels, columns, rows_here)
-    main = halo_x(flat, "gx", 2)
-    halo = halo_y(main, "gy", 2).transpose(0, 2, 1)
+    main, halo = halos_at_once(flat, 2)
     offsets = block_offset[:, 0]
     wind_main, wind_halo = main[:wind_channels], halo[:wind_channels]
     tracer_main, tracer_halo = main[wind_channels:], halo[wind_channels:]

time: 257 us -> 290 us (1.13)
  local copies, waits for them, and re-layouts: 58 us -> 75.2 us
  starting transfers between devices: 51.4 us -> 68.5 us
    ppermute x4 -> x8, starting transfers between devices: 13.5 us -> 29.7 us  [moved(): return lax.ppermute(piece, ('gx', 'gy'), pairs)]
    transpose x1 -> x3, other arithmetic: 0.01 us -> 16 us  [the longest x2 15.9 us: advect_group(): interpolated.transpose(1, 2, 0, 3, 4)]
    add x2 -> x0, other arithmetic: 16 us -> none  [interpolate(): running_total + tap_term]
    mul x0 -> x10, local copies, waits for them, and re-layouts: none -> 14.7 us  [lagrange(): factor = factor * ((position - anchor) / (target - anchor))]
    ppermute x5, waiting for transfers between devices: 31.9 us -> 22.4 us  [local(): held = jnp.concatenate([held, lax.ppermute(held, 'gx', ring)], axis=0)]
    ppermute x8, waiting for transfers between devices: 20.3 us -> 26.9 us  [shifted_2(): lax.ppermute(value, axis, [(source, source + steps) for source in range(l...]
    another operation x8, other arithmetic: 1.45 us -> 5.68 us
    transpose x0 -> x2, local copies, waits for them, and re-layouts: none -> 4.15 us  [advect_group(): interpolated.transpose(1, 2, 0, 3, 4)]
  transfers between devices with their start and end apart: 17 -> 21, of which waited for: 6 -> 5; matrix products, arithmetic and copies ran while one was open for 30% -> 34% of each run, Pallas kernels for 0% -> 0%
where the time goes in v3:
time: 290 us; the launch traced here: 287 us
  local copies, waits for them, and re-layouts  75.2 us (26%)
  starting transfers between devices  68.5 us (24%)
  waiting for transfers between devices  50.8 us (18%)
  between operations  46.1 us (16%)
  other arithmetic  43.1 us (15%)
    ppermute x8, starting transfers between devices, moved(): return lax.ppermute(piece, ('gx', 'gy'), pairs)  29.7 us
    unnamed x113, local copies, waits for them, and re-layouts  28.2 us
    ppermute x8, waiting for transfers between devices, shifted_2(): lax.ppermute(value, axis, [(source, source + steps) for source in range(l...  26.9 us
    ppermute x8, starting transfers between devices, shifted_2(): lax.ppermute(value, axis, [(source, source + steps) for source in range(l...  26 us
    ppermute x5, waiting for transfers between devices, local(): held = jnp.concatenate([held, lax.ppermute(held, 'gx', ring)], axis=0)  22.4 us
    transpose x2, other arithmetic, advect_group(): interpolated.transpose(1, 2, 0, 3, 4)  15.9 us
    mul x10, local copies, waits for them, and re-layouts, lagrange(): factor = factor * ((position - anchor) / (target - anchor))  14.7 us
    ppermute x5, starting transfers between devices, local(): held = jnp.concatenate([held, lax.ppermute(held, 'gx', ring)], axis=0)  12.8 us
  transfers between devices with their start and end apart: 21, of which 5 were waited for; matrix products, arithmetic and copies ran while one was open for 34% of the time, Pallas kernels for 0%

profile of v3, /device:TPU:34, one launch (start us, length us, event | category | flops | bytes accessed | tf_op | source)
XLA Modules:
  0.0 286.9 jit_solution(9251610331713949611)
XLA Ops:
  0.6 2.4 copy.83
  3.7 2.9 %collective-permute-start.2 = (f32[32,2,2]{1,0,2:T(8,128)}, f32[32,2,2]{1,0,2:T(8,128)S(1)}, u32[]{:S(2)}, u32[]{:S(2)}) collective-permute-start(f32[32,2,2]{1,0,2:T(8,128)} %get-tuple-element.52), channel_id=1, source_target_pairs={{0,9},{1,10},{2,11},{3,12},{4,13},{5,14},{6,15},{8,17},{9,18},{10,... | collective-permute-start | bytes 1544 | tf_op jit(solution)/shard_map/ppermute | solution.py:125
  6.6 5.7 %collective-permute-start.4 = (f32[32,2,2]{1,0,2:T(8,128)S(1)}, f32[32,2,2]{1,0,2:T(8,128)S(1)}, u32[]{:S(2)}, u32[]{:S(2)}) collective-permute-start(f32[32,2,2]{1,0,2:T(8,128)S(1)} %get-tuple-element.54), channel_id=1, source_target_pairs={{8,1},{9,2},{10,3},{11,4},{12,5},{13,6},{14,7},{16,9},{17,10},{18,... | collective-permute-start | bytes 1544 | tf_op jit(solution)/shard_map/ppermute | solution.py:125
  12.3 1.9 collective-permute-start.5
  14.2 5.7 %collective-permute-start.7 = (f32[32,2,2]{1,0,2:T(8,128)S(1)}, f32[32,2,2]{1,0,2:T(8,128)S(1)}, u32[]{:S(2)}, u32[]{:S(2)}) collective-permute-start(f32[32,2,2]{1,0,2:T(8,128)S(1)} %get-tuple-element.55), channel_id=1, source_target_pairs={{9,0},{10,1},{11,2},{12,3},{13,4},{14,5},{15,6},{17,8},{18,9},{19,... | collective-permute-start | bytes 1544 | tf_op jit(solution)/shard_map/ppermute | solution.py:125
  20.0 2.7 fusion.101
  22.7 2.7 copy.84
  25.4 1.9 collective-permute-start
  33.3 2.0 multiply_multiply_fusion.9
  35.4 2.1 multiply_multiply_fusion.8
  39.7 1.5 fusion.84
  41.2 1.4 fusion.92
  62.6 1.3 copy.85
  74.0 1.9 collective-permute-start.3
  75.9 3.6 %collective-permute-start.6 = (f32[32,128,2]{1,0,2:T(8,128)S(1)}, f32[32,128,2]{1,0,2:T(8,128)S(1)}, u32[]{:S(2)}, u32[]{:S(2)}) collective-permute-start(f32[32,128,2]{1,0,2:T(8,128)S(1)} %get-tuple-element.57), channel_id=1, source_target_pairs={{1,0},{2,1},{3,2},{4,3},{5,4},{6,5},{7,6},{9,8},{10,9},{11,10},{12... | collective-permute-start | bytes 98312 | tf_op jit(solution)/shard_map/ppermute | solution.py:125
  79.6 2.8 copy_dynamic-update-slice_fusion
  82.4 6.0 %collective-permute-start.1 = (f32[32,2,128]{2,0,1:T(8,128)S(1)}, f32[32,2,128]{2,0,1:T(8,128)S(1)}, u32[]{:S(2)}, u32[]{:S(2)}) collective-permute-start(f32[32,2,128]{2,0,1:T(8,128)S(1)} %copy.85), channel_id=1, source_target_pairs={{8,0},{9,1},{10,2},{11,3},{12,4},{13,5},{14,6},{15,7},{16,8},{17,9... | collective-permute-start | bytes 98312 | tf_op jit(solution)/shard_map/ppermute | solution.py:125
  88.6 1.4 collective-permute-done.1
  94.3 4.3 %collective-permute-start.8 = (f32[16,84,128]{2,0,1:T(8,128)}, f32[16,84,128]{2,0,1:T(8,128)}, u32[]{:S(2)}, u32[]{:S(2)}) collective-permute-start(f32[16,84,128]{2,0,1:T(8,128)} %constant_dynamic-update-slice_fusion.2), channel_id=1, source_target_pairs={{0,16},{8,24},{16,32},{24,40},{32,48},{40,56},{48,64},{56,72},{64,... | collective-permute-start | bytes 2064392 | tf_op jit(solution)/shard_map/ppermute | solution.py:30
  109.1 1.4 copy.81
  110.5 2.2 copy.82
  112.7 2.2 copy.88
  114.9 2.2 copy.89
  117.1 1.1 copy.90
  118.2 1.1 copy.91
  119.3 1.1 copy.92
  120.4 1.1 copy.93
  121.6 1.1 copy.94
  122.7 1.1 copy.95
  129.4 5.4 %collective-permute-start.9 = (f32[16,84,128]{2,0,1:T(8,128)}, f32[16,84,128]{2,0,1:T(8,128)S(1)}, u32[]{:S(2)}, u32[]{:S(2)}) collective-permute-start(f32[16,84,128]{2,0,1:T(8,128)} %constant_dynamic-update-slice_fusion.7), channel_id=1, source_target_pairs={{0,8},{8,16},{16,24},{24,32},{32,40},{40,48},{48,56},{56,64},{64,7... | collective-permute-start | bytes 2064392 | tf_op jit(solution)/shard_map/ppermute | solution.py:30
  135.6 2.5 collective-permute-start.10
  138.8 3.6 %collective-permute-start.11 = (f32[16,84,128]{2,0,1:T(8,128)}, f32[16,84,128]{2,0,1:T(8,128)S(1)}, u32[]{:S(2)}, u32[]{:S(2)}) collective-permute-start(f32[16,84,128]{2,0,1:T(8,128)} %constant_dynamic-update-slice_fusion.17), channel_id=1, source_target_pairs={{16,0},{24,8},{32,16},{40,24},{48,32},{56,40},{64,48},{72,56},{80,... | collective-permute-start | bytes 2064392 | tf_op jit(solution)/shard_map/ppermute | solution.py:30
  142.7 1.1 slice_dynamic-update-slice_fusion.3
  143.8 7.2 %collective-permute-done.9 = f32[16,84,128]{2,0,1:T(8,128)S(1)} collective-permute-done((f32[16,84,128]{2,0,1:T(8,128)}, f32[16,84,128]{2,0,1:T(8,128)S(1)}, u32[]{:S(2)}, u32[]{:S(2)}) %collective-permute-start.9) | collective-permute-done | bytes 688160 | tf_op jit(solution)/shard_map/ppermute | solution.py:30
  155.4 2.1 collective-permute-start.16
  158.2 4.2 %collective-permute-start.15 = (f32[16,84,128]{2,0,1:T(8,128)}, f32[16,84,128]{2,0,1:T(8,128)}, u32[]{:S(2)}, u32[]{:S(2)}) collective-permute-start(f32[16,84,128]{2,0,1:T(8,128)} %constant_dynamic-update-slice_fusion.49), channel_id=1, source_target_pairs={{8,0},{16,8},{24,16},{32,24},{40,32},{48,40},{56,48},{64,56},{72,6... | collective-permute-start | bytes 2064392 | tf_op jit(solution)/shard_map/ppermute | solution.py:30
  163.2 1.9 collective-permute-start.14
  165.8 19.7 %collective-permute-done.10 = f32[16,84,128]{2,0,1:T(8,128)S(1)} collective-permute-done((f32[16,84,128]{2,0,1:T(8,128)}, f32[16,84,128]{2,0,1:T(8,128)S(1)}, u32[]{:S(2)}, u32[]{:S(2)}) %collective-permute-start.10) | collective-permute-done | bytes 688160 | tf_op jit(solution)/shard_map/ppermute | solution.py:30
  185.5 1.9 collective-permute-start.13
  187.6 1.7 copy-done.16
  197.3 1.1 copy-done.13
  200.8 1.1 maximum_bitcast_fusion
  201.9 8.0 %fusion.33 = f32[2,8,8,16,128]{4,1,0,3,2:T(8,128)} fusion(f32[8,2,8,20,132]{4,2,1,3,0:T(8,128)S(1)} %maximum_bitcast_fusion, f32[8,8,16,128]{3,1,2,0:T(8,128)} %copy.95, f32[8,8,16,128]{3,1,2,0:T(8,128)} %copy.94, f32[8,8,16,128]{3,1,2,0:T(8,128)} %copy.93, f32[8,8,16,128]{3,1,2,0:T(8,128)} %copy.92, f32[8,8,16,128]{3,1,2,0:T(8,128)} %copy.91, ...), kind=kLoop, calls=%fused_computation.64 | loop fusion | flops 14155776 | bytes 32505856 | tf_op jit(solution)/shard_map/transpose | solution.py:241
  209.8 1.6 copy.96
  211.5 1.1 fusion.61
  215.7 5.3 %collective-permute-done.12 = f32[1,5,8,128]{3,2,1,0:T(8,128)S(1)} collective-permute-done((f32[1,5,8,128]{3,2,1,0:T(8,128)S(1)}, f32[1,5,8,128]{3,2,1,0:T(8,128)S(1)}, u32[]{:S(2)}, u32[]{:S(2)}) %collective-permute-start.12) | collective-permute-done | bytes 20512 | tf_op jit(solution)/shard_map/ppermute | solution.py:281
  221.0 1.1 slice.472
  222.9 1.1 slice.471
  224.8 1.1 slice.470
  226.9 1.1 slice.469
  229.3 1.6 copy-done.17
  231.7 2.4 collective-permute-start.17
  235.0 2.0 copy.102
  237.0 2.0 copy.103
  239.1 6.6 %collective-permute-start.18 = (f32[4,5,8,128]{3,2,1,0:T(8,128)S(1)}, f32[4,5,8,128]{3,2,1,0:T(8,128)S(1)}, u32[]{:S(2)}, u32[]{:S(2)}) collective-permute-start(f32[4,5,8,128]{3,2,1,0:T(8,128)S(1)} %pad_maximum_fusion.2), channel_id=1, source_target_pairs={{0,32},{8,40},{16,48},{24,56},{32,64},{40,72},{48,80},{56,88},{64,... | collective-permute-start | bytes 245768 | tf_op jit(solution)/shard_map/ppermute | solution.py:281
  245.7 3.2 %maximum_bitcast_fusion.1 = f32[8,2,8,20,132]{4,2,1,3,0:T(8,128)S(1)} fusion(f32[8,16,20,2]{3,1,2,0:T(8,128)} %copy.103, f32[8,16,20,128]{3,1,2,0:T(8,128)} %copy-done.15, f32[8,16,20,2]{3,1,2,0:T(8,128)} %copy.102), kind=kLoop, calls=%fused_computation.1 | loop fusion | flops 675840 | bytes 2703360 | tf_op jit(solution)/shard_map/reshape | solution.py:237
  249.6 3.5 %collective-permute-start.19 = (f32[8,5,8,128]{3,2,1,0:T(8,128)}, f32[8,5,8,128]{3,2,1,0:T(8,128)S(1)}, u32[]{:S(2)}, u32[]{:S(2)}) collective-permute-start(f32[8,5,8,128]{3,2,1,0:T(8,128)} %pad_maximum_fusion.1), channel_id=1, source_target_pairs={{0,64},{8,72},{16,80},{24,88},{32,96},{40,104},{48,112},{56,120},{... | collective-permute-start | bytes 491528 | tf_op jit(solution)/shard_map/ppermute | solution.py:281
  253.1 7.9 %fusion.3 = f32[2,8,8,16,128]{4,1,0,3,2:T(8,128)} fusion(f32[8,2,8,20,132]{4,2,1,3,0:T(8,128)S(1)} %maximum_bitcast_fusion.1, f32[8,8,16,128]{3,1,2,0:T(8,128)} %copy.95, f32[8,8,16,128]{3,1,2,0:T(8,128)} %copy.94, f32[8,8,16,128]{3,1,2,0:T(8,128)} %copy.93, f32[8,8,16,128]{3,1,2,0:T(8,128)} %copy.92, f32[8,8,16,128]{3,1,2,0:T(8,128)} %copy.91, ...), kind=kLoop, calls=%fused_computation.9 | loop fusion | flops 14155776 | bytes 32505856 | tf_op jit(solution)/shard_map/transpose | solution.py:241
  261.0 2.5 copy.104
  263.9 17.1 %collective-permute-done.20 = f32[16,5,8,128]{3,2,1,0:T(8,128)S(1)} collective-permute-done((f32[16,5,8,128]{3,2,1,0:T(8,128)S(1)}, f32[16,5,8,128]{3,2,1,0:T(8,128)S(1)}, u32[]{:S(2)}, u32[]{:S(2)}) %collective-permute-start.20) | collective-permute-done | bytes 327712 | tf_op jit(solution)/shard_map/ppermute | solution.py:281
  281.0 1.0 fusion.60.packed_ref
  282.0 2.2 shard_map.86
  284.2 1.4 multiply_subtract_fusion
  285.6 1.3 copy.105
  (191 shorter events, 42.9 us)
Async XLA Ops:
  3.7 72.2 %collective-permute-start.2 = (f32[32,2,2]{1,0,2:T(8,128)}, f32[32,2,2]{1,0,2:T(8,128)S(1)}, u32[]{:S(2)}, u32[]{:S(2)}) collective-permute-start(f32[32,2,2]{1,0,2:T(8,128)} %get-tuple-element.52), channel_id=1, source_target_pairs={{0,9},{1,10},{2,11},{3,12},{4,13},{5,14},{6,15},{8,17},{9,18},{10,... | collective-permute-start | bytes 1544 | tf_op jit(solution)/shard_map/ppermute | solution.py:125
  6.6 75.8 %collective-permute-start.4 = (f32[32,2,2]{1,0,2:T(8,128)S(1)}, f32[32,2,2]{1,0,2:T(8,128)S(1)}, u32[]{:S(2)}, u32[]{:S(2)}) collective-permute-start(f32[32,2,2]{1,0,2:T(8,128)S(1)} %get-tuple-element.54), channel_id=1, source_target_pairs={{8,1},{9,2},{10,3},{11,4},{12,5},{13,6},{14,7},{16,9},{17,10},{18,... | collective-permute-start | bytes 1544 | tf_op jit(solution)/shard_map/ppermute | solution.py:125
  12.3 76.1 %collective-permute-start.5 = (f32[32,2,2]{1,0,2:T(8,128)S(1)}, f32[32,2,2]{1,0,2:T(8,128)S(1)}, u32[]{:S(2)}, u32[]{:S(2)}) collective-permute-start(f32[32,2,2]{1,0,2:T(8,128)S(1)} %get-tuple-element.53), channel_id=1, source_target_pairs={{1,8},{2,9},{3,10},{4,11},{5,12},{6,13},{7,14},{9,16},{10,17},{11,... | collective-permute-start | bytes 1544 | tf_op jit(solution)/shard_map/ppermute | solution.py:125
  14.2 74.2 %collective-permute-start.7 = (f32[32,2,2]{1,0,2:T(8,128)S(1)}, f32[32,2,2]{1,0,2:T(8,128)S(1)}, u32[]{:S(2)}, u32[]{:S(2)}) collective-permute-start(f32[32,2,2]{1,0,2:T(8,128)S(1)} %get-tuple-element.55), channel_id=1, source_target_pairs={{9,0},{10,1},{11,2},{12,3},{13,4},{14,5},{15,6},{17,8},{18,9},{19,... | collective-permute-start | bytes 1544 | tf_op jit(solution)/shard_map/ppermute | solution.py:125
  22.7 4.7 %copy-start.22 = (s32[256,1]{0,1:T(1,128)S(1)}, s32[256,1]{0,1:T(1,128)}, u32[]{:S(2)}) copy-start(s32[256,1]{0,1:T(1,128)} %param.10) | copy-start | bytes 3076
  22.7 10.6 %copy-start.18 = (f32[8,128,128]{2,1,0:T(8,128)S(1)}, f32[8,128,128]{2,1,0:T(8,128)}, u32[]{:S(2)}) copy-start(f32[8,128,128]{2,1,0:T(8,128)} %param.8) | copy-start | bytes 1572868
  25.4 48.6 %collective-permute-start = (f32[32,2,128]{2,0,1:T(8,128)S(1)}, f32[32,2,128]{2,0,1:T(8,128)S(1)}, u32[]{:S(2)}, u32[]{:S(2)}) collective-permute-start(f32[32,2,128]{2,0,1:T(8,128)S(1)} %copy.84), channel_id=1, source_target_pairs={{0,8},{1,9},{2,10},{3,11},{4,12},{5,13},{6,14},{7,15},{8,16},{9,17... | collective-permute-start | bytes 98312 | tf_op jit(solution)/shard_map/ppermute | solution.py:125
  33.3 2.1 copy-start.19
  35.3 2.1 copy-start.5
  37.4 0.7 copy-start.28
  37.4 0.7 copy-start.29
  37.5 25.2 %copy-start.4 = (f32[32,2,128]{1,0,2:T(8,128)S(1)}, f32[32,2,128]{1,0,2:T(8,128)}, u32[]{:S(2)}) copy-start(f32[32,2,128]{1,0,2:T(8,128)} %get-tuple-element.58) | copy-start | bytes 98308
  74.0 14.5 %collective-permute-start.3 = (f32[32,128,2]{1,0,2:T(8,128)S(1)}, f32[32,128,2]{1,0,2:T(8,128)S(1)}, u32[]{:S(2)}, u32[]{:S(2)}) collective-permute-start(f32[32,128,2]{1,0,2:T(8,128)S(1)} %get-tuple-element.56), channel_id=1, source_target_pairs={{0,1},{1,2},{2,3},{3,4},{4,5},{5,6},{6,7},{8,9},{9,10},{10,11},{11... | collective-permute-start | bytes 98312 | tf_op jit(solution)/shard_map/ppermute | solution.py:125
  75.9 12.5 %collective-permute-start.6 = (f32[32,128,2]{1,0,2:T(8,128)S(1)}, f32[32,128,2]{1,0,2:T(8,128)S(1)}, u32[]{:S(2)}, u32[]{:S(2)}) collective-permute-start(f32[32,128,2]{1,0,2:T(8,128)S(1)} %get-tuple-element.57), channel_id=1, source_target_pairs={{1,0},{2,1},{3,2},{4,3},{5,4},{6,5},{7,6},{9,8},{10,9},{11,10},{12... | collective-permute-start | bytes 98312 | tf_op jit(solution)/shard_map/ppermute | solution.py:125
  82.4 7.6 %collective-permute-start.1 = (f32[32,2,128]{2,0,1:T(8,128)S(1)}, f32[32,2,128]{2,0,1:T(8,128)S(1)}, u32[]{:S(2)}, u32[]{:S(2)}) collective-permute-start(f32[32,2,128]{2,0,1:T(8,128)S(1)} %copy.85), channel_id=1, source_target_pairs={{8,0},{9,1},{10,2},{11,3},{12,4},{13,5},{14,6},{15,7},{16,8},{17,9... | collective-permute-start | bytes 98312 | tf_op jit(solution)/shard_map/ppermute | solution.py:125
  90.0 61.1 %copy-start.2 = (f32[32,132,128]{2,0,1:T(8,128)}, f32[32,132,128]{2,0,1:T(8,128)S(1)}, u32[]{:S(2)}) copy-start(f32[32,132,128]{2,0,1:T(8,128)S(1)} %constant_dynamic-update-slice_fusion) | copy-start | bytes 6488068
  93.5 5.8 %copy-start.23 = (f32[16,84,128]{2,0,1:T(8,128)}, f32[16,84,128]{2,0,1:T(8,128)S(1)}, u32[]{:S(2)}) copy-start(f32[16,84,128]{2,0,1:T(8,128)S(1)} %get-tuple-element.78) | copy-start | bytes 2064388
  93.5 5.8 %copy-start.24 = (f32[16,84,128]{2,0,1:T(8,128)}, f32[16,84,128]{2,0,1:T(8,128)S(1)}, u32[]{:S(2)}) copy-start(f32[16,84,128]{2,0,1:T(8,128)S(1)} %get-tuple-element.79) | copy-start | bytes 2064388
  93.5 5.8 %copy-start.25 = (f32[16,84,128]{2,0,1:T(8,128)}, f32[16,84,128]{2,0,1:T(8,128)S(1)}, u32[]{:S(2)}) copy-start(f32[16,84,128]{2,0,1:T(8,128)S(1)} %get-tuple-element.80) | copy-start | bytes 2064388
  94.3 48.4 %collective-permute-start.8 = (f32[16,84,128]{2,0,1:T(8,128)}, f32[16,84,128]{2,0,1:T(8,128)}, u32[]{:S(2)}, u32[]{:S(2)}) collective-permute-start(f32[16,84,128]{2,0,1:T(8,128)} %constant_dynamic-update-slice_fusion.2), channel_id=1, source_target_pairs={{0,16},{8,24},{16,32},{24,40},{32,48},{40,56},{48,64},{56,72},{64,... | collective-permute-start | bytes 2064392 | tf_op jit(solution)/shard_map/ppermute | solution.py:30
  109.0 8.1 %copy-start.12 = (f32[8,8,16,128]{3,2,0,1:T(8,128)S(1)}, f32[8,8,16,128]{3,2,0,1:T(8,128)}, u32[]{:S(2)}) copy-start(f32[8,8,16,128]{3,2,0,1:T(8,128)} %get-tuple-element.104) | copy-start | bytes 1572868
  110.5 7.8 %copy-start.11 = (f32[8,8,16,128]{3,2,0,1:T(8,128)S(1)}, f32[8,8,16,128]{3,2,0,1:T(8,128)}, u32[]{:S(2)}) copy-start(f32[8,8,16,128]{3,2,0,1:T(8,128)} %get-tuple-element.103) | copy-start | bytes 1572868
  112.7 6.7 %copy-start.10 = (f32[8,8,16,128]{3,2,0,1:T(8,128)S(1)}, f32[8,8,16,128]{3,2,0,1:T(8,128)}, u32[]{:S(2)}) copy-start(f32[8,8,16,128]{3,2,0,1:T(8,128)} %get-tuple-element.100) | copy-start | bytes 1572868
  114.9 5.5 %copy-start.9 = (f32[8,8,16,128]{3,2,0,1:T(8,128)S(1)}, f32[8,8,16,128]{3,2,0,1:T(8,128)}, u32[]{:S(2)}) copy-start(f32[8,8,16,128]{3,2,0,1:T(8,128)} %get-tuple-element.97) | copy-start | bytes 1572868
  117.1 4.4 %copy-start.8 = (f32[8,8,16,128]{3,2,0,1:T(8,128)S(1)}, f32[8,8,16,128]{3,2,0,1:T(8,128)}, u32[]{:S(2)}) copy-start(f32[8,8,16,128]{3,2,0,1:T(8,128)} %get-tuple-element.99) | copy-start | bytes 1572868
  118.2 4.4 %copy-start.7 = (f32[8,8,16,128]{3,2,0,1:T(8,128)S(1)}, f32[8,8,16,128]{3,2,0,1:T(8,128)}, u32[]{:S(2)}) copy-start(f32[8,8,16,128]{3,2,0,1:T(8,128)} %get-tuple-element.98) | copy-start | bytes 1572868
  119.3 15.5 %copy-start.26 = (f32[8,1]{1,0:T(8,128)S(1)}, f32[8,1]{1,0:T(8,128)}, u32[]{:S(2)}) copy-start(f32[8,1]{1,0:T(8,128)} %get-tuple-element.180) | copy-start | bytes 100
  119.3 15.5 %copy-start.27 = (f32[8,1]{1,0:T(8,128)S(1)}, f32[8,1]{1,0:T(8,128)}, u32[]{:S(2)}) copy-start(f32[8,1]{1,0:T(8,128)} %get-tuple-element.181) | copy-start | bytes 100
  129.4 21.7 %collective-permute-start.9 = (f32[16,84,128]{2,0,1:T(8,128)}, f32[16,84,128]{2,0,1:T(8,128)S(1)}, u32[]{:S(2)}, u32[]{:S(2)}) collective-permute-start(f32[16,84,128]{2,0,1:T(8,128)} %constant_dynamic-update-slice_fusion.7), channel_id=1, source_target_pairs={{0,8},{8,16},{16,24},{24,32},{32,40},{40,48},{48,56},{56,64},{64,7... | collective-permute-start | bytes 2064392 | tf_op jit(solution)/shard_map/ppermute | solution.py:30
  135.6 49.9 %collective-permute-start.10 = (f32[16,84,128]{2,0,1:T(8,128)}, f32[16,84,128]{2,0,1:T(8,128)S(1)}, u32[]{:S(2)}, u32[]{:S(2)}) collective-permute-start(f32[16,84,128]{2,0,1:T(8,128)} %constant_dynamic-update-slice_fusion.12), channel_id=1, source_target_pairs={{8,0},{16,8},{24,16},{32,24},{40,32},{48,40},{56,48},{64,56},{72,6... | collective-permute-start | bytes 2064392 | tf_op jit(solution)/shard_map/ppermute | solution.py:30
  138.8 48.6 %collective-permute-start.11 = (f32[16,84,128]{2,0,1:T(8,128)}, f32[16,84,128]{2,0,1:T(8,128)S(1)}, u32[]{:S(2)}, u32[]{:S(2)}) collective-permute-start(f32[16,84,128]{2,0,1:T(8,128)} %constant_dynamic-update-slice_fusion.17), channel_id=1, source_target_pairs={{16,0},{24,8},{32,16},{40,24},{48,32},{56,40},{64,48},{72,56},{80,... | collective-permute-start | bytes 2064392 | tf_op jit(solution)/shard_map/ppermute | solution.py:30
  155.4 65.6 %collective-permute-start.16 = (f32[16,84,128]{2,0,1:T(8,128)}, f32[16,84,128]{2,0,1:T(8,128)}, u32[]{:S(2)}, u32[]{:S(2)}) collective-permute-start(f32[16,84,128]{2,0,1:T(8,128)} %constant_dynamic-update-slice_fusion.54), channel_id=1, source_target_pairs={{16,0},{24,8},{32,16},{40,24},{48,32},{56,40},{64,48},{72,56},{80,... | collective-permute-start | bytes 2064392 | tf_op jit(solution)/shard_map/ppermute | solution.py:30
  158.2 64.7 %collective-permute-start.15 = (f32[16,84,128]{2,0,1:T(8,128)}, f32[16,84,128]{2,0,1:T(8,128)}, u32[]{:S(2)}, u32[]{:S(2)}) collective-permute-start(f32[16,84,128]{2,0,1:T(8,128)} %constant_dynamic-update-slice_fusion.49), channel_id=1, source_target_pairs={{8,0},{16,8},{24,16},{32,24},{40,32},{48,40},{56,48},{64,56},{72,6... | collective-permute-start | bytes 2064392 | tf_op jit(solution)/shard_map/ppermute | solution.py:30
  163.2 61.6 %collective-permute-start.14 = (f32[16,84,128]{2,0,1:T(8,128)}, f32[16,84,128]{2,0,1:T(8,128)}, u32[]{:S(2)}, u32[]{:S(2)}) collective-permute-start(f32[16,84,128]{2,0,1:T(8,128)} %constant_dynamic-update-slice_fusion.44), channel_id=1, source_target_pairs={{0,8},{8,16},{16,24},{24,32},{32,40},{40,48},{48,56},{56,64},{64,7... | collective-permute-start | bytes 2064392 | tf_op jit(solution)/shard_map/ppermute | solution.py:30
  185.5 41.4 %collective-permute-start.13 = (f32[16,84,128]{2,0,1:T(8,128)}, f32[16,84,128]{2,0,1:T(8,128)}, u32[]{:S(2)}, u32[]{:S(2)}) collective-permute-start(f32[16,84,128]{2,0,1:T(8,128)} %constant_dynamic-update-slice_fusion.39), channel_id=1, source_target_pairs={{0,16},{8,24},{16,32},{24,40},{32,48},{40,56},{48,64},{56,72},{64,... | collective-permute-start | bytes 2064392 | tf_op jit(solution)/shard_map/ppermute | solution.py:30
  187.5 1.8 copy-start.16
  197.3 1.1 copy-start.13
  199.5 1.3 copy-start.14
  209.8 1.6 copy-start.6
  212.5 1.0 copy-start
  214.2 6.9 %collective-permute-start.12 = (f32[1,5,8,128]{3,2,1,0:T(8,128)S(1)}, f32[1,5,8,128]{3,2,1,0:T(8,128)S(1)}, u32[]{:S(2)}, u32[]{:S(2)}) collective-permute-start(f32[1,5,8,128]{3,2,1,0:T(8,128)S(1)} %maximum_bitcast_fusion.3), channel_id=1, source_target_pairs={{0,8},{8,16},{16,24},{24,32},{32,40},{40,48},{48,56},{56,64},{64,7... | collective-permute-start | bytes 61448 | tf_op jit(solution)/shard_map/ppermute | solution.py:281
  226.0 2.9 %copy-start.3 = (f32[32,132,128]{2,0,1:T(8,128)S(1)}, f32[32,132,128]{2,0,1:T(8,128)}, u32[]{:S(2)}) copy-start(f32[32,132,128]{2,0,1:T(8,128)} %copy-done.2) | copy-start | bytes 6488068
  229.1 1.8 copy-start.17
  231.7 7.3 %collective-permute-start.17 = (f32[2,5,8,128]{3,2,1,0:T(8,128)S(1)}, f32[2,5,8,128]{3,2,1,0:T(8,128)S(1)}, u32[]{:S(2)}, u32[]{:S(2)}) collective-permute-start(f32[2,5,8,128]{3,2,1,0:T(8,128)S(1)} %pad_maximum_fusion.3), channel_id=1, source_target_pairs={{0,16},{8,24},{16,32},{24,40},{32,48},{40,56},{48,64},{56,72},{64,... | collective-permute-start | bytes 122888 | tf_op jit(solution)/shard_map/ppermute | solution.py:281
  235.0 4.0 %copy-start.15 = (f32[8,16,20,128]{3,1,2,0:T(8,128)}, f32[8,16,20,128]{3,1,2,0:T(8,128)S(1)}, u32[]{:S(2)}) copy-start(f32[8,16,20,128]{3,1,2,0:T(8,128)S(1)} %constant_dynamic-update-slice_fusion.77) | copy-start | bytes 3932164
  239.1 9.8 %collective-permute-start.18 = (f32[4,5,8,128]{3,2,1,0:T(8,128)S(1)}, f32[4,5,8,128]{3,2,1,0:T(8,128)S(1)}, u32[]{:S(2)}, u32[]{:S(2)}) collective-permute-start(f32[4,5,8,128]{3,2,1,0:T(8,128)S(1)} %pad_maximum_fusion.2), channel_id=1, source_target_pairs={{0,32},{8,40},{16,48},{24,56},{32,64},{40,72},{48,80},{56,88},{64,... | collective-permute-start | bytes 245768 | tf_op jit(solution)/shard_map/ppermute | solution.py:281
  249.6 14.0 %collective-permute-start.19 = (f32[8,5,8,128]{3,2,1,0:T(8,128)}, f32[8,5,8,128]{3,2,1,0:T(8,128)S(1)}, u32[]{:S(2)}, u32[]{:S(2)}) collective-permute-start(f32[8,5,8,128]{3,2,1,0:T(8,128)} %pad_maximum_fusion.1), channel_id=1, source_target_pairs={{0,64},{8,72},{16,80},{24,88},{32,96},{40,104},{48,112},{56,120},{... | collective-permute-start | bytes 491528 | tf_op jit(solution)/shard_map/ppermute | solution.py:281
  263.6 17.4 %collective-permute-start.20 = (f32[16,5,8,128]{3,2,1,0:T(8,128)S(1)}, f32[16,5,8,128]{3,2,1,0:T(8,128)S(1)}, u32[]{:S(2)}, u32[]{:S(2)}) collective-permute-start(f32[16,5,8,128]{3,2,1,0:T(8,128)S(1)} %pad_maximum_fusion), channel_id=1, source_target_pairs={{0,128},{8,136},{16,144},{24,152},{32,160},{40,168},{48,176},{56,1... | collective-permute-start | bytes 983048 | tf_op jit(solution)/shard_map/ppermute | solution.py:281
  263.8 20.4 %copy-start.1 = (f32[8,2,128,128]{2,3,1,0:T(8,128)S(1)}, f32[8,2,128,128]{2,3,1,0:T(8,128)}, u32[]{:S(2)}) copy-start(f32[8,2,128,128]{2,3,1,0:T(8,128)} %copy-done) | copy-start | bytes 3145732
  263.8 20.4 %copy-start.20 = (f32[8,128]{0,1:T(8,128)S(1)}, f32[8,128]{0,1:T(8,128)}, u32[]{:S(2)}) copy-start(f32[8,128]{0,1:T(8,128)} %copy.101) | copy-start | bytes 12292
  263.9 20.4 %copy-start.21 = (f32[8,128]{0,1:T(8,128)S(1)}, f32[8,128]{0,1:T(8,128)}, u32[]{:S(2)}) copy-start(f32[8,128]{0,1:T(8,128)} %copy.99) | copy-start | bytes 12292

commit v4 on v0

--- a/solution.py
+++ b/solution.py
@@ -244,17 +244,11 @@
     first_row = local_solve[:, :, 0, :]
     last_row = local_solve[:, :, columns - 1, :]
     packed = jnp.concatenate([first_row, last_row, coef_rows[None]], axis=0)
-    held = packed[None]
-    step = 1
-    while step < count:
-        ring = [(i, (i + step) % count) for i in range(count)]
-        held = jnp.concatenate([held, lax.ppermute(held, "gx", ring)], axis=0)
-        if step == 1:
-            held, tracer_received = lax.optimization_barrier((held, tracer_received))
-        step *= 2
-    reverse = held[::-1]
-    doubled = jnp.concatenate([reverse, reverse], axis=0)
-    packed_all = lax.dynamic_slice_in_dim(doubled, count - 1 - position, count, 0)
+    slots = lax.dynamic_update_slice_in_dim(
+        jnp.zeros((count,) + packed.shape, packed.dtype), packed[None], position, 0
+    )
+    packed_all = lax.psum(slots, "gx")
+    tracer_received = lax.optimization_barrier((slots, tracer_received))[1]
     left_value, right_value = interface_solve(packed_all, position, first_row.shape[0])
     wind_fields = (
         local_solve

time: 257 us -> 369 us (1.44)
  waiting for transfers between devices: 52.3 us -> 162 us
  between operations: 46.7 us -> 60.1 us
  starting transfers between devices: 51.4 us -> 39.4 us
    psum x0 -> x1, waiting for transfers between devices: none -> 132 us  [local(): packed_all = lax.psum(slots, 'gx')]
    ppermute x5 -> x0, waiting for transfers between devices: 31.9 us -> none  [local(): held = jnp.concatenate([held, lax.ppermute(held, 'gx', ring)], axis=0)]
    ppermute x5 -> x0, starting transfers between devices: 12.1 us -> none  [local(): held = jnp.concatenate([held, lax.ppermute(held, 'gx', ring)], axis=0)]
    ppermute x8, waiting for transfers between devices: 20.3 us -> 29.7 us  [shifted_2(): lax.ppermute(value, axis, [(source, source + steps) for source in range(l...]
    unnamed x94 -> x90, local copies, waits for them, and re-layouts: 26.5 us -> 27.2 us
  transfers between devices with their start and end apart: 17 -> 13, of which waited for: 6 -> 6; matrix products, arithmetic and copies ran while one was open for 30% -> 22% of each run, Pallas kernels for 0% -> 0%
where the time goes in v4:
time: 369 us; the launch traced here: 365 us
  waiting for transfers between devices  162 us (44%)
  between operations  60.1 us (16%)
  local copies, waits for them, and re-layouts  59.9 us (16%)
  starting transfers between devices  39.4 us (11%)
  other arithmetic  39 us (11%)
    psum x1, waiting for transfers between devices, local(): packed_all = lax.psum(slots, 'gx')  132 us
    ppermute x8, waiting for transfers between devices, shifted_2(): lax.ppermute(value, axis, [(source, source + steps) for source in range(l...  29.7 us
    unnamed x90, local copies, waits for them, and re-layouts  27.2 us
    ppermute x8, starting transfers between devices, shifted_2(): lax.ppermute(value, axis, [(source, source + steps) for source in range(l...  25.8 us
    add x2, other arithmetic, interpolate(): running_total + tap_term  16 us
    slice x4, local copies, waits for them, and re-layouts, send_windows(): received_main[delta] = sent[:, 0:span]  8.06 us
  transfers between devices with their start and end apart: 13, of which 6 were waited for; matrix products, arithmetic and copies ran while one was open for 22% of the time, Pallas kernels for 0%

profile of v4, /device:TPU:34, one launch (start us, length us, event | category | flops | bytes accessed | tf_op | source)
XLA Modules:
  0.0 365.4 jit_solution(2702450005790734533)
XLA Ops:
  7.2 2.9 copy.83
  10.2 1.3 copy-done.4
  11.5 3.5 collective-permute-start
  15.0 4.5 %collective-permute-start.1 = (f32[32,2,128]{2,0,1:T(8,128)S(1)}, f32[32,2,128]{2,0,1:T(8,128)S(1)}, u32[]{:S(2)}, u32[]{:S(2)}) collective-permute-start(f32[32,2,128]{2,0,1:T(8,128)S(1)} %get-tuple-element.53), channel_id=1, source_target_pairs={{8,0},{16,8},{24,16},{32,24},{40,32},{48,40},{56,48},{64,56},{72,6... | collective-permute-start | bytes 98312 | tf_op jit(solution)/shard_map/ppermute | solution.py:118
  21.8 3.9 %fusion.63 = (f32[8,8,16,128]{3,1,2,0:T(8,128)}, f32[8,8,16,128]{3,1,2,0:T(8,128)}, f32[8,8,16,128]{3,1,2,0:T(8,128)}, f32[8,8,16,128]{3,1,2,0:T(8,128)}, f32[8,...) fusion(f32[8,8,16,128]{3,2,1,0:T(8,128)S(1)} %bitcast.373, ...), kind=kLoop, calls=%fused_computation.131 | loop fusion | flops 9175040 | bytes 6291456 | tf_op jit(solution)/shard_map/mul | solution.py:40
  26.0 0.8 fusion.100
  26.9 0.8 fusion.108
  57.9 1.8 pad_maximum_fusion
  59.7 2.9 fusion.115
  62.7 3.2 copy.50
  65.9 1.9 collective-permute-start.2
  67.8 3.2 copy.51
  71.1 3.6 collective-permute-start.3
  77.9 0.9 constant_dynamic-update-slice_fusion
  78.9 3.0 collective-permute-start.4
  98.5 2.6 collective-permute-start.5
  101.9 5.4 %collective-permute-start.6 = (f32[16,84,128]{2,0,1:T(8,128)}, f32[16,84,128]{2,0,1:T(8,128)S(1)}, u32[]{:S(2)}, u32[]{:S(2)}) collective-permute-start(f32[16,84,128]{2,0,1:T(8,128)} %constant_dynamic-update-slice_fusion.10), channel_id=1, source_target_pairs={{8,0},{16,8},{24,16},{32,24},{40,32},{48,40},{56,48},{64,56},{72,6... | collective-permute-start | bytes 2064392 | tf_op jit(solution)/shard_map/ppermute | solution.py:30
  108.0 3.3 collective-permute-start.7
  111.7 8.9 %collective-permute-done.5 = f32[16,84,128]{2,0,1:T(8,128)S(1)} collective-permute-done((f32[16,84,128]{2,0,1:T(8,128)}, f32[16,84,128]{2,0,1:T(8,128)S(1)}, u32[]{:S(2)}, u32[]{:S(2)}) %collective-permute-start.5) | collective-permute-done | bytes 688160 | tf_op jit(solution)/shard_map/ppermute | solution.py:30
  120.8 0.9 constant_dynamic-update-slice_fusion.56
  121.6 0.9 constant_dynamic-update-slice_fusion.55
  122.5 0.9 constant_dynamic-update-slice_fusion.54
  123.4 0.9 constant_dynamic-update-slice_fusion.53
  125.0 2.8 collective-permute-start.11
  128.5 2.2 collective-permute-start.10
  131.4 3.7 %collective-permute-start.9 = (f32[16,84,128]{2,0,1:T(8,128)}, f32[16,84,128]{2,0,1:T(8,128)}, u32[]{:S(2)}, u32[]{:S(2)}) collective-permute-start(f32[16,84,128]{2,0,1:T(8,128)} %constant_dynamic-update-slice_fusion.42), channel_id=1, source_target_pairs={{0,8},{8,16},{16,24},{24,32},{32,40},{40,48},{48,56},{56,64},{64,7... | collective-permute-start | bytes 2064392 | tf_op jit(solution)/shard_map/ppermute | solution.py:30
  135.8 1.5 collective-permute-done.6
  137.3 3.0 collective-permute-start.8
  140.3 9.9 %collective-permute-done.7 = f32[16,84,128]{2,0,1:T(8,128)S(1)} collective-permute-done((f32[16,84,128]{2,0,1:T(8,128)}, f32[16,84,128]{2,0,1:T(8,128)S(1)}, u32[]{:S(2)}, u32[]{:S(2)}) %collective-permute-start.7) | collective-permute-done | bytes 688160 | tf_op jit(solution)/shard_map/ppermute | solution.py:30
  150.4 1.7 copy-done.12
  152.3 0.9 constant_dynamic-update-slice_fusion.35
  153.3 0.9 constant_dynamic-update-slice_fusion.34
  154.3 0.9 constant_dynamic-update-slice_fusion.33
  155.3 0.9 constant_dynamic-update-slice_fusion.32
  156.4 0.9 constant_dynamic-update-slice_fusion.31
  157.4 0.9 constant_dynamic-update-slice_fusion.30
  158.4 0.9 constant_dynamic-update-slice_fusion.29
  159.5 2.0 copy.52
  161.4 2.0 copy.53
  163.4 3.2 maximum_bitcast_fusion
  166.7 8.0 %fusion.31 = f32[8,2,8,16,128]{4,2,1,3,0:T(8,128)} fusion(f32[8,2,8,20,132]{4,2,1,3,0:T(8,128)S(1)} %maximum_bitcast_fusion, f32[8,8,16,128]{3,1,2,0:T(8,128)} %get-tuple-element.179, f32[8,8,16,128]{3,1,2,0:T(8,128)} %get-tuple-element.178, f32[8,8,16,128]{3,1,2,0:T(8,128)} %get-tuple-element.176, f32[8,8,16,128]{3,1,2,0:T(8,128)} %get-tuple-element.177, ...), kind=kLoop, calls=%fused_computation.61 | loop fusion | flops 14155776 | bytes 32505856 | tf_op jit(solution)/shard_map/add | solution.py:58
  174.7 2.7 fusion.58
  177.4 1.0 copy-done.2
  179.1 0.8 collective-permute-done.11
  179.9 2.0 slice.448
  181.8 0.8 slice.452
  182.6 8.5 %collective-permute-done.10 = f32[16,84,128]{2,0,1:T(8,128)} collective-permute-done((f32[16,84,128]{2,0,1:T(8,128)}, f32[16,84,128]{2,0,1:T(8,128)}, u32[]{:S(2)}, u32[]{:S(2)}) %collective-permute-start.10) | collective-permute-done | bytes 688160 | tf_op jit(solution)/shard_map/ppermute | solution.py:30
  191.1 2.0 slice.447
  193.1 0.8 slice.451
  193.9 2.0 slice.446
  195.9 0.8 slice.450
  196.6 2.1 slice.445
  198.8 0.8 slice.449
  199.5 1.2 constant_dynamic-update-slice_fusion.69
  200.8 1.2 constant_dynamic-update-slice_fusion.68
  203.2 2.1 copy.60
  205.3 2.0 copy.61
  207.4 3.2 maximum_bitcast_fusion.1
  210.6 8.0 %fusion.2 = f32[8,2,8,16,128]{4,2,1,3,0:T(8,128)} fusion(f32[8,2,8,20,132]{4,2,1,3,0:T(8,128)S(1)} %maximum_bitcast_fusion.1, f32[8,8,16,128]{3,1,2,0:T(8,128)} %get-tuple-element.179, f32[8,8,16,128]{3,1,2,0:T(8,128)} %get-tuple-element.178, f32[8,8,16,128]{3,1,2,0:T(8,128)} %get-tuple-element.176, f32[8,8,16,128]{3,1,2,0:T(8,128)} %get-tuple-element.177, ...), kind=kLoop, calls=%fused_computation.7 | loop fusion | flops 14155776 | bytes 32505856 | tf_op jit(solution)/shard_map/add | solution.py:58
  218.6 2.6 copy.63
  221.2 132.5 %all-reduce.11.cloned.1.call-done.packed_ref = f32[32,5,8,128]{3,2,1,0:T(8,128)} async-done(((f32[32,5,8,128]{3,2,1,0:T(8,128)}), f32[32,5,8,128]{3,2,1,0:T(8,128)}) %all-reduce.11.cloned.1.call-update) | async-done | bytes 655376 | tf_op jit(solution)/shard_map/psum | solution.py:250
  353.6 2.2 shard_map.86
  355.9 1.4 multiply_subtract_fusion
  357.3 1.3 copy.62
  (134 shorter events, 15.3 us)
Async XLA Ops:
  7.2 12.3 %copy-start.15 = (s32[256,1]{0,1:T(1,128)S(1)}, s32[256,1]{0,1:T(1,128)}, u32[]{:S(2)}) copy-start(s32[256,1]{0,1:T(1,128)} %param.10) | copy-start | bytes 3076
  7.2 14.0 %copy-start.13 = (f32[8,128,128]{2,1,0:T(8,128)S(1)}, f32[8,128,128]{2,1,0:T(8,128)}, u32[]{:S(2)}) copy-start(f32[8,128,128]{2,1,0:T(8,128)} %param.8) | copy-start | bytes 1572868
  7.2 14.0 %copy-start.14 = (f32[8,128,128]{2,1,0:T(8,128)S(1)}, f32[8,128,128]{2,1,0:T(8,128)}, u32[]{:S(2)}) copy-start(f32[8,128,128]{2,1,0:T(8,128)} %param.9) | copy-start | bytes 1572868
  7.2 346.4 %all-reduce.11.cloned.1.call-start = ((), (), s32[]{:S(2)}) async-start(), calls=%async_computation | async-start | bytes 1310720 | tf_op jit(solution)/shard_map/psum | solution.py:250
  10.1 1.4 copy-start.4
  10.1 11.1 %copy-start.6 = (f32[8,128,128]{2,1,0:T(8,128)S(1)}, f32[8,128,128]{2,1,0:T(8,128)}, u32[]{:S(2)}) copy-start(f32[8,128,128]{2,1,0:T(8,128)} %param.11) | copy-start | bytes 1572868
  11.5 46.4 %collective-permute-start = (f32[32,2,128]{2,0,1:T(8,128)S(1)}, f32[32,2,128]{2,0,1:T(8,128)S(1)}, u32[]{:S(2)}, u32[]{:S(2)}) collective-permute-start(f32[32,2,128]{2,0,1:T(8,128)S(1)} %get-tuple-element.52), channel_id=1, source_target_pairs={{0,8},{8,16},{16,24},{24,32},{32,40},{40,48},{48,56},{56,64},{64,7... | collective-permute-start | bytes 98312 | tf_op jit(solution)/shard_map/ppermute | solution.py:117
  15.0 43.0 %collective-permute-start.1 = (f32[32,2,128]{2,0,1:T(8,128)S(1)}, f32[32,2,128]{2,0,1:T(8,128)S(1)}, u32[]{:S(2)}, u32[]{:S(2)}) collective-permute-start(f32[32,2,128]{2,0,1:T(8,128)S(1)} %get-tuple-element.53), channel_id=1, source_target_pairs={{8,0},{16,8},{24,16},{32,24},{40,32},{48,40},{56,48},{64,56},{72,6... | collective-permute-start | bytes 98312 | tf_op jit(solution)/shard_map/ppermute | solution.py:118
  21.8 3.9 %copy-start.19 = (f32[8,1]{0,1:T(1,128)S(1)}, f32[8,1]{0,1:T(1,128)}, u32[]{:S(2)}) copy-start(f32[8,1]{0,1:T(1,128)} %param.13) | copy-start | bytes 100
  21.8 4.0 %copy-start.20 = (f32[8,1]{0,1:T(1,128)S(1)}, f32[8,1]{0,1:T(1,128)}, u32[]{:S(2)}) copy-start(f32[8,1]{0,1:T(1,128)} %param.12) | copy-start | bytes 100
  59.7 60.9 %copy-start = (f32[32,132,128]{2,0,1:T(8,128)}, f32[32,132,128]{2,0,1:T(8,128)S(1)}, u32[]{:S(2)}) copy-start(f32[32,132,128]{2,0,1:T(8,128)S(1)} %pad_maximum_fusion) | copy-start | bytes 6488068
  65.9 11.7 %collective-permute-start.2 = (f32[32,132,2]{1,0,2:T(8,128)S(1)}, f32[32,132,2]{1,0,2:T(8,128)S(1)}, u32[]{:S(2)}, u32[]{:S(2)}) collective-permute-start(f32[32,132,2]{1,0,2:T(8,128)S(1)} %copy.50), channel_id=1, source_target_pairs={{0,1},{1,2},{2,3},{3,4},{4,5},{5,6},{6,7},{8,9},{9,10},{10,11},{11... | collective-permute-start | bytes 101384 | tf_op jit(solution)/shard_map/ppermute | solution.py:126
  71.1 6.5 %collective-permute-start.3 = (f32[32,132,2]{1,0,2:T(8,128)S(1)}, f32[32,132,2]{1,0,2:T(8,128)S(1)}, u32[]{:S(2)}, u32[]{:S(2)}) collective-permute-start(f32[32,132,2]{1,0,2:T(8,128)S(1)} %copy.51), channel_id=1, source_target_pairs={{1,0},{2,1},{3,2},{4,3},{5,4},{6,5},{7,6},{9,8},{10,9},{11,10},{12... | collective-permute-start | bytes 101384 | tf_op jit(solution)/shard_map/ppermute | solution.py:127
  77.6 5.0 %copy-start.16 = (f32[16,84,128]{2,0,1:T(8,128)}, f32[16,84,128]{2,0,1:T(8,128)S(1)}, u32[]{:S(2)}) copy-start(f32[16,84,128]{2,0,1:T(8,128)S(1)} %get-tuple-element.70) | copy-start | bytes 2064388
  77.6 5.0 %copy-start.17 = (f32[16,84,128]{2,0,1:T(8,128)}, f32[16,84,128]{2,0,1:T(8,128)S(1)}, u32[]{:S(2)}) copy-start(f32[16,84,128]{2,0,1:T(8,128)S(1)} %get-tuple-element.71) | copy-start | bytes 2064388
  77.6 5.0 %copy-start.18 = (f32[16,84,128]{2,0,1:T(8,128)}, f32[16,84,128]{2,0,1:T(8,128)S(1)}, u32[]{:S(2)}) copy-start(f32[16,84,128]{2,0,1:T(8,128)S(1)} %get-tuple-element.72) | copy-start | bytes 2064388
  78.9 32.7 %collective-permute-start.4 = (f32[16,84,128]{2,0,1:T(8,128)}, f32[16,84,128]{2,0,1:T(8,128)S(1)}, u32[]{:S(2)}, u32[]{:S(2)}) collective-permute-start(f32[16,84,128]{2,0,1:T(8,128)} %constant_dynamic-update-slice_fusion), channel_id=1, source_target_pairs={{0,16},{8,24},{16,32},{24,40},{32,48},{40,56},{48,64},{56,72},{64,... | collective-permute-start | bytes 2064392 | tf_op jit(solution)/shard_map/ppermute | solution.py:30
  98.5 22.0 %collective-permute-start.5 = (f32[16,84,128]{2,0,1:T(8,128)}, f32[16,84,128]{2,0,1:T(8,128)S(1)}, u32[]{:S(2)}, u32[]{:S(2)}) collective-permute-start(f32[16,84,128]{2,0,1:T(8,128)} %constant_dynamic-update-slice_fusion.5), channel_id=1, source_target_pairs={{0,8},{8,16},{16,24},{24,32},{32,40},{40,48},{48,56},{56,64},{64,7... | collective-permute-start | bytes 2064392 | tf_op jit(solution)/shard_map/ppermute | solution.py:30
  101.9 35.4 %collective-permute-start.6 = (f32[16,84,128]{2,0,1:T(8,128)}, f32[16,84,128]{2,0,1:T(8,128)S(1)}, u32[]{:S(2)}, u32[]{:S(2)}) collective-permute-start(f32[16,84,128]{2,0,1:T(8,128)} %constant_dynamic-update-slice_fusion.10), channel_id=1, source_target_pairs={{8,0},{16,8},{24,16},{32,24},{40,32},{48,40},{56,48},{64,56},{72,6... | collective-permute-start | bytes 2064392 | tf_op jit(solution)/shard_map/ppermute | solution.py:30
  108.0 42.3 %collective-permute-start.7 = (f32[16,84,128]{2,0,1:T(8,128)}, f32[16,84,128]{2,0,1:T(8,128)S(1)}, u32[]{:S(2)}, u32[]{:S(2)}) collective-permute-start(f32[16,84,128]{2,0,1:T(8,128)} %constant_dynamic-update-slice_fusion.15), channel_id=1, source_target_pairs={{16,0},{24,8},{32,16},{40,24},{48,32},{56,40},{64,48},{72,56},{80,... | collective-permute-start | bytes 2064392 | tf_op jit(solution)/shard_map/ppermute | solution.py:30
  125.0 54.9 %collective-permute-start.11 = (f32[16,84,128]{2,0,1:T(8,128)}, f32[16,84,128]{2,0,1:T(8,128)}, u32[]{:S(2)}, u32[]{:S(2)}) collective-permute-start(f32[16,84,128]{2,0,1:T(8,128)} %constant_dynamic-update-slice_fusion.52), channel_id=1, source_target_pairs={{16,0},{24,8},{32,16},{40,24},{48,32},{56,40},{64,48},{72,56},{80,... | collective-permute-start | bytes 2064392 | tf_op jit(solution)/shard_map/ppermute | solution.py:30
  128.5 62.6 %collective-permute-start.10 = (f32[16,84,128]{2,0,1:T(8,128)}, f32[16,84,128]{2,0,1:T(8,128)}, u32[]{:S(2)}, u32[]{:S(2)}) collective-permute-start(f32[16,84,128]{2,0,1:T(8,128)} %constant_dynamic-update-slice_fusion.47), channel_id=1, source_target_pairs={{8,0},{16,8},{24,16},{32,24},{40,32},{48,40},{56,48},{64,56},{72,6... | collective-permute-start | bytes 2064392 | tf_op jit(solution)/shard_map/ppermute | solution.py:30
  131.4 62.5 %collective-permute-start.9 = (f32[16,84,128]{2,0,1:T(8,128)}, f32[16,84,128]{2,0,1:T(8,128)}, u32[]{:S(2)}, u32[]{:S(2)}) collective-permute-start(f32[16,84,128]{2,0,1:T(8,128)} %constant_dynamic-update-slice_fusion.42), channel_id=1, source_target_pairs={{0,8},{8,16},{16,24},{24,32},{32,40},{40,48},{48,56},{56,64},{64,7... | collective-permute-start | bytes 2064392 | tf_op jit(solution)/shard_map/ppermute | solution.py:30
  137.3 59.3 %collective-permute-start.8 = (f32[16,84,128]{2,0,1:T(8,128)}, f32[16,84,128]{2,0,1:T(8,128)}, u32[]{:S(2)}, u32[]{:S(2)}) collective-permute-start(f32[16,84,128]{2,0,1:T(8,128)} %constant_dynamic-update-slice_fusion.37), channel_id=1, source_target_pairs={{0,16},{8,24},{16,32},{24,40},{32,48},{40,56},{48,64},{56,72},{64,... | collective-permute-start | bytes 2064392 | tf_op jit(solution)/shard_map/ppermute | solution.py:30
  150.3 1.8 copy-start.12
  159.3 2.1 copy-start.10
  163.4 3.2 copy-start.5
  177.4 1.0 copy-start.2
  179.1 16.8 %copy-start.9 = (f32[32,5,8,128]{3,2,1,0:T(8,128)}, f32[32,5,8,128]{3,2,1,0:T(8,128)S(1)}, u32[]{:S(2)}) copy-start(f32[32,5,8,128]{3,2,1,0:T(8,128)S(1)} %constant_dynamic-update-slice_fusion.78) | copy-start | bytes 1966084
  196.6 5.3 %copy-start.1 = (f32[32,132,128]{2,0,1:T(8,128)S(1)}, f32[32,132,128]{2,0,1:T(8,128)}, u32[]{:S(2)}) copy-start(f32[32,132,128]{2,0,1:T(8,128)} %copy-done) | copy-start | bytes 6488068
  199.5 2.5 copy-start.8
  200.7 1.4 copy-start.7
  202.4 2.9 copy-start.11
  218.6 137.3 %copy-start.3 = (f32[8,2,128,128]{2,3,1,0:T(8,128)S(1)}, f32[8,2,128,128]{2,3,1,0:T(8,128)}, u32[]{:S(2)}) copy-start(f32[8,2,128,128]{2,3,1,0:T(8,128)} %copy-done.2) | copy-start | bytes 3145732
Sparse Core Ops, SparseCore 0:
  199.7 153.9 all-reduce.10

commit v5 on v0

--- a/solution.py
+++ b/solution.py
@@ -200,12 +200,10 @@
     )
 
 
-def advect_group(windows, shift_x, shift_y, field_count):
-    block_count = windows.shape[0]
-    level_count, columns, rows_here = shift_x.shape
+def advect_group(windows, across, along, field_count):
+    block_count, _, level_count, _, rows_here = across.shape
+    columns = block_count * BX
     windows = windows.reshape(block_count, field_count, level_count, BX + 4, rows_here + 4)
-    across = shift_x.reshape(level_count, block_count, BX, rows_here).transpose(1, 0, 2, 3)[:, None]
-    along = shift_y.reshape(level_count, block_count, BX, rows_here).transpose(1, 0, 2, 3)[:, None]
     interpolated = interpolate(windows, across, along, BX, rows_here)
     return interpolated.transpose(1, 2, 0, 3, 4).reshape(
         field_count, level_count, columns, rows_here
@@ -223,6 +221,9 @@
     main = halo_x(flat, "gx", 2)
     halo = halo_y(main, "gy", 2).transpose(0, 2, 1)
     offsets = block_offset[:, 0]
+    across = shift_x.reshape(level_count, block_count, BX, rows_here).transpose(1, 0, 2, 3)[:, None]
+    along = shift_y.reshape(level_count, block_count, BX, rows_here).transpose(1, 0, 2, 3)[:, None]
+    across, along, main, halo = lax.optimization_barrier((across, along, main, halo))
     wind_main, wind_halo = main[:wind_channels], halo[:wind_channels]
     tracer_main, tracer_halo = main[wind_channels:], halo[wind_channels:]
     wind_received = send_windows(wind_main, wind_halo, offsets, position, count, block_count)
@@ -230,7 +231,7 @@
     wind_windows = assemble_windows(
         wind_main, wind_halo, *wind_received, offsets, position, block_count
     )
-    winds = advect_group(wind_windows, shift_x, shift_y, 2)
+    winds = advect_group(wind_windows, across, along, 2)
     local_solve = jnp.einsum("lij,wljy->wliy", group_inverse, winds, precision=PRECISE)
     lower_here = lower_coupling[:, 0]
     upper_here = upper_coupling[:, 0]
@@ -264,7 +265,7 @@
     tracer_windows = assemble_windows(
         tracer_main, tracer_halo, *tracer_received, offsets, position, block_count
     )
-    tracers = advect_group(tracer_windows, shift_x, shift_y, field_count - 2)
+    tracers = advect_group(tracer_windows, across, along, field_count - 2)
     return (wind_fields, tracers)
 
 

time: 257 us -> 263 us (1.023)
  starting transfers between devices: 51.4 us -> 62.9 us
    ppermute x5, waiting for transfers between devices: 31.9 us -> 19 us  [local(): held = jnp.concatenate([held, lax.ppermute(held, 'gx', ring)], axis=0)]
    ppermute x8, starting transfers between devices: 25.8 us -> 38.1 us  [shifted_2(): lax.ppermute(value, axis, [(source, source + steps) for source in range(l...]
    ppermute x8, waiting for transfers between devices: 20.3 us -> 31.3 us  [shifted_2(): lax.ppermute(value, axis, [(source, source + steps) for source in range(l...]
    concatenate x8, other arithmetic: 5.91 us -> 3.2 us  [send_windows(): jnp.concatenate([send_main, send_halo], axis=1)]
    unnamed x94 -> x90, local copies, waits for them, and re-layouts: 26.5 us -> 23.9 us
  transfers between devices with their start and end apart: 17 -> 17, of which waited for: 6 -> 5; matrix products, arithmetic and copies ran while one was open for 30% -> 28% of each run, Pallas kernels for 0% -> 0%
where the time goes in v5:
time: 263 us; the launch traced here: 260 us
  starting transfers between devices  62.9 us (24%)
  local copies, waits for them, and re-layouts  57 us (22%)
  waiting for transfers between devices  50.3 us (19%)
  between operations  46.5 us (18%)
  other arithmetic  38.1 us (14%)
  matrix products  2.71 us (1%)
    ppermute x8, starting transfers between devices, shifted_2(): lax.ppermute(value, axis, [(source, source + steps) for source in range(l...  38.1 us
    ppermute x8, waiting for transfers between devices, shifted_2(): lax.ppermute(value, axis, [(source, source + steps) for source in range(l...  31.3 us
    unnamed x90, local copies, waits for them, and re-layouts  23.9 us
    ppermute x5, waiting for transfers between devices, local(): held = jnp.concatenate([held, lax.ppermute(held, 'gx', ring)], axis=0)  19 us
    add x2, other arithmetic, interpolate(): running_total + tap_term  15.9 us
    ppermute x5, starting transfers between devices, local(): held = jnp.concatenate([held, lax.ppermute(held, 'gx', ring)], axis=0)  11.3 us
    reshape x2, other arithmetic, advect_group(): windows.reshape(block_count, field_count, level_count, BX + 4, rows_here...  6.36 us
    slice x2, local copies, waits for them, and re-layouts, halo_y(): low = lax.ppermute(block[:, :, block.shape[2] - width:], axis, forward)  6.02 us
  transfers between devices with their start and end apart: 17, of which 5 were waited for; matrix products, arithmetic and copies ran while one was open for 28% of the time, Pallas kernels for 0%

profile of v5, /device:TPU:34, one launch (start us, length us, event | category | flops | bytes accessed | tf_op | source)
XLA Modules:
  0.0 259.8 jit_solution(901254099406145028)
XLA Ops:
  0.7 2.9 %copy.75 = f32[4,8,128,128]{3,1,0,2:T(8,128)S(1)} copy(f32[4,8,128,128]{3,2,1,0:T(8,128)} %param.7) | data formatting | bytes 4194304 | tf_op args[0]
  3.6 1.3 copy-done.4
  4.9 3.5 %collective-permute-start = (f32[32,2,128]{2,0,1:T(8,128)S(1)}, f32[32,2,128]{2,0,1:T(8,128)S(1)}, u32[]{:S(2)}, u32[]{:S(2)}) collective-permute-start(f32[32,2,128]{2,0,1:T(8,128)S(1)} %get-tuple-element.62), channel_id=1, source_target_pairs={{0,8},{8,16},{16,24},{24,32},{32,40},{40,48},{48,56},{56,64},{64,7... | collective-permute-start | bytes 98312 | tf_op jit(solution)/shard_map/ppermute | solution.py:117
  8.4 4.5 %collective-permute-start.1 = (f32[32,2,128]{2,0,1:T(8,128)S(1)}, f32[32,2,128]{2,0,1:T(8,128)S(1)}, u32[]{:S(2)}, u32[]{:S(2)}) collective-permute-start(f32[32,2,128]{2,0,1:T(8,128)S(1)} %get-tuple-element.63), channel_id=1, source_target_pairs={{8,0},{16,8},{24,16},{32,24},{40,32},{48,40},{56,48},{64,56},{72,6... | collective-permute-start | bytes 98312 | tf_op jit(solution)/shard_map/ppermute | solution.py:118
  15.1 1.6 copy_bitcast_fusion.2
  17.0 0.8 fusion.83
  19.4 1.8 pad_maximum_fusion
  21.1 2.8 %fusion.98 = (f32[32,132,2]{2,0,1:T(8,128)}, f32[32,132,2]{2,0,1:T(8,128)}) fusion(f32[32,132,128]{2,0,1:T(8,128)S(1)} %pad_maximum_fusion), kind=kLoop, calls=%fused_computation.384 | loop fusion | bytes 135168 | tf_op jit(solution)/shard_map/slice | solution.py:126
  24.0 3.2 %copy.50 = f32[32,132,2]{1,0,2:T(8,128)S(1)} copy(f32[32,132,2]{2,0,1:T(8,128)} %get-tuple-element.60) | data formatting | bytes 67584 | tf_op jit(solution)/shard_map/slice | solution.py:126
  27.2 1.9 collective-permute-start.2
  29.1 3.2 %copy.51 = f32[32,132,2]{1,0,2:T(8,128)S(1)} copy(f32[32,132,2]{2,0,1:T(8,128)} %get-tuple-element.61) | data formatting | bytes 67584 | tf_op jit(solution)/shard_map/slice | solution.py:127
  32.3 3.6 %collective-permute-start.3 = (f32[32,132,2]{1,0,2:T(8,128)S(1)}, f32[32,132,2]{1,0,2:T(8,128)S(1)}, u32[]{:S(2)}, u32[]{:S(2)}) collective-permute-start(f32[32,132,2]{1,0,2:T(8,128)S(1)} %copy.51), channel_id=1, source_target_pairs={{1,0},{2,1},{3,2},{4,3},{5,4},{6,5},{7,6},{9,8},{10,9},{11,10},{12... | collective-permute-start | bytes 101384 | tf_op jit(solution)/shard_map/ppermute | solution.py:127
  82.0 3.0 %collective-permute-start.4 = (f32[16,84,128]{2,0,1:T(8,128)S(1)}, f32[16,84,128]{2,0,1:T(8,128)S(1)}, u32[]{:S(2)}, u32[]{:S(2)}) collective-permute-start(f32[16,84,128]{2,0,1:T(8,128)S(1)} %constant_dynamic-update-slice_fusion), channel_id=1, source_target_pairs={{0,16},{8,24},{16,32},{24,40},{32,48},{40,56},{48,64},{56,72},{64,... | collective-permute-start | bytes 2064392 | tf_op jit(solution)/shard_map/ppermute | solution.py:30
  85.1 2.6 collective-permute-start.5
  87.8 5.4 %collective-permute-start.6 = (f32[16,84,128]{2,0,1:T(8,128)S(1)}, f32[16,84,128]{2,0,1:T(8,128)S(1)}, u32[]{:S(2)}, u32[]{:S(2)}) collective-permute-start(f32[16,84,128]{2,0,1:T(8,128)S(1)} %constant_dynamic-update-slice_fusion.10), channel_id=1, source_target_pairs={{8,0},{16,8},{24,16},{32,24},{40,32},{48,40},{56,48},{64,56},{72,6... | collective-permute-start | bytes 2064392 | tf_op jit(solution)/shard_map/ppermute | solution.py:30
  93.3 3.5 %collective-permute-start.7 = (f32[16,84,128]{2,0,1:T(8,128)S(1)}, f32[16,84,128]{2,0,1:T(8,128)S(1)}, u32[]{:S(2)}, u32[]{:S(2)}) collective-permute-start(f32[16,84,128]{2,0,1:T(8,128)S(1)} %constant_dynamic-update-slice_fusion.15), channel_id=1, source_target_pairs={{16,0},{24,8},{32,16},{40,24},{48,32},{56,40},{64,48},{72,56},{80,... | collective-permute-start | bytes 2064392 | tf_op jit(solution)/shard_map/ppermute | solution.py:30
  96.7 2.0 multiply_bitcast_fusion.9
  99.0 2.2 multiply_bitcast_fusion.8
  101.2 4.1 %collective-permute-done.4 = f32[16,84,128]{2,0,1:T(8,128)S(1)} collective-permute-done((f32[16,84,128]{2,0,1:T(8,128)S(1)}, f32[16,84,128]{2,0,1:T(8,128)S(1)}, u32[]{:S(2)}, u32[]{:S(2)}) %collective-permute-start.4) | collective-permute-done | bytes 688160 | tf_op jit(solution)/shard_map/ppermute | solution.py:30
  105.3 13.1 %collective-permute-done.5 = f32[16,84,128]{2,0,1:T(8,128)S(1)} collective-permute-done((f32[16,84,128]{2,0,1:T(8,128)S(1)}, f32[16,84,128]{2,0,1:T(8,128)S(1)}, u32[]{:S(2)}, u32[]{:S(2)}) %collective-permute-start.5) | collective-permute-done | bytes 688160 | tf_op jit(solution)/shard_map/ppermute | solution.py:30
  118.6 0.9 constant_dynamic-update-slice_fusion.56
  119.5 0.8 constant_dynamic-update-slice_fusion.55
  120.4 0.9 constant_dynamic-update-slice_fusion.54
  121.2 0.9 constant_dynamic-update-slice_fusion.53
  122.8 1.9 collective-permute-start.12
  125.5 17.1 %collective-permute-start.11 = (f32[16,84,128]{2,0,1:T(8,128)}, f32[16,84,128]{2,0,1:T(8,128)}, u32[]{:S(2)}, u32[]{:S(2)}) collective-permute-start(f32[16,84,128]{2,0,1:T(8,128)} %constant_dynamic-update-slice_fusion.47), channel_id=1, source_target_pairs={{8,0},{16,8},{24,16},{32,24},{40,32},{48,40},{56,48},{64,56},{72,6... | collective-permute-start | bytes 2064392 | tf_op jit(solution)/shard_map/ppermute | solution.py:30
  143.3 2.8 %collective-permute-start.10 = (f32[16,84,128]{2,0,1:T(8,128)}, f32[16,84,128]{2,0,1:T(8,128)}, u32[]{:S(2)}, u32[]{:S(2)}) collective-permute-start(f32[16,84,128]{2,0,1:T(8,128)} %constant_dynamic-update-slice_fusion.42), channel_id=1, source_target_pairs={{0,8},{8,16},{16,24},{24,32},{32,40},{40,48},{48,56},{56,64},{64,7... | collective-permute-start | bytes 2064392 | tf_op jit(solution)/shard_map/ppermute | solution.py:30
  146.8 14.1 %collective-permute-done.6 = f32[16,84,128]{2,0,1:T(8,128)S(1)} collective-permute-done((f32[16,84,128]{2,0,1:T(8,128)S(1)}, f32[16,84,128]{2,0,1:T(8,128)S(1)}, u32[]{:S(2)}, u32[]{:S(2)}) %collective-permute-start.6) | collective-permute-done | bytes 688160 | tf_op jit(solution)/shard_map/ppermute | solution.py:30
  160.9 1.9 collective-permute-start.9
  163.0 1.7 copy-done.10
  164.9 0.9 constant_dynamic-update-slice_fusion.35
  165.9 0.9 constant_dynamic-update-slice_fusion.34
  167.0 0.9 constant_dynamic-update-slice_fusion.33
  168.0 0.9 constant_dynamic-update-slice_fusion.32
  169.0 0.9 constant_dynamic-update-slice_fusion.31
  170.0 0.9 constant_dynamic-update-slice_fusion.30
  171.0 0.9 constant_dynamic-update-slice_fusion.29
  172.1 2.0 copy.52
  174.1 2.1 copy.53
  176.2 3.2 %maximum_bitcast_fusion = f32[8,2,8,20,132]{4,2,1,3,0:T(8,128)S(1)} fusion(f32[8,16,20,2]{3,1,2,0:T(8,128)} %copy.53, f32[8,16,20,128]{3,1,2,0:T(8,128)} %copy-done.8, f32[8,16,20,2]{3,1,2,0:T(8,128)} %copy.52), kind=kLoop, calls=%fused_computation | loop fusion | flops 675840 | bytes 2703360 | tf_op jit(solution)/shard_map/reshape | solution.py:206
  179.4 8.0 %fusion.31 = f32[8,2,8,16,128]{4,2,1,3,0:T(8,128)} fusion(f32[8,2,8,20,132]{4,2,1,3,0:T(8,128)S(1)} %maximum_bitcast_fusion, f32[8,8,16,128]{3,1,2,0:T(8,128)} %get-tuple-element.100, f32[8,8,16,128]{3,1,2,0:T(8,128)} %get-tuple-element.99, f32[8,8,16,128]{3,1,2,0:T(8,128)} %get-tuple-element.101, f32[8,8,16,128]{3,1,2,0:T(8,128)} %get-tuple-element.102, ...), kind=kLoop, calls=%fused_computation.63 | loop fusion | flops 14155776 | bytes 32505856 | tf_op jit(solution)/shard_map/add | solution.py:58
  187.4 2.7 %fusion.58 = f32[8,2,128,128]{2,3,1,0:T(8,128)S(1)} fusion(f32[2,8,128,128]{3,1,0,2:T(8,128)} %bitcast.279, f32[8,128,128]{2,1,0:T(8,128)} %param.11), kind=kOutput, calls=%fused_computation.115 | convolution fusion | flops 402653184 | bytes 2621440 | tf_op jit(solution)/shard_map/lij,wljy->wliy/dot_general | solution.py:235
  190.1 1.0 copy-done.2
  193.5 4.4 %collective-permute-done.8 = f32[1,5,8,128]{3,2,1,0:T(8,128)S(1)} collective-permute-done((f32[1,5,8,128]{3,2,1,0:T(8,128)S(1)}, f32[1,5,8,128]{3,2,1,0:T(8,128)S(1)}, u32[]{:S(2)}, u32[]{:S(2)}) %collective-permute-start.8) | collective-permute-done | bytes 20512 | tf_op jit(solution)/shard_map/ppermute | solution.py:252
  197.9 1.1 slice.444
  199.8 1.1 slice.443
  201.7 1.1 slice.442
  202.9 0.9 slice.446
  203.8 1.1 slice.441
  206.2 1.7 copy-done.11
  208.7 2.8 %collective-permute-start.13 = (f32[2,5,8,128]{3,2,1,0:T(8,128)S(1)}, f32[2,5,8,128]{3,2,1,0:T(8,128)S(1)}, u32[]{:S(2)}, u32[]{:S(2)}) collective-permute-start(f32[2,5,8,128]{3,2,1,0:T(8,128)S(1)} %pad_maximum_fusion.4), channel_id=1, source_target_pairs={{0,16},{8,24},{16,32},{24,40},{32,48},{40,56},{48,64},{56,72},{64,... | collective-permute-start | bytes 122888 | tf_op jit(solution)/shard_map/ppermute | solution.py:252
  211.6 0.9 constant_dynamic-update-slice_fusion.75
  212.5 2.1 copy.60
  214.6 2.0 copy.61
  216.6 1.9 collective-permute-start.14
  218.5 3.2 %maximum_bitcast_fusion.1 = f32[8,2,8,20,132]{4,2,1,3,0:T(8,128)S(1)} fusion(f32[8,16,20,2]{3,1,2,0:T(8,128)} %copy.61, f32[8,16,20,128]{3,1,2,0:T(8,128)} %copy-done.9, f32[8,16,20,2]{3,1,2,0:T(8,128)} %copy.60), kind=kLoop, calls=%fused_computation.1 | loop fusion | flops 675840 | bytes 2703360 | tf_op jit(solution)/shard_map/reshape | solution.py:206
  222.4 5.6 %collective-permute-start.15 = (f32[8,5,8,128]{3,2,1,0:T(8,128)}, f32[8,5,8,128]{3,2,1,0:T(8,128)S(1)}, u32[]{:S(2)}, u32[]{:S(2)}) collective-permute-start(f32[8,5,8,128]{3,2,1,0:T(8,128)} %pad_maximum_fusion.2), channel_id=1, source_target_pairs={{0,64},{8,72},{16,80},{24,88},{32,96},{40,104},{48,112},{56,120},{... | collective-permute-start | bytes 491528 | tf_op jit(solution)/shard_map/ppermute | solution.py:252
  228.0 7.9 %fusion.2 = f32[8,2,8,16,128]{4,2,1,3,0:T(8,128)} fusion(f32[8,2,8,20,132]{4,2,1,3,0:T(8,128)S(1)} %maximum_bitcast_fusion.1, f32[8,8,16,128]{3,1,2,0:T(8,128)} %get-tuple-element.100, f32[8,8,16,128]{3,1,2,0:T(8,128)} %get-tuple-element.99, f32[8,8,16,128]{3,1,2,0:T(8,128)} %get-tuple-element.101, f32[8,8,16,128]{3,1,2,0:T(8,128)} %get-tuple-element.102, ...), kind=kLoop, calls=%fused_computation.9 | loop fusion | flops 14155776 | bytes 32505856 | tf_op jit(solution)/shard_map/add | solution.py:58
  235.9 2.5 copy.63
  239.3 14.6 %collective-permute-done.16 = f32[16,5,8,128]{3,2,1,0:T(8,128)S(1)} collective-permute-done((f32[16,5,8,128]{3,2,1,0:T(8,128)S(1)}, f32[16,5,8,128]{3,2,1,0:T(8,128)S(1)}, u32[]{:S(2)}, u32[]{:S(2)}) %collective-permute-start.16) | collective-permute-done | bytes 327712 | tf_op jit(solution)/shard_map/ppermute | solution.py:252
  253.9 1.0 fusion.60.packed_ref
  254.9 2.2 shard_map.86
  257.1 1.4 multiply_subtract_fusion
  258.5 1.3 copy.62
  (147 shorter events, 16.9 us)
Async XLA Ops:
  0.6 12.2 %copy-start.16 = (s32[256,1]{0,1:T(1,128)S(1)}, s32[256,1]{0,1:T(1,128)}, u32[]{:S(2)}) copy-start(s32[256,1]{0,1:T(1,128)} %param.10) | copy-start | bytes 3076
  0.6 13.9 %copy-start.5 = (f32[8,128,128]{2,1,0:T(8,128)S(1)}, f32[8,128,128]{2,1,0:T(8,128)}, u32[]{:S(2)}) copy-start(f32[8,128,128]{2,1,0:T(8,128)} %param.11) | copy-start | bytes 1572868
  3.5 1.3 copy-start.4
  3.5 11.6 %copy-start.12 = (f32[8,128,128]{2,1,0:T(8,128)S(1)}, f32[8,128,128]{2,1,0:T(8,128)}, u32[]{:S(2)}) copy-start(f32[8,128,128]{2,1,0:T(8,128)} %param.9) | copy-start | bytes 1572868
  3.5 11.6 %copy-start.13 = (f32[8,128,128]{2,1,0:T(8,128)S(1)}, f32[8,128,128]{2,1,0:T(8,128)}, u32[]{:S(2)}) copy-start(f32[8,128,128]{2,1,0:T(8,128)} %param.8) | copy-start | bytes 1572868
  4.9 14.5 %collective-permute-start = (f32[32,2,128]{2,0,1:T(8,128)S(1)}, f32[32,2,128]{2,0,1:T(8,128)S(1)}, u32[]{:S(2)}, u32[]{:S(2)}) collective-permute-start(f32[32,2,128]{2,0,1:T(8,128)S(1)} %get-tuple-element.62), channel_id=1, source_target_pairs={{0,8},{8,16},{16,24},{24,32},{32,40},{40,48},{48,56},{56,64},{64,7... | collective-permute-start | bytes 98312 | tf_op jit(solution)/shard_map/ppermute | solution.py:117
  8.4 11.0 %collective-permute-start.1 = (f32[32,2,128]{2,0,1:T(8,128)S(1)}, f32[32,2,128]{2,0,1:T(8,128)S(1)}, u32[]{:S(2)}, u32[]{:S(2)}) collective-permute-start(f32[32,2,128]{2,0,1:T(8,128)S(1)} %get-tuple-element.63), channel_id=1, source_target_pairs={{8,0},{16,8},{24,16},{32,24},{40,32},{48,40},{56,48},{64,56},{72,6... | collective-permute-start | bytes 98312 | tf_op jit(solution)/shard_map/ppermute | solution.py:118
  14.7 2.0 copy-start.17
  14.7 2.1 copy-start.18
  21.1 97.3 %copy-start = (f32[32,132,128]{2,0,1:T(8,128)}, f32[32,132,128]{2,0,1:T(8,128)S(1)}, u32[]{:S(2)}) copy-start(f32[32,132,128]{2,0,1:T(8,128)S(1)} %pad_maximum_fusion) | copy-start | bytes 6488068
  27.2 54.0 %collective-permute-start.2 = (f32[32,132,2]{1,0,2:T(8,128)S(1)}, f32[32,132,2]{1,0,2:T(8,128)S(1)}, u32[]{:S(2)}, u32[]{:S(2)}) collective-permute-start(f32[32,132,2]{1,0,2:T(8,128)S(1)} %copy.50), channel_id=1, source_target_pairs={{0,1},{1,2},{2,3},{3,4},{4,5},{5,6},{6,7},{8,9},{9,10},{10,11},{11... | collective-permute-start | bytes 101384 | tf_op jit(solution)/shard_map/ppermute | solution.py:126
  32.3 48.8 %collective-permute-start.3 = (f32[32,132,2]{1,0,2:T(8,128)S(1)}, f32[32,132,2]{1,0,2:T(8,128)S(1)}, u32[]{:S(2)}, u32[]{:S(2)}) collective-permute-start(f32[32,132,2]{1,0,2:T(8,128)S(1)} %copy.51), channel_id=1, source_target_pairs={{1,0},{2,1},{3,2},{4,3},{5,4},{6,5},{7,6},{9,8},{10,9},{11,10},{12... | collective-permute-start | bytes 101384 | tf_op jit(solution)/shard_map/ppermute | solution.py:127
  81.4 15.3 %copy-start.7 = (f32[8,1,8,16,128]{4,2,3,0,1:T(8,128)S(1)}, f32[8,1,8,16,128]{4,2,3,0,1:T(8,128)}, u32[]{:S(2)}) copy-start(f32[8,1,8,16,128]{4,2,3,0,1:T(8,128)} %get-tuple-element.17) | copy-start | bytes 1572868
  82.0 23.3 %collective-permute-start.4 = (f32[16,84,128]{2,0,1:T(8,128)S(1)}, f32[16,84,128]{2,0,1:T(8,128)S(1)}, u32[]{:S(2)}, u32[]{:S(2)}) collective-permute-start(f32[16,84,128]{2,0,1:T(8,128)S(1)} %constant_dynamic-update-slice_fusion), channel_id=1, source_target_pairs={{0,16},{8,24},{16,32},{24,40},{32,48},{40,56},{48,64},{56,72},{64,... | collective-permute-start | bytes 2064392 | tf_op jit(solution)/shard_map/ppermute | solution.py:30
  85.1 33.3 %collective-permute-start.5 = (f32[16,84,128]{2,0,1:T(8,128)S(1)}, f32[16,84,128]{2,0,1:T(8,128)S(1)}, u32[]{:S(2)}, u32[]{:S(2)}) collective-permute-start(f32[16,84,128]{2,0,1:T(8,128)S(1)} %constant_dynamic-update-slice_fusion.5), channel_id=1, source_target_pairs={{0,8},{8,16},{16,24},{24,32},{32,40},{40,48},{48,56},{56,64},{64,7... | collective-permute-start | bytes 2064392 | tf_op jit(solution)/shard_map/ppermute | solution.py:30
  87.8 73.1 %collective-permute-start.6 = (f32[16,84,128]{2,0,1:T(8,128)S(1)}, f32[16,84,128]{2,0,1:T(8,128)S(1)}, u32[]{:S(2)}, u32[]{:S(2)}) collective-permute-start(f32[16,84,128]{2,0,1:T(8,128)S(1)} %constant_dynamic-update-slice_fusion.10), channel_id=1, source_target_pairs={{8,0},{16,8},{24,16},{32,24},{40,32},{48,40},{56,48},{64,56},{72,6... | collective-permute-start | bytes 2064392 | tf_op jit(solution)/shard_map/ppermute | solution.py:30
  93.3 5.8 %copy-start.6 = (f32[8,1,8,16,128]{4,2,3,0,1:T(8,128)S(1)}, f32[8,1,8,16,128]{4,2,3,0,1:T(8,128)}, u32[]{:S(2)}) copy-start(f32[8,1,8,16,128]{4,2,3,0,1:T(8,128)} %get-tuple-element.18) | copy-start | bytes 1572868
  93.3 69.6 %collective-permute-start.7 = (f32[16,84,128]{2,0,1:T(8,128)S(1)}, f32[16,84,128]{2,0,1:T(8,128)S(1)}, u32[]{:S(2)}, u32[]{:S(2)}) collective-permute-start(f32[16,84,128]{2,0,1:T(8,128)S(1)} %constant_dynamic-update-slice_fusion.15), channel_id=1, source_target_pairs={{16,0},{24,8},{32,16},{40,24},{48,32},{56,40},{64,48},{72,56},{80,... | collective-permute-start | bytes 2064392 | tf_op jit(solution)/shard_map/ppermute | solution.py:30
  122.8 75.1 %collective-permute-start.12 = (f32[16,84,128]{2,0,1:T(8,128)}, f32[16,84,128]{2,0,1:T(8,128)}, u32[]{:S(2)}, u32[]{:S(2)}) collective-permute-start(f32[16,84,128]{2,0,1:T(8,128)} %constant_dynamic-update-slice_fusion.52), channel_id=1, source_target_pairs={{16,0},{24,8},{32,16},{40,24},{48,32},{56,40},{64,48},{72,56},{80,... | collective-permute-start | bytes 2064392 | tf_op jit(solution)/shard_map/ppermute | solution.py:30
  125.5 74.4 %collective-permute-start.11 = (f32[16,84,128]{2,0,1:T(8,128)}, f32[16,84,128]{2,0,1:T(8,128)}, u32[]{:S(2)}, u32[]{:S(2)}) collective-permute-start(f32[16,84,128]{2,0,1:T(8,128)} %constant_dynamic-update-slice_fusion.47), channel_id=1, source_target_pairs={{8,0},{16,8},{24,16},{32,24},{40,32},{48,40},{56,48},{64,56},{72,6... | collective-permute-start | bytes 2064392 | tf_op jit(solution)/shard_map/ppermute | solution.py:30
  143.3 58.4 %collective-permute-start.10 = (f32[16,84,128]{2,0,1:T(8,128)}, f32[16,84,128]{2,0,1:T(8,128)}, u32[]{:S(2)}, u32[]{:S(2)}) collective-permute-start(f32[16,84,128]{2,0,1:T(8,128)} %constant_dynamic-update-slice_fusion.42), channel_id=1, source_target_pairs={{0,8},{8,16},{16,24},{24,32},{32,40},{40,48},{48,56},{56,64},{64,7... | collective-permute-start | bytes 2064392 | tf_op jit(solution)/shard_map/ppermute | solution.py:30
  160.9 42.9 %collective-permute-start.9 = (f32[16,84,128]{2,0,1:T(8,128)}, f32[16,84,128]{2,0,1:T(8,128)}, u32[]{:S(2)}, u32[]{:S(2)}) collective-permute-start(f32[16,84,128]{2,0,1:T(8,128)} %constant_dynamic-update-slice_fusion.37), channel_id=1, source_target_pairs={{0,16},{8,24},{16,32},{24,40},{32,48},{40,56},{48,64},{56,72},{64,... | collective-permute-start | bytes 2064392 | tf_op jit(solution)/shard_map/ppermute | solution.py:30
  162.9 1.8 copy-start.10
  172.0 2.2 copy-start.8
  190.1 1.0 copy-start.2
  191.7 6.2 %collective-permute-start.8 = (f32[1,5,8,128]{3,2,1,0:T(8,128)S(1)}, f32[1,5,8,128]{3,2,1,0:T(8,128)S(1)}, u32[]{:S(2)}, u32[]{:S(2)}) collective-permute-start(f32[1,5,8,128]{3,2,1,0:T(8,128)S(1)} %maximum_bitcast_fusion.3), channel_id=1, source_target_pairs={{0,8},{8,16},{16,24},{24,32},{32,40},{40,48},{48,56},{56,64},{64,7... | collective-permute-start | bytes 61448 | tf_op jit(solution)/shard_map/ppermute | solution.py:252
  202.8 2.9 %copy-start.1 = (f32[32,132,128]{2,0,1:T(8,128)S(1)}, f32[32,132,128]{2,0,1:T(8,128)}, u32[]{:S(2)}) copy-start(f32[32,132,128]{2,0,1:T(8,128)} %copy-done) | copy-start | bytes 6488068
  206.0 1.9 copy-start.11
  208.7 7.9 %collective-permute-start.13 = (f32[2,5,8,128]{3,2,1,0:T(8,128)S(1)}, f32[2,5,8,128]{3,2,1,0:T(8,128)S(1)}, u32[]{:S(2)}, u32[]{:S(2)}) collective-permute-start(f32[2,5,8,128]{3,2,1,0:T(8,128)S(1)} %pad_maximum_fusion.4), channel_id=1, source_target_pairs={{0,16},{8,24},{16,32},{24,40},{32,48},{40,56},{48,64},{56,72},{64,... | collective-permute-start | bytes 122888 | tf_op jit(solution)/shard_map/ppermute | solution.py:252
  212.5 4.1 %copy-start.9 = (f32[8,16,20,128]{3,1,2,0:T(8,128)}, f32[8,16,20,128]{3,1,2,0:T(8,128)S(1)}, u32[]{:S(2)}) copy-start(f32[8,16,20,128]{3,1,2,0:T(8,128)S(1)} %constant_dynamic-update-slice_fusion.75) | copy-start | bytes 3932164
  216.6 5.1 %collective-permute-start.14 = (f32[4,5,8,128]{3,2,1,0:T(8,128)S(1)}, f32[4,5,8,128]{3,2,1,0:T(8,128)S(1)}, u32[]{:S(2)}, u32[]{:S(2)}) collective-permute-start(f32[4,5,8,128]{3,2,1,0:T(8,128)S(1)} %pad_maximum_fusion.3), channel_id=1, source_target_pairs={{0,32},{8,40},{16,48},{24,56},{32,64},{40,72},{48,80},{56,88},{64,... | collective-permute-start | bytes 245768 | tf_op jit(solution)/shard_map/ppermute | solution.py:252
  222.4 16.1 %collective-permute-start.15 = (f32[8,5,8,128]{3,2,1,0:T(8,128)}, f32[8,5,8,128]{3,2,1,0:T(8,128)S(1)}, u32[]{:S(2)}, u32[]{:S(2)}) collective-permute-start(f32[8,5,8,128]{3,2,1,0:T(8,128)} %pad_maximum_fusion.2), channel_id=1, source_target_pairs={{0,64},{8,72},{16,80},{24,88},{32,96},{40,104},{48,112},{56,120},{... | collective-permute-start | bytes 491528 | tf_op jit(solution)/shard_map/ppermute | solution.py:252
  238.5 15.3 %collective-permute-start.16 = (f32[16,5,8,128]{3,2,1,0:T(8,128)S(1)}, f32[16,5,8,128]{3,2,1,0:T(8,128)S(1)}, u32[]{:S(2)}, u32[]{:S(2)}) collective-permute-start(f32[16,5,8,128]{3,2,1,0:T(8,128)S(1)} %pad_maximum_fusion.1), channel_id=1, source_target_pairs={{0,128},{8,136},{16,144},{24,152},{32,160},{40,168},{48,176},{56,1... | collective-permute-start | bytes 983048 | tf_op jit(solution)/shard_map/ppermute | solution.py:252
  239.2 17.9 %copy-start.3 = (f32[8,2,128,128]{2,3,1,0:T(8,128)S(1)}, f32[8,2,128,128]{2,3,1,0:T(8,128)}, u32[]{:S(2)}) copy-start(f32[8,2,128,128]{2,3,1,0:T(8,128)} %copy-done.2) | copy-start | bytes 3145732
  239.2 17.9 %copy-start.14 = (f32[8,128]{0,1:T(8,128)S(1)}, f32[8,128]{0,1:T(8,128)}, u32[]{:S(2)}) copy-start(f32[8,128]{0,1:T(8,128)} %copy.57) | copy-start | bytes 12292
  239.2 17.9 %copy-start.15 = (f32[8,128]{0,1:T(8,128)S(1)}, f32[8,128]{0,1:T(8,128)}, u32[]{:S(2)}) copy-start(f32[8,128]{0,1:T(8,128)} %copy.59) | copy-start | bytes 12292

commit v6 on v0

--- a/solution.py
+++ b/solution.py
@@ -59,10 +59,10 @@
     return running_total
 
 
-def _solve_body(pos_ref, packed_ref, left_ref, right_ref, alpha_s, beta_s, p_s, q_s, f_s):
+def _solve_body(pos_ref, packed_ref, solve_ref, lspike_ref, rspike_ref, out_ref, alpha_s, beta_s, p_s, q_s, f_s):
     count = packed_ref.shape[0]
-    width = left_ref.shape[0]
-    levels, lanes = left_ref.shape[1], left_ref.shape[2]
+    width, levels = out_ref.shape[0], out_ref.shape[1]
+    lanes = out_ref.shape[3]
     p = jnp.zeros((width, levels, lanes), jnp.float32)
     q = jnp.zeros((levels, lanes), jnp.float32)
     for j in range(count):
@@ -88,18 +88,25 @@
         ahead = alpha_s[j] + beta_s[j] * ahead
         f_s[j] = ahead
     pos = pos_ref[0]
-    left_ref[...] = p_s[pos] + q_s[pos] * f_s[pos]
-    right_ref[...] = f_s[pos + 1]
-
-def interface_solve(packed_all, position, width):
+    left = p_s[pos] + q_s[pos] * f_s[pos]
+    right = f_s[pos + 1]
+    for w in range(width):
+        for level in range(levels):
+            out_ref[w, level] = (
+                solve_ref[w, level]
+                - lspike_ref[level] * left[w, level : level + 1, :]
+                - rspike_ref[level] * right[w, level : level + 1, :]
+            )
+
+def interface_update(packed_all, position, local_solve, left_spike, right_spike):
     count, _, levels, lanes = packed_all.shape
-    out = jax.ShapeDtypeStruct((width, levels, lanes), jnp.float32)
+    width = local_solve.shape[0]
     vmem = pltpu.VMEM
     return pl.pallas_call(
         _solve_body,
-        out_shape=(out, out),
-        in_specs=[pl.BlockSpec(memory_space=pltpu.SMEM), pl.BlockSpec(memory_space=vmem)],
-        out_specs=(pl.BlockSpec(memory_space=vmem), pl.BlockSpec(memory_space=vmem)),
+        out_shape=jax.ShapeDtypeStruct(local_solve.shape, jnp.float32),
+        in_specs=[pl.BlockSpec(memory_space=pltpu.SMEM)] + [pl.BlockSpec(memory_space=vmem)] * 4,
+        out_specs=pl.BlockSpec(memory_space=vmem),
         scratch_shapes=[
             pltpu.VMEM((count, width, levels, lanes), jnp.float32),
             pltpu.VMEM((count, levels, lanes), jnp.float32),
@@ -107,7 +114,13 @@
             pltpu.VMEM((count, levels, lanes), jnp.float32),
             pltpu.VMEM((count + 1, width, levels, lanes), jnp.float32),
         ],
-    )(jnp.reshape(position, (1,)).astype(jnp.int32), packed_all)
+    )(
+        jnp.reshape(position, (1,)).astype(jnp.int32),
+        packed_all,
+        local_solve,
+        left_spike[:, :, None],
+        right_spike[:, :, None],
+    )
 
 
 def halo_x(block, axis, width):
@@ -255,12 +268,7 @@
     reverse = held[::-1]
     doubled = jnp.concatenate([reverse, reverse], axis=0)
     packed_all = lax.dynamic_slice_in_dim(doubled, count - 1 - position, count, 0)
-    left_value, right_value = interface_solve(packed_all, position, first_row.shape[0])
-    wind_fields = (
-        local_solve
-        - left_spike[None, :, :, None] * left_value[:, :, None, :]
-        - right_spike[None, :, :, None] * right_value[:, :, None, :]
-    )
+    wind_fields = interface_update(packed_all, position, local_solve, left_spike, right_spike)
     tracer_windows = assemble_windows(
         tracer_main, tracer_halo, *tracer_received, offsets, position, block_count
     )

time: 257 us -> 254 us (0.988)
  local copies, waits for them, and re-layouts: 58 us -> 52.8 us
  waiting for transfers between devices: 52.3 us -> 56.3 us
    ppermute x5, waiting for transfers between devices: 31.9 us -> 35.5 us  [local(): held = jnp.concatenate([held, lax.ppermute(held, 'gx', ring)], axis=0)]
    unnamed x94 -> x85, local copies, waits for them, and re-layouts: 26.5 us -> 23.6 us
  transfers between devices with their start and end apart: 17 -> 17, of which waited for: 6 -> 6; matrix products, arithmetic and copies ran while one was open for 30% -> 29% of each run, Pallas kernels for 0% -> 0%
where the time goes in v6:
time: 254 us; the launch traced here: 252 us
  waiting for transfers between devices  56.3 us (22%)
  local copies, waits for them, and re-layouts  52.8 us (21%)
  starting transfers between devices  50.4 us (20%)
  between operations  45.9 us (18%)
  other arithmetic  40.4 us (16%)
  Pallas kernels  3.56 us (1%)
  matrix products  2.71 us (1%)
    ppermute x5, waiting for transfers between devices, local(): held = jnp.concatenate([held, lax.ppermute(held, 'gx', ring)], axis=0)  35.5 us
    ppermute x8, starting transfers between devices, shifted_2(): lax.ppermute(value, axis, [(source, source + steps) for source in range(l...  25.7 us
    unnamed x85, local copies, waits for them, and re-layouts  23.6 us
    ppermute x8, waiting for transfers between devices, shifted_2(): lax.ppermute(value, axis, [(source, source + steps) for source in range(l...  20.7 us
    add x2, other arithmetic, interpolate(): running_total + tap_term  15.9 us
    ppermute x5, starting transfers between devices, local(): held = jnp.concatenate([held, lax.ppermute(held, 'gx', ring)], axis=0)  11.2 us
    reshape x2, other arithmetic, advect_group(): windows.reshape(block_count, field_count, level_count, BX + 4, rows_here...  6.42 us
    slice x2, local copies, waits for them, and re-layouts, halo_y(): low = lax.ppermute(block[:, :, block.shape[2] - width:], axis, forward)  5.99 us
  transfers between devices with their start and end apart: 17, of which 6 were waited for; matrix products, arithmetic and copies ran while one was open for 29% of the time, Pallas kernels for 0%

profile of v6, /device:TPU:34, one launch (start us, length us, event | category | flops | bytes accessed | tf_op | source)
XLA Modules:
  0.0 252.0 jit_solution(517391883964888012)
XLA Ops:
  0.7 2.9 %copy.67 = f32[4,8,128,128]{3,1,0,2:T(8,128)S(1)} copy(f32[4,8,128,128]{3,2,1,0:T(8,128)} %param.7) | data formatting | bytes 4194304 | tf_op args[0]
  3.6 1.3 copy-done.2
  4.9 3.5 %collective-permute-start = (f32[32,2,128]{2,0,1:T(8,128)S(1)}, f32[32,2,128]{2,0,1:T(8,128)S(1)}, u32[]{:S(2)}, u32[]{:S(2)}) collective-permute-start(f32[32,2,128]{2,0,1:T(8,128)S(1)} %get-tuple-element.48), channel_id=1, source_target_pairs={{0,8},{8,16},{16,24},{24,32},{32,40},{40,48},{48,56},{56,64},{64,7... | collective-permute-start | bytes 98312 | tf_op jit(solution)/shard_map/ppermute | solution.py:130
  8.4 4.5 %collective-permute-start.1 = (f32[32,2,128]{2,0,1:T(8,128)S(1)}, f32[32,2,128]{2,0,1:T(8,128)S(1)}, u32[]{:S(2)}, u32[]{:S(2)}) collective-permute-start(f32[32,2,128]{2,0,1:T(8,128)S(1)} %get-tuple-element.49), channel_id=1, source_target_pairs={{8,0},{16,8},{24,16},{32,24},{40,32},{48,40},{56,48},{64,56},{72,6... | collective-permute-start | bytes 98312 | tf_op jit(solution)/shard_map/ppermute | solution.py:131
  14.7 1.2 slice_multiply_fusion.50
  16.1 3.9 %fusion.63 = (f32[8,8,16,128]{3,1,2,0:T(8,128)}, f32[8,8,16,128]{3,1,2,0:T(8,128)}, f32[8,8,16,128]{3,1,2,0:T(8,128)}, f32[8,8,16,128]{3,1,2,0:T(8,128)}, f32[8,...) fusion(f32[8,8,16,128]{3,2,1,0:T(8,128)S(1)} %bitcast.362, ...), kind=kLoop, calls=%fused_computation.132 | loop fusion | flops 9175040 | bytes 6291456 | tf_op jit(solution)/shard_map/mul | solution.py:40
  20.1 0.8 fusion.100
  20.9 0.8 fusion.108
  51.7 1.8 pad_maximum_fusion
  53.5 2.8 %fusion.115 = (f32[32,132,2]{2,0,1:T(8,128)}, f32[32,132,2]{2,0,1:T(8,128)}) fusion(f32[32,132,128]{2,0,1:T(8,128)S(1)} %pad_maximum_fusion), kind=kLoop, calls=%fused_computation.408 | loop fusion | bytes 135168 | tf_op jit(solution)/shard_map/slice | solution.py:139
  56.4 3.2 %copy.40 = f32[32,132,2]{1,0,2:T(8,128)S(1)} copy(f32[32,132,2]{2,0,1:T(8,128)} %get-tuple-element.46) | data formatting | bytes 67584 | tf_op jit(solution)/shard_map/slice | solution.py:139
  59.6 1.9 collective-permute-start.2
  61.5 3.2 %copy.41 = f32[32,132,2]{1,0,2:T(8,128)S(1)} copy(f32[32,132,2]{2,0,1:T(8,128)} %get-tuple-element.47) | data formatting | bytes 67584 | tf_op jit(solution)/shard_map/slice | solution.py:140
  64.7 3.6 %collective-permute-start.3 = (f32[32,132,2]{1,0,2:T(8,128)S(1)}, f32[32,132,2]{1,0,2:T(8,128)S(1)}, u32[]{:S(2)}, u32[]{:S(2)}) collective-permute-start(f32[32,132,2]{1,0,2:T(8,128)S(1)} %copy.41), channel_id=1, source_target_pairs={{1,0},{2,1},{3,2},{4,3},{5,4},{6,5},{7,6},{9,8},{10,9},{11,10},{12... | collective-permute-start | bytes 101384 | tf_op jit(solution)/shard_map/ppermute | solution.py:140
  71.6 0.9 constant_dynamic-update-slice_fusion
  72.5 3.0 %collective-permute-start.4 = (f32[16,84,128]{2,0,1:T(8,128)}, f32[16,84,128]{2,0,1:T(8,128)S(1)}, u32[]{:S(2)}, u32[]{:S(2)}) collective-permute-start(f32[16,84,128]{2,0,1:T(8,128)} %constant_dynamic-update-slice_fusion), channel_id=1, source_target_pairs={{0,16},{8,24},{16,32},{24,40},{32,48},{40,56},{48,64},{56,72},{64,... | collective-permute-start | bytes 2064392 | tf_op jit(solution)/shard_map/ppermute | solution.py:30
  91.5 2.6 %collective-permute-start.5 = (f32[16,84,128]{2,0,1:T(8,128)}, f32[16,84,128]{2,0,1:T(8,128)S(1)}, u32[]{:S(2)}, u32[]{:S(2)}) collective-permute-start(f32[16,84,128]{2,0,1:T(8,128)} %constant_dynamic-update-slice_fusion.5), channel_id=1, source_target_pairs={{0,8},{8,16},{16,24},{24,32},{32,40},{40,48},{48,56},{56,64},{64,7... | collective-permute-start | bytes 2064392 | tf_op jit(solution)/shard_map/ppermute | solution.py:30
  94.9 5.4 %collective-permute-start.6 = (f32[16,84,128]{2,0,1:T(8,128)}, f32[16,84,128]{2,0,1:T(8,128)S(1)}, u32[]{:S(2)}, u32[]{:S(2)}) collective-permute-start(f32[16,84,128]{2,0,1:T(8,128)} %constant_dynamic-update-slice_fusion.10), channel_id=1, source_target_pairs={{8,0},{16,8},{24,16},{32,24},{40,32},{48,40},{56,48},{64,56},{72,6... | collective-permute-start | bytes 2064392 | tf_op jit(solution)/shard_map/ppermute | solution.py:30
  100.9 3.3 %collective-permute-start.7 = (f32[16,84,128]{2,0,1:T(8,128)}, f32[16,84,128]{2,0,1:T(8,128)S(1)}, u32[]{:S(2)}, u32[]{:S(2)}) collective-permute-start(f32[16,84,128]{2,0,1:T(8,128)} %constant_dynamic-update-slice_fusion.15), channel_id=1, source_target_pairs={{16,0},{24,8},{32,16},{40,24},{48,32},{56,40},{64,48},{72,56},{80,... | collective-permute-start | bytes 2064392 | tf_op jit(solution)/shard_map/ppermute | solution.py:30
  104.6 8.9 %collective-permute-done.5 = f32[16,84,128]{2,0,1:T(8,128)S(1)} collective-permute-done((f32[16,84,128]{2,0,1:T(8,128)}, f32[16,84,128]{2,0,1:T(8,128)S(1)}, u32[]{:S(2)}, u32[]{:S(2)}) %collective-permute-start.5) | collective-permute-done | bytes 688160 | tf_op jit(solution)/shard_map/ppermute | solution.py:30
  113.7 0.9 constant_dynamic-update-slice_fusion.56
  114.6 0.8 constant_dynamic-update-slice_fusion.55
  115.4 0.8 constant_dynamic-update-slice_fusion.54
  116.3 0.8 constant_dynamic-update-slice_fusion.53
  117.8 2.8 %collective-permute-start.12 = (f32[16,84,128]{2,0,1:T(8,128)}, f32[16,84,128]{2,0,1:T(8,128)}, u32[]{:S(2)}, u32[]{:S(2)}) collective-permute-start(f32[16,84,128]{2,0,1:T(8,128)} %constant_dynamic-update-slice_fusion.52), channel_id=1, source_target_pairs={{16,0},{24,8},{32,16},{40,24},{48,32},{56,40},{64,48},{72,56},{80,... | collective-permute-start | bytes 2064392 | tf_op jit(solution)/shard_map/ppermute | solution.py:30
  121.3 2.2 collective-permute-start.11
  124.2 3.7 %collective-permute-start.10 = (f32[16,84,128]{2,0,1:T(8,128)}, f32[16,84,128]{2,0,1:T(8,128)}, u32[]{:S(2)}, u32[]{:S(2)}) collective-permute-start(f32[16,84,128]{2,0,1:T(8,128)} %constant_dynamic-update-slice_fusion.42), channel_id=1, source_target_pairs={{0,8},{8,16},{16,24},{24,32},{32,40},{40,48},{48,56},{56,64},{64,7... | collective-permute-start | bytes 2064392 | tf_op jit(solution)/shard_map/ppermute | solution.py:30
  128.6 1.7 collective-permute-done.6
  130.3 2.8 %collective-permute-start.9 = (f32[16,84,128]{2,0,1:T(8,128)}, f32[16,84,128]{2,0,1:T(8,128)}, u32[]{:S(2)}, u32[]{:S(2)}) collective-permute-start(f32[16,84,128]{2,0,1:T(8,128)} %constant_dynamic-update-slice_fusion.37), channel_id=1, source_target_pairs={{0,16},{8,24},{16,32},{24,40},{32,48},{40,56},{48,64},{56,72},{64,... | collective-permute-start | bytes 2064392 | tf_op jit(solution)/shard_map/ppermute | solution.py:30
  133.1 10.1 %collective-permute-done.7 = f32[16,84,128]{2,0,1:T(8,128)S(1)} collective-permute-done((f32[16,84,128]{2,0,1:T(8,128)}, f32[16,84,128]{2,0,1:T(8,128)S(1)}, u32[]{:S(2)}, u32[]{:S(2)}) %collective-permute-start.7) | collective-permute-done | bytes 688160 | tf_op jit(solution)/shard_map/ppermute | solution.py:30
  143.3 1.7 copy-done.8
  145.3 0.9 constant_dynamic-update-slice_fusion.35
  146.3 0.9 constant_dynamic-update-slice_fusion.34
  147.3 0.9 constant_dynamic-update-slice_fusion.33
  148.3 0.9 constant_dynamic-update-slice_fusion.32
  149.3 0.9 constant_dynamic-update-slice_fusion.31
  150.4 0.9 constant_dynamic-update-slice_fusion.30
  151.4 0.9 constant_dynamic-update-slice_fusion.29
  152.4 2.0 copy.42
  154.5 2.0 copy.43
  156.5 3.2 %maximum_bitcast_fusion = f32[8,2,8,20,132]{4,2,1,3,0:T(8,128)S(1)} fusion(f32[8,16,20,2]{3,1,2,0:T(8,128)} %copy.43, f32[8,16,20,128]{3,1,2,0:T(8,128)} %copy-done.6, f32[8,16,20,2]{3,1,2,0:T(8,128)} %copy.42), kind=kLoop, calls=%fused_computation | loop fusion | flops 675840 | bytes 2703360 | tf_op jit(solution)/shard_map/reshape | solution.py:219
  159.7 8.0 %fusion.31 = f32[8,2,8,16,128]{4,2,1,3,0:T(8,128)} fusion(f32[8,2,8,20,132]{4,2,1,3,0:T(8,128)S(1)} %maximum_bitcast_fusion, f32[8,8,16,128]{3,1,2,0:T(8,128)} %get-tuple-element.177, f32[8,8,16,128]{3,1,2,0:T(8,128)} %get-tuple-element.176, f32[8,8,16,128]{3,1,2,0:T(8,128)} %get-tuple-element.174, f32[8,8,16,128]{3,1,2,0:T(8,128)} %get-tuple-element.175, ...), kind=kLoop, calls=%fused_computation.64 | loop fusion | flops 14155776 | bytes 32505856 | tf_op jit(solution)/shard_map/add | solution.py:58
  167.7 2.7 %convolution_bitcast_fusion.solve_ref = f32[2,8,128,128]{3,2,1,0:T(8,128)S(1)} fusion(f32[2,8,128,128]{3,1,0,2:T(8,128)} %bitcast.360, f32[8,128,128]{2,1,0:T(8,128)} %param.11), kind=kOutput, calls=%fused_computation.4 | convolution fusion | flops 402653184 | bytes 2621440 | tf_op jit(solution)/shard_map/lij,wljy->wliy/dot_general | solution.py:247
  170.5 15.8 %collective-permute-done.8 = f32[1,5,8,128]{3,2,1,0:T(8,128)S(1)} collective-permute-done((f32[1,5,8,128]{3,2,1,0:T(8,128)S(1)}, f32[1,5,8,128]{3,2,1,0:T(8,128)S(1)}, u32[]{:S(2)}, u32[]{:S(2)}) %collective-permute-start.8) | collective-permute-done | bytes 20512 | tf_op jit(solution)/shard_map/ppermute | solution.py:264
  186.4 1.1 slice.448
  187.5 0.8 slice.452
  188.3 1.1 slice.447
  190.2 1.1 slice.446
  191.3 0.9 slice.450
  192.3 1.1 slice.445
  193.4 0.8 slice.449
  194.7 1.6 copy-done.9
  197.1 4.1 %collective-permute-start.13 = (f32[2,5,8,128]{3,2,1,0:T(8,128)S(1)}, f32[2,5,8,128]{3,2,1,0:T(8,128)S(1)}, u32[]{:S(2)}, u32[]{:S(2)}) collective-permute-start(f32[2,5,8,128]{3,2,1,0:T(8,128)S(1)} %pad_maximum_fusion.4), channel_id=1, source_target_pairs={{0,16},{8,24},{16,32},{24,40},{32,48},{40,56},{48,64},{56,72},{64,... | collective-permute-start | bytes 122888 | tf_op jit(solution)/shard_map/ppermute | solution.py:264
  201.2 0.9 constant_dynamic-update-slice_fusion.75
  202.2 2.0 copy.47
  204.2 2.0 copy.48
  206.2 0.8 collective-permute-start.14
  207.0 3.2 %maximum_bitcast_fusion.1 = f32[8,2,8,20,132]{4,2,1,3,0:T(8,128)S(1)} fusion(f32[8,16,20,2]{3,1,2,0:T(8,128)} %copy.48, f32[8,16,20,128]{3,1,2,0:T(8,128)} %copy-done.7, f32[8,16,20,2]{3,1,2,0:T(8,128)} %copy.47), kind=kLoop, calls=%fused_computation.1 | loop fusion | flops 675840 | bytes 2703360 | tf_op jit(solution)/shard_map/reshape | solution.py:219
  211.4 6.0 %collective-permute-start.15 = (f32[8,5,8,128]{3,2,1,0:T(8,128)}, f32[8,5,8,128]{3,2,1,0:T(8,128)S(1)}, u32[]{:S(2)}, u32[]{:S(2)}) collective-permute-start(f32[8,5,8,128]{3,2,1,0:T(8,128)} %pad_maximum_fusion.2), channel_id=1, source_target_pairs={{0,64},{8,72},{16,80},{24,88},{32,96},{40,104},{48,112},{56,120},{... | collective-permute-start | bytes 491528 | tf_op jit(solution)/shard_map/ppermute | solution.py:264
  217.5 8.0 %fusion.2 = f32[8,2,8,16,128]{4,2,1,3,0:T(8,128)} fusion(f32[8,2,8,20,132]{4,2,1,3,0:T(8,128)S(1)} %maximum_bitcast_fusion.1, f32[8,8,16,128]{3,1,2,0:T(8,128)} %get-tuple-element.177, f32[8,8,16,128]{3,1,2,0:T(8,128)} %get-tuple-element.176, f32[8,8,16,128]{3,1,2,0:T(8,128)} %get-tuple-element.174, f32[8,8,16,128]{3,1,2,0:T(8,128)} %get-tuple-element.175, ...), kind=kLoop, calls=%fused_computation.10 | loop fusion | flops 14155776 | bytes 32505856 | tf_op jit(solution)/shard_map/add | solution.py:58
  225.4 2.5 %copy.49 = f32[2,8,128,128]{3,2,1,0:T(8,128)} copy(f32[2,8,128,128]{3,1,0,2:T(8,128)} %bitcast.359) | data formatting | bytes 2097152
  228.3 19.1 %collective-permute-done.16 = f32[16,5,8,128]{3,2,1,0:T(8,128)S(1)} collective-permute-done((f32[16,5,8,128]{3,2,1,0:T(8,128)S(1)}, f32[16,5,8,128]{3,2,1,0:T(8,128)S(1)}, u32[]{:S(2)}, u32[]{:S(2)}) %collective-permute-start.16) | collective-permute-done | bytes 327712 | tf_op jit(solution)/shard_map/ppermute | solution.py:264
  247.5 1.0 fusion.59.packed_ref
  248.5 3.6 %shard_map.86 = f32[2,8,128,128]{3,2,1,0:T(8,128)} custom-call(s32[1]{0:T(128)} %bitcast.pos_ref, f32[32,5,8,128]{3,2,1,0:T(8,128)} %fusion.59.packed_ref, f32[2,8,128,128]{3,2,1,0:T(8,128)} %copy-done.5, f32[8,128,1]{2,1,0:T(8,128)} %get-tuple-element.85.lspike_ref, f32[8,128,1]{2,1,0:T(8,128)} %get-tuple-element.84.rspike_ref), custom_call_target="tpu_custom_call" | custom-call | tf_op jit(solution)/shard_map/pallas_call | solution.py:105
  (138 shorter events, 16.2 us)
Async XLA Ops:
  0.6 12.3 %copy-start.12 = (s32[256,1]{0,1:T(1,128)S(1)}, s32[256,1]{0,1:T(1,128)}, u32[]{:S(2)}) copy-start(s32[256,1]{0,1:T(1,128)} %param.10) | copy-start | bytes 3076
  0.6 13.9 %copy-start.10 = (f32[8,128,128]{2,1,0:T(8,128)S(1)}, f32[8,128,128]{2,1,0:T(8,128)}, u32[]{:S(2)}) copy-start(f32[8,128,128]{2,1,0:T(8,128)} %param.8) | copy-start | bytes 1572868
  0.7 14.0 %copy-start.11 = (f32[8,128,128]{2,1,0:T(8,128)S(1)}, f32[8,128,128]{2,1,0:T(8,128)}, u32[]{:S(2)}) copy-start(f32[8,128,128]{2,1,0:T(8,128)} %param.9) | copy-start | bytes 1572868
  3.6 1.4 copy-start.2
  3.6 11.1 %copy-start.4 = (f32[8,128,128]{2,1,0:T(8,128)S(1)}, f32[8,128,128]{2,1,0:T(8,128)}, u32[]{:S(2)}) copy-start(f32[8,128,128]{2,1,0:T(8,128)} %param.11) | copy-start | bytes 1572868
  3.6 11.1 %copy-start.16 = (f32[8,1]{0,1:T(1,128)S(1)}, f32[8,1]{0,1:T(1,128)}, u32[]{:S(2)}) copy-start(f32[8,1]{0,1:T(1,128)} %param.13) | copy-start | bytes 100
  3.6 11.1 %copy-start.17 = (f32[8,1]{0,1:T(1,128)S(1)}, f32[8,1]{0,1:T(1,128)}, u32[]{:S(2)}) copy-start(f32[8,1]{0,1:T(1,128)} %param.12) | copy-start | bytes 100
  4.9 46.8 %collective-permute-start = (f32[32,2,128]{2,0,1:T(8,128)S(1)}, f32[32,2,128]{2,0,1:T(8,128)S(1)}, u32[]{:S(2)}, u32[]{:S(2)}) collective-permute-start(f32[32,2,128]{2,0,1:T(8,128)S(1)} %get-tuple-element.48), channel_id=1, source_target_pairs={{0,8},{8,16},{16,24},{24,32},{32,40},{40,48},{48,56},{56,64},{64,7... | collective-permute-start | bytes 98312 | tf_op jit(solution)/shard_map/ppermute | solution.py:130
  8.4 43.3 %collective-permute-start.1 = (f32[32,2,128]{2,0,1:T(8,128)S(1)}, f32[32,2,128]{2,0,1:T(8,128)S(1)}, u32[]{:S(2)}, u32[]{:S(2)}) collective-permute-start(f32[32,2,128]{2,0,1:T(8,128)S(1)} %get-tuple-element.49), channel_id=1, source_target_pairs={{8,0},{16,8},{24,16},{32,24},{40,32},{48,40},{56,48},{64,56},{72,6... | collective-permute-start | bytes 98312 | tf_op jit(solution)/shard_map/ppermute | solution.py:131
  53.5 60.1 %copy-start = (f32[32,132,128]{2,0,1:T(8,128)}, f32[32,132,128]{2,0,1:T(8,128)S(1)}, u32[]{:S(2)}) copy-start(f32[32,132,128]{2,0,1:T(8,128)S(1)} %pad_maximum_fusion) | copy-start | bytes 6488068
  59.6 11.7 %collective-permute-start.2 = (f32[32,132,2]{1,0,2:T(8,128)S(1)}, f32[32,132,2]{1,0,2:T(8,128)S(1)}, u32[]{:S(2)}, u32[]{:S(2)}) collective-permute-start(f32[32,132,2]{1,0,2:T(8,128)S(1)} %copy.40), channel_id=1, source_target_pairs={{0,1},{1,2},{2,3},{3,4},{4,5},{5,6},{6,7},{8,9},{9,10},{10,11},{11... | collective-permute-start | bytes 101384 | tf_op jit(solution)/shard_map/ppermute | solution.py:139
  64.7 6.5 %collective-permute-start.3 = (f32[32,132,2]{1,0,2:T(8,128)S(1)}, f32[32,132,2]{1,0,2:T(8,128)S(1)}, u32[]{:S(2)}, u32[]{:S(2)}) collective-permute-start(f32[32,132,2]{1,0,2:T(8,128)S(1)} %copy.41), channel_id=1, source_target_pairs={{1,0},{2,1},{3,2},{4,3},{5,4},{6,5},{7,6},{9,8},{10,9},{11,10},{12... | collective-permute-start | bytes 101384 | tf_op jit(solution)/shard_map/ppermute | solution.py:140
  71.3 5.0 %copy-start.13 = (f32[16,84,128]{2,0,1:T(8,128)}, f32[16,84,128]{2,0,1:T(8,128)S(1)}, u32[]{:S(2)}) copy-start(f32[16,84,128]{2,0,1:T(8,128)S(1)} %get-tuple-element.66) | copy-start | bytes 2064388
  71.3 5.0 %copy-start.14 = (f32[16,84,128]{2,0,1:T(8,128)}, f32[16,84,128]{2,0,1:T(8,128)S(1)}, u32[]{:S(2)}) copy-start(f32[16,84,128]{2,0,1:T(8,128)S(1)} %get-tuple-element.67) | copy-start | bytes 2064388
  71.3 5.0 %copy-start.15 = (f32[16,84,128]{2,0,1:T(8,128)}, f32[16,84,128]{2,0,1:T(8,128)S(1)}, u32[]{:S(2)}) copy-start(f32[16,84,128]{2,0,1:T(8,128)S(1)} %get-tuple-element.68) | copy-start | bytes 2064388
  72.5 32.0 %collective-permute-start.4 = (f32[16,84,128]{2,0,1:T(8,128)}, f32[16,84,128]{2,0,1:T(8,128)S(1)}, u32[]{:S(2)}, u32[]{:S(2)}) collective-permute-start(f32[16,84,128]{2,0,1:T(8,128)} %constant_dynamic-update-slice_fusion), channel_id=1, source_target_pairs={{0,16},{8,24},{16,32},{24,40},{32,48},{40,56},{48,64},{56,72},{64,... | collective-permute-start | bytes 2064392 | tf_op jit(solution)/shard_map/ppermute | solution.py:30
  91.5 22.0 %collective-permute-start.5 = (f32[16,84,128]{2,0,1:T(8,128)}, f32[16,84,128]{2,0,1:T(8,128)S(1)}, u32[]{:S(2)}, u32[]{:S(2)}) collective-permute-start(f32[16,84,128]{2,0,1:T(8,128)} %constant_dynamic-update-slice_fusion.5), channel_id=1, source_target_pairs={{0,8},{8,16},{16,24},{24,32},{32,40},{40,48},{48,56},{56,64},{64,7... | collective-permute-start | bytes 2064392 | tf_op jit(solution)/shard_map/ppermute | solution.py:30
  94.9 35.4 %collective-permute-start.6 = (f32[16,84,128]{2,0,1:T(8,128)}, f32[16,84,128]{2,0,1:T(8,128)S(1)}, u32[]{:S(2)}, u32[]{:S(2)}) collective-permute-start(f32[16,84,128]{2,0,1:T(8,128)} %constant_dynamic-update-slice_fusion.10), channel_id=1, source_target_pairs={{8,0},{16,8},{24,16},{32,24},{40,32},{48,40},{56,48},{64,56},{72,6... | collective-permute-start | bytes 2064392 | tf_op jit(solution)/shard_map/ppermute | solution.py:30
  100.9 42.3 %collective-permute-start.7 = (f32[16,84,128]{2,0,1:T(8,128)}, f32[16,84,128]{2,0,1:T(8,128)S(1)}, u32[]{:S(2)}, u32[]{:S(2)}) collective-permute-start(f32[16,84,128]{2,0,1:T(8,128)} %constant_dynamic-update-slice_fusion.15), channel_id=1, source_target_pairs={{16,0},{24,8},{32,16},{40,24},{48,32},{56,40},{64,48},{72,56},{80,... | collective-permute-start | bytes 2064392 | tf_op jit(solution)/shard_map/ppermute | solution.py:30
  117.8 68.6 %collective-permute-start.12 = (f32[16,84,128]{2,0,1:T(8,128)}, f32[16,84,128]{2,0,1:T(8,128)}, u32[]{:S(2)}, u32[]{:S(2)}) collective-permute-start(f32[16,84,128]{2,0,1:T(8,128)} %constant_dynamic-update-slice_fusion.52), channel_id=1, source_target_pairs={{16,0},{24,8},{32,16},{40,24},{48,32},{56,40},{64,48},{72,56},{80,... | collective-permute-start | bytes 2064392 | tf_op jit(solution)/shard_map/ppermute | solution.py:30
  121.3 67.0 %collective-permute-start.11 = (f32[16,84,128]{2,0,1:T(8,128)}, f32[16,84,128]{2,0,1:T(8,128)}, u32[]{:S(2)}, u32[]{:S(2)}) collective-permute-start(f32[16,84,128]{2,0,1:T(8,128)} %constant_dynamic-update-slice_fusion.47), channel_id=1, source_target_pairs={{8,0},{16,8},{24,16},{32,24},{40,32},{48,40},{56,48},{64,56},{72,6... | collective-permute-start | bytes 2064392 | tf_op jit(solution)/shard_map/ppermute | solution.py:30
  124.2 66.0 %collective-permute-start.10 = (f32[16,84,128]{2,0,1:T(8,128)}, f32[16,84,128]{2,0,1:T(8,128)}, u32[]{:S(2)}, u32[]{:S(2)}) collective-permute-start(f32[16,84,128]{2,0,1:T(8,128)} %constant_dynamic-update-slice_fusion.42), channel_id=1, source_target_pairs={{0,8},{8,16},{16,24},{24,32},{32,40},{40,48},{48,56},{56,64},{64,7... | collective-permute-start | bytes 2064392 | tf_op jit(solution)/shard_map/ppermute | solution.py:30
  130.3 62.0 %collective-permute-start.9 = (f32[16,84,128]{2,0,1:T(8,128)}, f32[16,84,128]{2,0,1:T(8,128)}, u32[]{:S(2)}, u32[]{:S(2)}) collective-permute-start(f32[16,84,128]{2,0,1:T(8,128)} %constant_dynamic-update-slice_fusion.37), channel_id=1, source_target_pairs={{0,16},{8,24},{16,32},{24,40},{32,48},{40,56},{48,64},{56,72},{64,... | collective-permute-start | bytes 2064392 | tf_op jit(solution)/shard_map/ppermute | solution.py:30
  143.3 1.8 copy-start.8
  152.3 2.1 copy-start.6
  156.5 3.2 %copy-start.3 = (f32[8,8,16,128]{3,1,2,0:T(8,128)S(1)}, f32[8,8,16,128]{3,1,2,0:T(8,128)}, u32[]{:S(2)}) copy-start(f32[8,8,16,128]{3,1,2,0:T(8,128)} %get-tuple-element.93) | copy-start | bytes 1572868
  170.4 20.9 %copy-start.5 = (f32[2,8,128,128]{3,2,1,0:T(8,128)}, f32[2,8,128,128]{3,2,1,0:T(8,128)S(1)}, u32[]{:S(2)}) copy-start(f32[2,8,128,128]{3,2,1,0:T(8,128)S(1)} %convolution_bitcast_fusion.solve_ref) | copy-start | bytes 3145732
  170.4 15.9 %collective-permute-start.8 = (f32[1,5,8,128]{3,2,1,0:T(8,128)S(1)}, f32[1,5,8,128]{3,2,1,0:T(8,128)S(1)}, u32[]{:S(2)}, u32[]{:S(2)}) collective-permute-start(f32[1,5,8,128]{3,2,1,0:T(8,128)S(1)} %maximum_bitcast_fusion.3), channel_id=1, source_target_pairs={{0,8},{8,16},{16,24},{24,32},{32,40},{40,48},{48,56},{56,64},{64,7... | collective-permute-start | bytes 61448 | tf_op jit(solution)/shard_map/ppermute | solution.py:264
  191.3 2.9 %copy-start.1 = (f32[32,132,128]{2,0,1:T(8,128)S(1)}, f32[32,132,128]{2,0,1:T(8,128)}, u32[]{:S(2)}) copy-start(f32[32,132,128]{2,0,1:T(8,128)} %copy-done) | copy-start | bytes 6488068
  194.5 1.8 copy-start.9
  197.1 9.1 %collective-permute-start.13 = (f32[2,5,8,128]{3,2,1,0:T(8,128)S(1)}, f32[2,5,8,128]{3,2,1,0:T(8,128)S(1)}, u32[]{:S(2)}, u32[]{:S(2)}) collective-permute-start(f32[2,5,8,128]{3,2,1,0:T(8,128)S(1)} %pad_maximum_fusion.4), channel_id=1, source_target_pairs={{0,16},{8,24},{16,32},{24,40},{32,48},{40,56},{48,64},{56,72},{64,... | collective-permute-start | bytes 122888 | tf_op jit(solution)/shard_map/ppermute | solution.py:264
  202.2 4.1 %copy-start.7 = (f32[8,16,20,128]{3,1,2,0:T(8,128)}, f32[8,16,20,128]{3,1,2,0:T(8,128)S(1)}, u32[]{:S(2)}) copy-start(f32[8,16,20,128]{3,1,2,0:T(8,128)S(1)} %constant_dynamic-update-slice_fusion.75) | copy-start | bytes 3932164
  206.2 4.5 %collective-permute-start.14 = (f32[4,5,8,128]{3,2,1,0:T(8,128)S(1)}, f32[4,5,8,128]{3,2,1,0:T(8,128)S(1)}, u32[]{:S(2)}, u32[]{:S(2)}) collective-permute-start(f32[4,5,8,128]{3,2,1,0:T(8,128)S(1)} %pad_maximum_fusion.3), channel_id=1, source_target_pairs={{0,32},{8,40},{16,48},{24,56},{32,64},{40,72},{48,80},{56,88},{64,... | collective-permute-start | bytes 245768 | tf_op jit(solution)/shard_map/ppermute | solution.py:264
  211.4 16.5 %collective-permute-start.15 = (f32[8,5,8,128]{3,2,1,0:T(8,128)}, f32[8,5,8,128]{3,2,1,0:T(8,128)S(1)}, u32[]{:S(2)}, u32[]{:S(2)}) collective-permute-start(f32[8,5,8,128]{3,2,1,0:T(8,128)} %pad_maximum_fusion.2), channel_id=1, source_target_pairs={{0,64},{8,72},{16,80},{24,88},{32,96},{40,104},{48,112},{56,120},{... | collective-permute-start | bytes 491528 | tf_op jit(solution)/shard_map/ppermute | solution.py:264
  228.0 19.4 %collective-permute-start.16 = (f32[16,5,8,128]{3,2,1,0:T(8,128)S(1)}, f32[16,5,8,128]{3,2,1,0:T(8,128)S(1)}, u32[]{:S(2)}, u32[]{:S(2)}) collective-permute-start(f32[16,5,8,128]{3,2,1,0:T(8,128)S(1)} %pad_maximum_fusion.1), channel_id=1, source_target_pairs={{0,128},{8,136},{16,144},{24,152},{32,160},{40,168},{48,176},{56,1... | collective-permute-start | bytes 983048 | tf_op jit(solution)/shard_map/ppermute | solution.py:264

commit v7 on v6

--- a/solution.py
+++ b/solution.py
@@ -65,10 +65,12 @@
     lanes = out_ref.shape[3]
     p = jnp.zeros((width, levels, lanes), jnp.float32)
     q = jnp.zeros((levels, lanes), jnp.float32)
+    pos = pos_ref[0]
     for j in range(count):
-        first = packed_ref[j, 0:width]
-        last = packed_ref[j, width : 2 * width]
-        coef = packed_ref[j, 2 * width]
+        held_at = (pos - j + count) % count
+        first = packed_ref[held_at, 0:width]
+        last = packed_ref[held_at, width : 2 * width]
+        coef = packed_ref[held_at, 2 * width]
         lead_left = jnp.broadcast_to(coef[:, 0:1], (levels, lanes))
         tail_left = jnp.broadcast_to(coef[:, 1:2], (levels, lanes))
         lead_right = jnp.broadcast_to(coef[:, 2:3], (levels, lanes))
@@ -87,7 +89,6 @@
     for j in range(count - 1, -1, -1):
         ahead = alpha_s[j] + beta_s[j] * ahead
         f_s[j] = ahead
-    pos = pos_ref[0]
     left = p_s[pos] + q_s[pos] * f_s[pos]
     right = f_s[pos + 1]
     for w in range(width):
@@ -265,9 +266,7 @@
         if step == 1:
             held, tracer_received = lax.optimization_barrier((held, tracer_received))
         step *= 2
-    reverse = held[::-1]
-    doubled = jnp.concatenate([reverse, reverse], axis=0)
-    packed_all = lax.dynamic_slice_in_dim(doubled, count - 1 - position, count, 0)
+    packed_all = held
     wind_fields = interface_update(packed_all, position, local_solve, left_spike, right_spike)
     tracer_windows = assemble_windows(
         tracer_main, tracer_halo, *tracer_received, offsets, position, block_count

time: 254 us -> 254 us (level)
    unnamed x85 -> x87, local copies, waits for them, and re-layouts: 23.6 us -> 24.5 us
where the time goes in v7:
time: 254 us; the launch traced here: 252 us
  waiting for transfers between devices  56.3 us (22%)
  local copies, waits for them, and re-layouts  53.6 us (21%)
  starting transfers between devices  50.4 us (20%)
  between operations  45.9 us (18%)
  other arithmetic  39.4 us (16%)
  Pallas kernels  3.6 us (1%)
  matrix products  2.71 us (1%)
    ppermute x5, waiting for transfers between devices, local(): held = jnp.concatenate([held, lax.ppermute(held, 'gx', ring)], axis=0)  35.5 us
    ppermute x8, starting transfers between devices, shifted_2(): lax.ppermute(value, axis, [(source, source + steps) for source in range(l...  25.7 us
    unnamed x87, local copies, waits for them, and re-layouts  24.5 us
    ppermute x8, waiting for transfers between devices, shifted_2(): lax.ppermute(value, axis, [(source, source + steps) for source in range(l...  20.7 us
    add x2, other arithmetic, interpolate(): running_total + tap_term  15.9 us
    ppermute x5, starting transfers between devices, local(): held = jnp.concatenate([held, lax.ppermute(held, 'gx', ring)], axis=0)  11.2 us
    reshape x2, other arithmetic, advect_group(): windows.reshape(block_count, field_count, level_count, BX + 4, rows_here...  6.42 us
    slice x2, local copies, waits for them, and re-layouts, halo_y(): low = lax.ppermute(block[:, :, block.shape[2] - width:], axis, forward)  5.99 us
  transfers between devices with their start and end apart: 17, of which 6 were waited for; matrix products, arithmetic and copies ran while one was open for 29% of the time, Pallas kernels for 0%

profile of v7, /device:TPU:34, one launch (start us, length us, event | category | flops | bytes accessed | tf_op | source)
XLA Modules:
  0.0 251.9 jit_solution(18092056397202524723)
XLA Ops:
  0.7 2.9 %copy.67 = f32[4,8,128,128]{3,1,0,2:T(8,128)S(1)} copy(f32[4,8,128,128]{3,2,1,0:T(8,128)} %param.7) | data formatting | bytes 4194304 | tf_op args[0]
  3.6 1.3 copy-done.2
  4.9 3.5 %collective-permute-start = (f32[32,2,128]{2,0,1:T(8,128)S(1)}, f32[32,2,128]{2,0,1:T(8,128)S(1)}, u32[]{:S(2)}, u32[]{:S(2)}) collective-permute-start(f32[32,2,128]{2,0,1:T(8,128)S(1)} %get-tuple-element.48), channel_id=1, source_target_pairs={{0,8},{8,16},{16,24},{24,32},{32,40},{40,48},{48,56},{56,64},{64,7... | collective-permute-start | bytes 98312 | tf_op jit(solution)/shard_map/ppermute | solution.py:131
  8.4 4.5 %collective-permute-start.1 = (f32[32,2,128]{2,0,1:T(8,128)S(1)}, f32[32,2,128]{2,0,1:T(8,128)S(1)}, u32[]{:S(2)}, u32[]{:S(2)}) collective-permute-start(f32[32,2,128]{2,0,1:T(8,128)S(1)} %get-tuple-element.49), channel_id=1, source_target_pairs={{8,0},{16,8},{24,16},{32,24},{40,32},{48,40},{56,48},{64,56},{72,6... | collective-permute-start | bytes 98312 | tf_op jit(solution)/shard_map/ppermute | solution.py:132
  14.7 1.2 slice_multiply_fusion.50
  16.1 3.9 %fusion.62 = (f32[8,8,16,128]{3,1,2,0:T(8,128)}, f32[8,8,16,128]{3,1,2,0:T(8,128)}, f32[8,8,16,128]{3,1,2,0:T(8,128)}, f32[8,8,16,128]{3,1,2,0:T(8,128)}, f32[8,...) fusion(f32[8,8,16,128]{3,2,1,0:T(8,128)S(1)} %bitcast.362, ...), kind=kLoop, calls=%fused_computation.129 | loop fusion | flops 9175040 | bytes 6291456 | tf_op jit(solution)/shard_map/mul | solution.py:40
  20.1 0.8 fusion.99
  20.9 0.8 fusion.107
  51.7 1.8 pad_maximum_fusion
  53.5 2.8 %fusion.114 = (f32[32,132,2]{2,0,1:T(8,128)}, f32[32,132,2]{2,0,1:T(8,128)}) fusion(f32[32,132,128]{2,0,1:T(8,128)S(1)} %pad_maximum_fusion), kind=kLoop, calls=%fused_computation.405 | loop fusion | bytes 135168 | tf_op jit(solution)/shard_map/slice | solution.py:140
  56.4 3.2 %copy.40 = f32[32,132,2]{1,0,2:T(8,128)S(1)} copy(f32[32,132,2]{2,0,1:T(8,128)} %get-tuple-element.46) | data formatting | bytes 67584 | tf_op jit(solution)/shard_map/slice | solution.py:140
  59.6 1.9 collective-permute-start.2
  61.5 3.2 %copy.41 = f32[32,132,2]{1,0,2:T(8,128)S(1)} copy(f32[32,132,2]{2,0,1:T(8,128)} %get-tuple-element.47) | data formatting | bytes 67584 | tf_op jit(solution)/shard_map/slice | solution.py:141
  64.7 3.6 %collective-permute-start.3 = (f32[32,132,2]{1,0,2:T(8,128)S(1)}, f32[32,132,2]{1,0,2:T(8,128)S(1)}, u32[]{:S(2)}, u32[]{:S(2)}) collective-permute-start(f32[32,132,2]{1,0,2:T(8,128)S(1)} %copy.41), channel_id=1, source_target_pairs={{1,0},{2,1},{3,2},{4,3},{5,4},{6,5},{7,6},{9,8},{10,9},{11,10},{12... | collective-permute-start | bytes 101384 | tf_op jit(solution)/shard_map/ppermute | solution.py:141
  71.6 0.9 constant_dynamic-update-slice_fusion
  72.5 3.0 %collective-permute-start.4 = (f32[16,84,128]{2,0,1:T(8,128)}, f32[16,84,128]{2,0,1:T(8,128)S(1)}, u32[]{:S(2)}, u32[]{:S(2)}) collective-permute-start(f32[16,84,128]{2,0,1:T(8,128)} %constant_dynamic-update-slice_fusion), channel_id=1, source_target_pairs={{0,16},{8,24},{16,32},{24,40},{32,48},{40,56},{48,64},{56,72},{64,... | collective-permute-start | bytes 2064392 | tf_op jit(solution)/shard_map/ppermute | solution.py:30
  91.5 2.6 %collective-permute-start.5 = (f32[16,84,128]{2,0,1:T(8,128)}, f32[16,84,128]{2,0,1:T(8,128)S(1)}, u32[]{:S(2)}, u32[]{:S(2)}) collective-permute-start(f32[16,84,128]{2,0,1:T(8,128)} %constant_dynamic-update-slice_fusion.5), channel_id=1, source_target_pairs={{0,8},{8,16},{16,24},{24,32},{32,40},{40,48},{48,56},{56,64},{64,7... | collective-permute-start | bytes 2064392 | tf_op jit(solution)/shard_map/ppermute | solution.py:30
  94.9 5.4 %collective-permute-start.6 = (f32[16,84,128]{2,0,1:T(8,128)}, f32[16,84,128]{2,0,1:T(8,128)S(1)}, u32[]{:S(2)}, u32[]{:S(2)}) collective-permute-start(f32[16,84,128]{2,0,1:T(8,128)} %constant_dynamic-update-slice_fusion.10), channel_id=1, source_target_pairs={{8,0},{16,8},{24,16},{32,24},{40,32},{48,40},{56,48},{64,56},{72,6... | collective-permute-start | bytes 2064392 | tf_op jit(solution)/shard_map/ppermute | solution.py:30
  100.9 3.3 %collective-permute-start.7 = (f32[16,84,128]{2,0,1:T(8,128)}, f32[16,84,128]{2,0,1:T(8,128)S(1)}, u32[]{:S(2)}, u32[]{:S(2)}) collective-permute-start(f32[16,84,128]{2,0,1:T(8,128)} %constant_dynamic-update-slice_fusion.15), channel_id=1, source_target_pairs={{16,0},{24,8},{32,16},{40,24},{48,32},{56,40},{64,48},{72,56},{80,... | collective-permute-start | bytes 2064392 | tf_op jit(solution)/shard_map/ppermute | solution.py:30
  104.6 8.9 %collective-permute-done.5 = f32[16,84,128]{2,0,1:T(8,128)S(1)} collective-permute-done((f32[16,84,128]{2,0,1:T(8,128)}, f32[16,84,128]{2,0,1:T(8,128)S(1)}, u32[]{:S(2)}, u32[]{:S(2)}) %collective-permute-start.5) | collective-permute-done | bytes 688160 | tf_op jit(solution)/shard_map/ppermute | solution.py:30
  113.7 0.9 constant_dynamic-update-slice_fusion.56
  114.6 0.8 constant_dynamic-update-slice_fusion.55
  115.4 0.8 constant_dynamic-update-slice_fusion.54
  116.3 0.8 constant_dynamic-update-slice_fusion.53
  117.8 2.8 %collective-permute-start.12 = (f32[16,84,128]{2,0,1:T(8,128)}, f32[16,84,128]{2,0,1:T(8,128)}, u32[]{:S(2)}, u32[]{:S(2)}) collective-permute-start(f32[16,84,128]{2,0,1:T(8,128)} %constant_dynamic-update-slice_fusion.52), channel_id=1, source_target_pairs={{16,0},{24,8},{32,16},{40,24},{48,32},{56,40},{64,48},{72,56},{80,... | collective-permute-start | bytes 2064392 | tf_op jit(solution)/shard_map/ppermute | solution.py:30
  121.3 2.2 collective-permute-start.11
  124.2 3.7 %collective-permute-start.10 = (f32[16,84,128]{2,0,1:T(8,128)}, f32[16,84,128]{2,0,1:T(8,128)}, u32[]{:S(2)}, u32[]{:S(2)}) collective-permute-start(f32[16,84,128]{2,0,1:T(8,128)} %constant_dynamic-update-slice_fusion.42), channel_id=1, source_target_pairs={{0,8},{8,16},{16,24},{24,32},{32,40},{40,48},{48,56},{56,64},{64,7... | collective-permute-start | bytes 2064392 | tf_op jit(solution)/shard_map/ppermute | solution.py:30
  128.6 1.7 collective-permute-done.6
  130.3 2.8 %collective-permute-start.9 = (f32[16,84,128]{2,0,1:T(8,128)}, f32[16,84,128]{2,0,1:T(8,128)}, u32[]{:S(2)}, u32[]{:S(2)}) collective-permute-start(f32[16,84,128]{2,0,1:T(8,128)} %constant_dynamic-update-slice_fusion.37), channel_id=1, source_target_pairs={{0,16},{8,24},{16,32},{24,40},{32,48},{40,56},{48,64},{56,72},{64,... | collective-permute-start | bytes 2064392 | tf_op jit(solution)/shard_map/ppermute | solution.py:30
  133.1 10.1 %collective-permute-done.7 = f32[16,84,128]{2,0,1:T(8,128)S(1)} collective-permute-done((f32[16,84,128]{2,0,1:T(8,128)}, f32[16,84,128]{2,0,1:T(8,128)S(1)}, u32[]{:S(2)}, u32[]{:S(2)}) %collective-permute-start.7) | collective-permute-done | bytes 688160 | tf_op jit(solution)/shard_map/ppermute | solution.py:30
  143.3 1.7 copy-done.8
  145.3 0.9 constant_dynamic-update-slice_fusion.35
  146.3 0.9 constant_dynamic-update-slice_fusion.34
  147.3 0.9 constant_dynamic-update-slice_fusion.33
  148.3 0.9 constant_dynamic-update-slice_fusion.32
  149.3 0.9 constant_dynamic-update-slice_fusion.31
  150.4 0.9 constant_dynamic-update-slice_fusion.30
  151.4 0.9 constant_dynamic-update-slice_fusion.29
  152.4 2.0 copy.42
  154.5 2.0 copy.43
  156.5 3.2 %maximum_bitcast_fusion = f32[8,2,8,20,132]{4,2,1,3,0:T(8,128)S(1)} fusion(f32[8,16,20,2]{3,1,2,0:T(8,128)} %copy.43, f32[8,16,20,128]{3,1,2,0:T(8,128)} %copy-done.6, f32[8,16,20,2]{3,1,2,0:T(8,128)} %copy.42), kind=kLoop, calls=%fused_computation | loop fusion | flops 675840 | bytes 2703360 | tf_op jit(solution)/shard_map/reshape | solution.py:220
  159.7 8.0 %fusion.31 = f32[8,2,8,16,128]{4,2,1,3,0:T(8,128)} fusion(f32[8,2,8,20,132]{4,2,1,3,0:T(8,128)S(1)} %maximum_bitcast_fusion, f32[8,8,16,128]{3,1,2,0:T(8,128)} %get-tuple-element.177, f32[8,8,16,128]{3,1,2,0:T(8,128)} %get-tuple-element.176, f32[8,8,16,128]{3,1,2,0:T(8,128)} %get-tuple-element.174, f32[8,8,16,128]{3,1,2,0:T(8,128)} %get-tuple-element.175, ...), kind=kLoop, calls=%fused_computation.62 | loop fusion | flops 14155776 | bytes 32505856 | tf_op jit(solution)/shard_map/add | solution.py:58
  167.7 2.7 %convolution_bitcast_fusion.solve_ref = f32[2,8,128,128]{3,2,1,0:T(8,128)S(1)} fusion(f32[2,8,128,128]{3,1,0,2:T(8,128)} %bitcast.360, f32[8,128,128]{2,1,0:T(8,128)} %param.11), kind=kOutput, calls=%fused_computation.4 | convolution fusion | flops 402653184 | bytes 2621440 | tf_op jit(solution)/shard_map/lij,wljy->wliy/dot_general | solution.py:248
  170.5 15.8 %collective-permute-done.8 = f32[1,5,8,128]{3,2,1,0:T(8,128)S(1)} collective-permute-done((f32[1,5,8,128]{3,2,1,0:T(8,128)S(1)}, f32[1,5,8,128]{3,2,1,0:T(8,128)S(1)}, u32[]{:S(2)}, u32[]{:S(2)}) %collective-permute-start.8) | collective-permute-done | bytes 20512 | tf_op jit(solution)/shard_map/ppermute | solution.py:265
  186.4 1.1 slice.448
  187.5 0.8 slice.452
  188.3 1.1 slice.447
  189.4 0.8 slice.451
  190.2 1.1 slice.446
  191.3 0.9 slice.450
  192.3 1.1 slice.445
  194.7 1.6 copy-done.9
  197.1 4.1 %collective-permute-start.13 = (f32[2,5,8,128]{3,2,1,0:T(8,128)S(1)}, f32[2,5,8,128]{3,2,1,0:T(8,128)S(1)}, u32[]{:S(2)}, u32[]{:S(2)}) collective-permute-start(f32[2,5,8,128]{3,2,1,0:T(8,128)S(1)} %pad_maximum_fusion.4), channel_id=1, source_target_pairs={{0,16},{8,24},{16,32},{24,40},{32,48},{40,56},{48,64},{56,72},{64,... | collective-permute-start | bytes 122888 | tf_op jit(solution)/shard_map/ppermute | solution.py:265
  201.2 0.9 constant_dynamic-update-slice_fusion.75
  202.2 2.0 copy.47
  204.2 2.0 copy.48
  206.2 0.8 collective-permute-start.14
  207.0 3.2 %maximum_bitcast_fusion.1 = f32[8,2,8,20,132]{4,2,1,3,0:T(8,128)S(1)} fusion(f32[8,16,20,2]{3,1,2,0:T(8,128)} %copy.48, f32[8,16,20,128]{3,1,2,0:T(8,128)} %copy-done.7, f32[8,16,20,2]{3,1,2,0:T(8,128)} %copy.47), kind=kLoop, calls=%fused_computation.1 | loop fusion | flops 675840 | bytes 2703360 | tf_op jit(solution)/shard_map/reshape | solution.py:220
  211.4 6.0 %collective-permute-start.15 = (f32[8,5,8,128]{3,2,1,0:T(8,128)}, f32[8,5,8,128]{3,2,1,0:T(8,128)S(1)}, u32[]{:S(2)}, u32[]{:S(2)}) collective-permute-start(f32[8,5,8,128]{3,2,1,0:T(8,128)} %pad_maximum_fusion.2), channel_id=1, source_target_pairs={{0,64},{8,72},{16,80},{24,88},{32,96},{40,104},{48,112},{56,120},{... | collective-permute-start | bytes 491528 | tf_op jit(solution)/shard_map/ppermute | solution.py:265
  217.5 8.0 %fusion.2 = f32[8,2,8,16,128]{4,2,1,3,0:T(8,128)} fusion(f32[8,2,8,20,132]{4,2,1,3,0:T(8,128)S(1)} %maximum_bitcast_fusion.1, f32[8,8,16,128]{3,1,2,0:T(8,128)} %get-tuple-element.177, f32[8,8,16,128]{3,1,2,0:T(8,128)} %get-tuple-element.176, f32[8,8,16,128]{3,1,2,0:T(8,128)} %get-tuple-element.174, f32[8,8,16,128]{3,1,2,0:T(8,128)} %get-tuple-element.175, ...), kind=kLoop, calls=%fused_computation.8 | loop fusion | flops 14155776 | bytes 32505856 | tf_op jit(solution)/shard_map/add | solution.py:58
  225.4 2.5 %copy.49 = f32[2,8,128,128]{3,2,1,0:T(8,128)} copy(f32[2,8,128,128]{3,1,0,2:T(8,128)} %bitcast.359) | data formatting | bytes 2097152
  228.3 19.1 %collective-permute-done.16 = f32[16,5,8,128]{3,2,1,0:T(8,128)S(1)} collective-permute-done((f32[16,5,8,128]{3,2,1,0:T(8,128)S(1)}, f32[16,5,8,128]{3,2,1,0:T(8,128)S(1)}, u32[]{:S(2)}, u32[]{:S(2)}) %collective-permute-start.16) | collective-permute-done | bytes 327712 | tf_op jit(solution)/shard_map/ppermute | solution.py:265
  247.4 0.8 copy-done.10
  248.3 3.6 %shard_map.86 = f32[2,8,128,128]{3,2,1,0:T(8,128)} custom-call(s32[1]{0:T(128)} %bitcast.pos_ref, f32[32,5,8,128]{3,2,1,0:T(8,128)} %copy-done.10, f32[2,8,128,128]{3,2,1,0:T(8,128)} %copy-done.5, f32[8,128,1]{2,1,0:T(8,128)} %get-tuple-element.85.lspike_ref, f32[8,128,1]{2,1,0:T(8,128)} %get-tuple-element.84.rspike_ref), custom_call_target="tpu_custom_call" | custom-call | tf_op jit(solution)/shard_map/pallas_call | solution.py:106
  (138 shorter events, 16.2 us)
Async XLA Ops:
  0.6 12.3 %copy-start.13 = (s32[256,1]{0,1:T(1,128)S(1)}, s32[256,1]{0,1:T(1,128)}, u32[]{:S(2)}) copy-start(s32[256,1]{0,1:T(1,128)} %param.10) | copy-start | bytes 3076
  0.6 13.9 %copy-start.11 = (f32[8,128,128]{2,1,0:T(8,128)S(1)}, f32[8,128,128]{2,1,0:T(8,128)}, u32[]{:S(2)}) copy-start(f32[8,128,128]{2,1,0:T(8,128)} %param.8) | copy-start | bytes 1572868
  0.7 14.0 %copy-start.12 = (f32[8,128,128]{2,1,0:T(8,128)S(1)}, f32[8,128,128]{2,1,0:T(8,128)}, u32[]{:S(2)}) copy-start(f32[8,128,128]{2,1,0:T(8,128)} %param.9) | copy-start | bytes 1572868
  3.6 1.4 copy-start.2
  3.6 11.1 %copy-start.4 = (f32[8,128,128]{2,1,0:T(8,128)S(1)}, f32[8,128,128]{2,1,0:T(8,128)}, u32[]{:S(2)}) copy-start(f32[8,128,128]{2,1,0:T(8,128)} %param.11) | copy-start | bytes 1572868
  3.6 11.1 %copy-start.17 = (f32[8,1]{0,1:T(1,128)S(1)}, f32[8,1]{0,1:T(1,128)}, u32[]{:S(2)}) copy-start(f32[8,1]{0,1:T(1,128)} %param.13) | copy-start | bytes 100
  3.6 11.1 %copy-start.18 = (f32[8,1]{0,1:T(1,128)S(1)}, f32[8,1]{0,1:T(1,128)}, u32[]{:S(2)}) copy-start(f32[8,1]{0,1:T(1,128)} %param.12) | copy-start | bytes 100
  4.9 46.8 %collective-permute-start = (f32[32,2,128]{2,0,1:T(8,128)S(1)}, f32[32,2,128]{2,0,1:T(8,128)S(1)}, u32[]{:S(2)}, u32[]{:S(2)}) collective-permute-start(f32[32,2,128]{2,0,1:T(8,128)S(1)} %get-tuple-element.48), channel_id=1, source_target_pairs={{0,8},{8,16},{16,24},{24,32},{32,40},{40,48},{48,56},{56,64},{64,7... | collective-permute-start | bytes 98312 | tf_op jit(solution)/shard_map/ppermute | solution.py:131
  8.4 43.3 %collective-permute-start.1 = (f32[32,2,128]{2,0,1:T(8,128)S(1)}, f32[32,2,128]{2,0,1:T(8,128)S(1)}, u32[]{:S(2)}, u32[]{:S(2)}) collective-permute-start(f32[32,2,128]{2,0,1:T(8,128)S(1)} %get-tuple-element.49), channel_id=1, source_target_pairs={{8,0},{16,8},{24,16},{32,24},{40,32},{48,40},{56,48},{64,56},{72,6... | collective-permute-start | bytes 98312 | tf_op jit(solution)/shard_map/ppermute | solution.py:132
  53.5 60.1 %copy-start = (f32[32,132,128]{2,0,1:T(8,128)}, f32[32,132,128]{2,0,1:T(8,128)S(1)}, u32[]{:S(2)}) copy-start(f32[32,132,128]{2,0,1:T(8,128)S(1)} %pad_maximum_fusion) | copy-start | bytes 6488068
  59.6 11.7 %collective-permute-start.2 = (f32[32,132,2]{1,0,2:T(8,128)S(1)}, f32[32,132,2]{1,0,2:T(8,128)S(1)}, u32[]{:S(2)}, u32[]{:S(2)}) collective-permute-start(f32[32,132,2]{1,0,2:T(8,128)S(1)} %copy.40), channel_id=1, source_target_pairs={{0,1},{1,2},{2,3},{3,4},{4,5},{5,6},{6,7},{8,9},{9,10},{10,11},{11... | collective-permute-start | bytes 101384 | tf_op jit(solution)/shard_map/ppermute | solution.py:140
  64.7 6.5 %collective-permute-start.3 = (f32[32,132,2]{1,0,2:T(8,128)S(1)}, f32[32,132,2]{1,0,2:T(8,128)S(1)}, u32[]{:S(2)}, u32[]{:S(2)}) collective-permute-start(f32[32,132,2]{1,0,2:T(8,128)S(1)} %copy.41), channel_id=1, source_target_pairs={{1,0},{2,1},{3,2},{4,3},{5,4},{6,5},{7,6},{9,8},{10,9},{11,10},{12... | collective-permute-start | bytes 101384 | tf_op jit(solution)/shard_map/ppermute | solution.py:141
  71.3 5.0 %copy-start.14 = (f32[16,84,128]{2,0,1:T(8,128)}, f32[16,84,128]{2,0,1:T(8,128)S(1)}, u32[]{:S(2)}) copy-start(f32[16,84,128]{2,0,1:T(8,128)S(1)} %get-tuple-element.66) | copy-start | bytes 2064388
  71.3 5.0 %copy-start.15 = (f32[16,84,128]{2,0,1:T(8,128)}, f32[16,84,128]{2,0,1:T(8,128)S(1)}, u32[]{:S(2)}) copy-start(f32[16,84,128]{2,0,1:T(8,128)S(1)} %get-tuple-element.67) | copy-start | bytes 2064388
  71.3 5.0 %copy-start.16 = (f32[16,84,128]{2,0,1:T(8,128)}, f32[16,84,128]{2,0,1:T(8,128)S(1)}, u32[]{:S(2)}) copy-start(f32[16,84,128]{2,0,1:T(8,128)S(1)} %get-tuple-element.68) | copy-start | bytes 2064388
  72.5 32.0 %collective-permute-start.4 = (f32[16,84,128]{2,0,1:T(8,128)}, f32[16,84,128]{2,0,1:T(8,128)S(1)}, u32[]{:S(2)}, u32[]{:S(2)}) collective-permute-start(f32[16,84,128]{2,0,1:T(8,128)} %constant_dynamic-update-slice_fusion), channel_id=1, source_target_pairs={{0,16},{8,24},{16,32},{24,40},{32,48},{40,56},{48,64},{56,72},{64,... | collective-permute-start | bytes 2064392 | tf_op jit(solution)/shard_map/ppermute | solution.py:30
  91.5 22.0 %collective-permute-start.5 = (f32[16,84,128]{2,0,1:T(8,128)}, f32[16,84,128]{2,0,1:T(8,128)S(1)}, u32[]{:S(2)}, u32[]{:S(2)}) collective-permute-start(f32[16,84,128]{2,0,1:T(8,128)} %constant_dynamic-update-slice_fusion.5), channel_id=1, source_target_pairs={{0,8},{8,16},{16,24},{24,32},{32,40},{40,48},{48,56},{56,64},{64,7... | collective-permute-start | bytes 2064392 | tf_op jit(solution)/shard_map/ppermute | solution.py:30
  94.9 35.4 %collective-permute-start.6 = (f32[16,84,128]{2,0,1:T(8,128)}, f32[16,84,128]{2,0,1:T(8,128)S(1)}, u32[]{:S(2)}, u32[]{:S(2)}) collective-permute-start(f32[16,84,128]{2,0,1:T(8,128)} %constant_dynamic-update-slice_fusion.10), channel_id=1, source_target_pairs={{8,0},{16,8},{24,16},{32,24},{40,32},{48,40},{56,48},{64,56},{72,6... | collective-permute-start | bytes 2064392 | tf_op jit(solution)/shard_map/ppermute | solution.py:30
  100.9 42.3 %collective-permute-start.7 = (f32[16,84,128]{2,0,1:T(8,128)}, f32[16,84,128]{2,0,1:T(8,128)S(1)}, u32[]{:S(2)}, u32[]{:S(2)}) collective-permute-start(f32[16,84,128]{2,0,1:T(8,128)} %constant_dynamic-update-slice_fusion.15), channel_id=1, source_target_pairs={{16,0},{24,8},{32,16},{40,24},{48,32},{56,40},{64,48},{72,56},{80,... | collective-permute-start | bytes 2064392 | tf_op jit(solution)/shard_map/ppermute | solution.py:30
  117.8 68.6 %collective-permute-start.12 = (f32[16,84,128]{2,0,1:T(8,128)}, f32[16,84,128]{2,0,1:T(8,128)}, u32[]{:S(2)}, u32[]{:S(2)}) collective-permute-start(f32[16,84,128]{2,0,1:T(8,128)} %constant_dynamic-update-slice_fusion.52), channel_id=1, source_target_pairs={{16,0},{24,8},{32,16},{40,24},{48,32},{56,40},{64,48},{72,56},{80,... | collective-permute-start | bytes 2064392 | tf_op jit(solution)/shard_map/ppermute | solution.py:30
  121.3 67.0 %collective-permute-start.11 = (f32[16,84,128]{2,0,1:T(8,128)}, f32[16,84,128]{2,0,1:T(8,128)}, u32[]{:S(2)}, u32[]{:S(2)}) collective-permute-start(f32[16,84,128]{2,0,1:T(8,128)} %constant_dynamic-update-slice_fusion.47), channel_id=1, source_target_pairs={{8,0},{16,8},{24,16},{32,24},{40,32},{48,40},{56,48},{64,56},{72,6... | collective-permute-start | bytes 2064392 | tf_op jit(solution)/shard_map/ppermute | solution.py:30
  124.2 66.0 %collective-permute-start.10 = (f32[16,84,128]{2,0,1:T(8,128)}, f32[16,84,128]{2,0,1:T(8,128)}, u32[]{:S(2)}, u32[]{:S(2)}) collective-permute-start(f32[16,84,128]{2,0,1:T(8,128)} %constant_dynamic-update-slice_fusion.42), channel_id=1, source_target_pairs={{0,8},{8,16},{16,24},{24,32},{32,40},{40,48},{48,56},{56,64},{64,7... | collective-permute-start | bytes 2064392 | tf_op jit(solution)/shard_map/ppermute | solution.py:30
  130.3 62.0 %collective-permute-start.9 = (f32[16,84,128]{2,0,1:T(8,128)}, f32[16,84,128]{2,0,1:T(8,128)}, u32[]{:S(2)}, u32[]{:S(2)}) collective-permute-start(f32[16,84,128]{2,0,1:T(8,128)} %constant_dynamic-update-slice_fusion.37), channel_id=1, source_target_pairs={{0,16},{8,24},{16,32},{24,40},{32,48},{40,56},{48,64},{56,72},{64,... | collective-permute-start | bytes 2064392 | tf_op jit(solution)/shard_map/ppermute | solution.py:30
  143.3 1.8 copy-start.8
  152.3 2.1 copy-start.6
  156.5 3.2 %copy-start.3 = (f32[8,8,16,128]{3,1,2,0:T(8,128)S(1)}, f32[8,8,16,128]{3,1,2,0:T(8,128)}, u32[]{:S(2)}) copy-start(f32[8,8,16,128]{3,1,2,0:T(8,128)} %get-tuple-element.93) | copy-start | bytes 1572868
  170.4 20.9 %copy-start.5 = (f32[2,8,128,128]{3,2,1,0:T(8,128)}, f32[2,8,128,128]{3,2,1,0:T(8,128)S(1)}, u32[]{:S(2)}) copy-start(f32[2,8,128,128]{3,2,1,0:T(8,128)S(1)} %convolution_bitcast_fusion.solve_ref) | copy-start | bytes 3145732
  170.4 15.9 %collective-permute-start.8 = (f32[1,5,8,128]{3,2,1,0:T(8,128)S(1)}, f32[1,5,8,128]{3,2,1,0:T(8,128)S(1)}, u32[]{:S(2)}, u32[]{:S(2)}) collective-permute-start(f32[1,5,8,128]{3,2,1,0:T(8,128)S(1)} %maximum_bitcast_fusion.3), channel_id=1, source_target_pairs={{0,8},{8,16},{16,24},{24,32},{32,40},{40,48},{48,56},{56,64},{64,7... | collective-permute-start | bytes 61448 | tf_op jit(solution)/shard_map/ppermute | solution.py:265
  191.3 2.9 %copy-start.1 = (f32[32,132,128]{2,0,1:T(8,128)S(1)}, f32[32,132,128]{2,0,1:T(8,128)}, u32[]{:S(2)}) copy-start(f32[32,132,128]{2,0,1:T(8,128)} %copy-done) | copy-start | bytes 6488068
  194.5 1.8 copy-start.9
  197.1 9.1 %collective-permute-start.13 = (f32[2,5,8,128]{3,2,1,0:T(8,128)S(1)}, f32[2,5,8,128]{3,2,1,0:T(8,128)S(1)}, u32[]{:S(2)}, u32[]{:S(2)}) collective-permute-start(f32[2,5,8,128]{3,2,1,0:T(8,128)S(1)} %pad_maximum_fusion.4), channel_id=1, source_target_pairs={{0,16},{8,24},{16,32},{24,40},{32,48},{40,56},{48,64},{56,72},{64,... | collective-permute-start | bytes 122888 | tf_op jit(solution)/shard_map/ppermute | solution.py:265
  202.2 4.1 %copy-start.7 = (f32[8,16,20,128]{3,1,2,0:T(8,128)}, f32[8,16,20,128]{3,1,2,0:T(8,128)S(1)}, u32[]{:S(2)}) copy-start(f32[8,16,20,128]{3,1,2,0:T(8,128)S(1)} %constant_dynamic-update-slice_fusion.75) | copy-start | bytes 3932164
  206.2 4.5 %collective-permute-start.14 = (f32[4,5,8,128]{3,2,1,0:T(8,128)S(1)}, f32[4,5,8,128]{3,2,1,0:T(8,128)S(1)}, u32[]{:S(2)}, u32[]{:S(2)}) collective-permute-start(f32[4,5,8,128]{3,2,1,0:T(8,128)S(1)} %pad_maximum_fusion.3), channel_id=1, source_target_pairs={{0,32},{8,40},{16,48},{24,56},{32,64},{40,72},{48,80},{56,88},{64,... | collective-permute-start | bytes 245768 | tf_op jit(solution)/shard_map/ppermute | solution.py:265
  211.4 16.5 %collective-permute-start.15 = (f32[8,5,8,128]{3,2,1,0:T(8,128)}, f32[8,5,8,128]{3,2,1,0:T(8,128)S(1)}, u32[]{:S(2)}, u32[]{:S(2)}) collective-permute-start(f32[8,5,8,128]{3,2,1,0:T(8,128)} %pad_maximum_fusion.2), channel_id=1, source_target_pairs={{0,64},{8,72},{16,80},{24,88},{32,96},{40,104},{48,112},{56,120},{... | collective-permute-start | bytes 491528 | tf_op jit(solution)/shard_map/ppermute | solution.py:265
  228.0 19.4 %collective-permute-start.16 = (f32[16,5,8,128]{3,2,1,0:T(8,128)S(1)}, f32[16,5,8,128]{3,2,1,0:T(8,128)S(1)}, u32[]{:S(2)}, u32[]{:S(2)}) collective-permute-start(f32[16,5,8,128]{3,2,1,0:T(8,128)S(1)} %pad_maximum_fusion.1), channel_id=1, source_target_pairs={{0,128},{8,136},{16,144},{24,152},{32,160},{40,168},{48,176},{56,1... | collective-permute-start | bytes 983048 | tf_op jit(solution)/shard_map/ppermute | solution.py:265
  247.4 0.8 copy-start.10
